TPU v7x, 128 devices: a whole 4x4x4 slice. The times are simulated.
128 devices in a mesh: cell: 32 (over y, z, core), own: 4 (over x).
Axes of the slice: x: 4, y: 4, z: 4, core: 2. Of those that a mesh axis runs over, the one named last changes fastest.
Arguments:
- hist: bfloat16 [262144, 3, 256], P(('cell', 'own')), as said below
- dest: int32 [262144, 1], P(('cell', 'own')), may hold values from 0 to 127; in each aligned block of 2048 rows (0 to 2047, 2048 to 4095, ...) at most 32 rows name the same one
- cell_in: int32 [262144], P(('cell', 'own')), may hold values from 0 to 1023
- offsets: int32 [4, 131072], P(None, ('cell', 'own')), may hold values from -4 to 4
Outputs:
- multipliers: float32 [2, 6, 131072], P(None, None, ('cell', 'own'))
- fit_stat: float32 [2, 131072], P(None, ('cell', 'own'))
Inputs may be any that keep to these rules, and one draw needn't show every extreme that they name: `dest`: the rows of one device name each cell block at most 32 times, and in every draw some device names some block exactly 32 times. `hist`: Positive, every entry at least three ten-thousandths of its row's largest.
All inputs are finite; a program needn't handle non-finite values.
Results may differ from a plain program's by a relative error of at most 0.0022.
Values may be sent and summed in bfloat16 or wider, within the bound.
No kernel may reach another device: no remote copies, remote signals or barrier semaphores. Data moves between devices by JAX's collectives and lax.ppermute only.
A program may use at most 64 MiB of HBM per device.

v0:
```python
import jax
import jax.numpy as jnp
from jax import lax
from jax.experimental import pallas as pl
from jax.experimental.pallas import tpu as pltpu
from jax.sharding import PartitionSpec as P

SPEC = 2
MOM = 6
NEWTON = 8
NEIGH = 4
W = 4
CODE = 32
EXTRA = 8


def with_halo(block, sides, width):
    for axis, dim in sides:
        count = lax.axis_size(axis)
        forward = [(i, i + 1) for i in range(count - 1)]
        backward = [(target, source) for source, target in forward]
        low = lax.ppermute(
            lax.slice_in_dim(block, block.shape[dim] - width, None, axis=dim), axis, forward
        )
        high = lax.ppermute(lax.slice_in_dim(block, 0, width, axis=dim), axis, backward)
        block = jnp.concatenate([low, block, high], axis=dim)
    return block


def legendre_table(levels, count):
    xpos = (2.0 * jnp.arange(levels, dtype=jnp.float32) + 1.0) / levels - 1.0
    prev = jnp.ones_like(xpos)
    curr = xpos
    table = [curr]
    for order in range(1, count):
        nxt = ((2 * order + 1) * xpos * curr - order * prev) / (order + 1)
        prev, curr = (curr, nxt)
        table.append(curr)
    return jnp.stack(table, axis=0)


def pair_list(count):
    return [(row, col) for row in range(count) for col in range(row + 1)]


def chol_solve(hess, rhs, count):
    lower = [[None] * count for _ in range(count)]
    for row in range(count):
        for col in range(row + 1):
            total = hess[row][col]
            for inner in range(col):
                total = total - lower[row][inner] * lower[col][inner]
            if row == col:
                lower[row][col] = jnp.sqrt(total)
            else:
                lower[row][col] = total / lower[col][col]
    forward = []
    for row in range(count):
        total = rhs[row]
        for inner in range(row):
            total = total - lower[row][inner] * forward[inner]
        forward.append(total / lower[row][row])
    backward = [None] * count
    for row in reversed(range(count)):
        total = forward[row]
        for inner in range(row + 1, count):
            total = total - lower[inner][row] * backward[inner]
        backward[row] = total / lower[row][row]
    return backward


def fit_kernel(t_ref, phit_ref, psi_ref, lam_ref, fit_ref, lam_s):
    spec, levels, cells = t_ref.shape
    count = lam_ref.shape[1]
    highest = lax.Precision.HIGHEST
    pairs = pair_list(count)
    phit = phit_ref[...]
    psi = psi_ref[...]

    def contract(a, b):
        return jnp.dot(a, b, precision=highest, preferred_element_type=jnp.float32)

    for s in range(spec):
        target = t_ref[s]
        got = contract(psi, target)
        total = got[count : count + 1]
        moments = [got[m : m + 1] / total for m in range(count)]
        lam_s[...] = jnp.zeros(lam_s.shape, jnp.float32)
        lam = [jnp.zeros((1, cells), jnp.float32) for _ in range(count)]
        for step in range(NEWTON):
            expo = jnp.exp(contract(phit, lam_s[...]))
            got = contract(psi, expo)
            norm = got[count : count + 1]
            first = [got[m : m + 1] / norm for m in range(count)]
            hess = [[None] * count for _ in range(count)]
            for k, (row, col) in enumerate(pairs):
                second = got[count + 1 + k : count + 2 + k] / norm
                value = second - first[row] * first[col]
                if row == col:
                    value = value + 0.01
                hess[row][col] = value
            rhs = [first[m] - moments[m] for m in range(count)]
            delta = chol_solve(hess, rhs, count)
            for m in range(count):
                lam[m] = lam[m] - 0.5 * delta[m]
                lam_s[m : m + 1, :] = lam[m]
        exponent = contract(phit, lam_s[...])
        log_norm = jnp.log(jnp.sum(jnp.exp(exponent), axis=0, keepdims=True))
        whole = jnp.sum(target, axis=0, keepdims=True)
        ratio = jnp.log(target / whole) - (exponent - log_norm)
        fit_ref[s : s + 1, :] = 2.0 * jnp.sum(target * ratio, axis=0, keepdims=True) / levels
        lam_ref[s] = lam_s[0:count, :]


def fit_all(target, count):
    spec, levels, cells = target.shape
    phi = legendre_table(levels, count)
    pairs = pair_list(count)
    width = 8
    phit = jnp.zeros((levels, width), jnp.float32).at[:, :count].set(phi.T)
    rows = [phi[m] for m in range(count)] + [jnp.ones((levels,), jnp.float32)]
    rows += [phi[r] * phi[c] for r, c in pairs]
    height = -(-len(rows) // 8) * 8
    rows += [jnp.zeros((levels,), jnp.float32)] * (height - len(rows))
    psi = jnp.stack(rows, axis=0)
    return pl.pallas_call(
        fit_kernel,
        out_shape=(
            jax.ShapeDtypeStruct((spec, count, cells), jnp.float32),
            jax.ShapeDtypeStruct((spec, cells), jnp.float32),
        ),
        scratch_shapes=[pltpu.VMEM((width, cells), jnp.float32)],
    )(target, phit, psi)


def smooth_levels(field):
    padded = jnp.pad(field, ((0, 0), (1, 1), (0, 0)))
    return 0.5 * field + 0.25 * (padded[:, :-2, :] + padded[:, 2:, :])


def body(hist, dest, cell_in, offsets):
    rows = hist.shape[0]
    width = hist.shape[2]
    cells = offsets.shape[1]
    devices = lax.axis_size(("cell", "own"))
    capacity = 2 * rows // devices
    slots = devices * capacity
    packed = jnp.sum(hist, axis=1, dtype=jnp.float32).astype(jnp.bfloat16)
    target_block = dest[:, 0]
    member = (target_block[:, None] == jnp.arange(devices, dtype=jnp.int32)[None, :]).astype(
        jnp.int32
    )
    ranks = jnp.sum((jnp.cumsum(member, axis=0) - 1) * member, axis=1)
    position = target_block * capacity + ranks
    codes = jnp.stack([cell_in // CODE + 1, cell_in % CODE], axis=1).astype(jnp.bfloat16)
    codes = jnp.pad(codes, ((0, 0), (0, 128 - 2)))
    payload = jnp.concatenate([packed, codes], axis=1)
    place = (jnp.arange(slots, dtype=jnp.int32)[:, None] == position[None, :]).astype(jnp.bfloat16)
    sent = jnp.dot(place, payload, preferred_element_type=jnp.float32)
    send_rows = sent[:, :width].astype(jnp.bfloat16).reshape(devices, capacity, width)
    code_rows = sent[:, width : width + 2].reshape(devices, capacity, 2)
    code_rows = jnp.swapaxes(code_rows, 1, 2).astype(jnp.bfloat16)
    code_rows = jnp.pad(code_rows, ((0, 0), (0, EXTRA - 2), (0, width - capacity)))
    message = jnp.concatenate([send_rows, code_rows], axis=1)
    got = lax.all_to_all(message, ("cell", "own"), split_axis=0, concat_axis=0, tiled=True)
    recv_rows = got[:, :capacity, :].reshape(slots, width)
    high = got[:, capacity, :capacity].astype(jnp.int32).reshape(slots)
    low = got[:, capacity + 1, :capacity].astype(jnp.int32).reshape(slots)
    recv_cells = jnp.where(high > 0, (high - 1) * CODE + low, -1)
    select = (recv_cells[:, None] == jnp.arange(cells, dtype=jnp.int32)[None, :]).astype(
        jnp.bfloat16
    )
    summed = lax.dot_general(
        recv_rows, select, (((0,), (0,)), ((), ())), preferred_element_type=jnp.float32
    )
    cellhist = summed.reshape(SPEC, width // SPEC, cells)
    levelled = smooth_levels(cellhist)
    rimmed = with_halo(levelled, ((("cell", "own"), 2),), W)
    target = 1.0 + levelled
    for shift in range(-W, W + 1):
        weight = jnp.sum((offsets == shift).astype(jnp.float32), axis=0)
        target = target + weight[None, None, :] * lax.slice_in_dim(
            rimmed, W + shift, W + shift + cells, axis=2
        )
    return fit_all(target, MOM)


def solution(mesh):
    placed = (
        P(("cell", "own"), None, None),
        P(("cell", "own"), None),
        P(("cell", "own")),
        P(None, ("cell", "own")),
    )
    return jax.shard_map(
        body,
        mesh=mesh,
        in_specs=placed,
        out_specs=(P(None, None, ("cell", "own")), P(None, ("cell", "own"))),
        check_vma=False,
    )
```

profile of v0, /device:TPU:8, one launch (start us, length us, event | category | flops | bytes accessed | tf_op | source)
XLA Modules:
  0.0 117.6 jit_solution(1983919666771251491)
XLA Ops:
  0.6 0.7 fusion.49
  1.4 0.8 copy.18
  2.2 1.1 copy.25
  3.3 0.3 fusion.42
  3.8 0.3 copy.19
  4.1 0.6 fusion.41
  4.8 0.9 copy-done
  5.6 1.7 %reduce_sum.103 = bf16[2048,256]{1,0:T(8,128)(2,1)} reduce(bf16[2048,3,256]{2,0,1:T(8,128)(2,1)S(1)} %copy-done, bf16[]{:T(256)} %constant.105.clone.1), dimensions={1}, to_apply=%region_3.4 | reduce | flops 1048576 | bytes 4194306 | tf_op jit(solution)/shard_map/reduce_sum | solution.py:148
  7.4 10.4 %fusion.6 = bf16[4096,384]{1,0:T(8,128)(2,1)S(1)} fusion(s32[2048]{0:T(1024)S(1)} %multiply_add_fusion, bf16[2048,2]{1,0:T(8,128)(2,1)} %copy.25, bf16[2048,256]{1,0:T(8,128)(2,1)} %reduce_sum.103), kind=kOutput, calls=%fused_computation.7 | convolution fusion | flops 6457131008 | bytes 4210688 | tf_op jit(solution)/shard_map/dot_general | solution.py:159
  17.9 0.1 slice.104
  18.0 0.8 copy.21
  18.9 1.8 %fusion.9 = bf16[128,40,256]{2,1,0:T(8,128)(2,1)} fusion(bf16[128,2,32]{2,1,0:T(2,128)(2,1)S(1)} %bitcast.27, bf16[128,32,256]{2,1,0:T(8,128)(2,1)S(1)} %bitcast.23), kind=kLoop, calls=%fused_computation.12 | loop fusion | flops 7864320 | bytes 4734976 | tf_op jit(solution)/shard_map/concatenate | solution.py:164
  20.6 10.4 %all-to-all-start = ((bf16[128,40,256]{2,1,0:T(8,128)(2,1)}), bf16[128,40,256]{2,1,0:T(8,128)(2,1)S(1)}, u32[]{:S(2)}, u32[]{:S(2)}) async-start(bf16[128,40,256]{2,1,0:T(8,128)(2,1)} %fusion.9), calls=%async_computation | async-start | bytes 5242880 | tf_op jit(solution)/shard_map/all_to_all | solution.py:165
  31.2 0.6 compare_reduce_fusion
  32.1 0.1 convert_reduce_fusion.8
  32.2 0.7 select_bitcast_fusion
  32.9 33.5 %all-to-all-done = bf16[128,40,256]{2,1,0:T(8,128)(2,1)S(1)} async-done(((bf16[128,40,256]{2,1,0:T(8,128)(2,1)}), bf16[128,40,256]{2,1,0:T(8,128)(2,1)S(1)}, u32[]{:S(2)}, u32[]{:S(2)}) %all-to-all-start) | async-done | bytes 2621472 | tf_op jit(solution)/shard_map/all_to_all | solution.py:165
  66.4 0.4 fusion.46
  66.8 0.1 reshape.284
  66.9 1.6 %slice.106 = bf16[128,32,256]{2,1,0:T(8,128)(2,1)} slice(bf16[128,40,256]{2,1,0:T(8,128)(2,1)S(1)} %all-to-all-done), slice={[0:128], [0:32], [0:256]} | slice | bytes 4194304 | tf_op jit(solution)/shard_map/slice | solution.py:166
  68.5 2.9 %copy.22 = bf16[256,4096]{1,0:T(8,128)(2,1)S(1)} copy(bf16[256,4096]{0,1:T(8,128)(2,1)} %bitcast.24) | data formatting | bytes 4194304 | tf_op jit(solution)/shard_map/dot_general | solution.py:173
  71.4 3.4 %fusion.3 = f32[2,128,1024]{2,1,0:T(8,128)S(1)} fusion(bf16[2,128,4096]{2,1,0:T(8,128)(2,1)S(1)} %bitcast.26, s32[4096]{0:T(1024)S(1)} %reshape.284), kind=kOutput, calls=%fused_computation.5 | convolution fusion | flops 2151677952 | bytes 3162112 | tf_op jit(solution)/shard_map/dot_general | solution.py:173
  74.8 0.3 fusion.17
  75.1 0.1 fusion.78
  75.2 2.5 %collective-permute-start = (f32[2,128,4]{2,1,0:T(8,128)S(1)}, f32[2,128,4]{2,1,0:T(8,128)S(1)}, u32[]{:S(2)}, u32[]{:S(2)}) collective-permute-start(f32[2,128,4]{2,1,0:T(8,128)S(1)} %get-tuple-element.29), channel_id=1, source_target_pairs={{0,1},{1,2},{2,3},{3,4},{4,5},{5,6},{6,7},{7,8},{8,9},{9,10},{10,1... | collective-permute-start | bytes 12296 | tf_op jit(solution)/shard_map/ppermute | solution.py:22
  77.7 7.3 %collective-permute-start.1 = (f32[2,128,4]{2,1,0:T(8,128)S(1)}, f32[2,128,4]{2,1,0:T(8,128)S(1)}, u32[]{:S(2)}, u32[]{:S(2)}) collective-permute-start(f32[2,128,4]{2,1,0:T(8,128)S(1)} %get-tuple-element.30), channel_id=1, source_target_pairs={{1,0},{2,1},{3,2},{4,3},{5,4},{6,5},{7,6},{8,7},{9,8},{10,9},{11,1... | collective-permute-start | bytes 12296 | tf_op jit(solution)/shard_map/ppermute | solution.py:25
  85.0 0.1 copy.26
  85.1 0.6 scatter.4.clone.phit_ref
  85.8 2.4 %stack.20.psi_ref = f32[32,128]{1,0:T(8,128)} concatenate(f32[1,128]{1,0:T(1,128)S(1)} %get-tuple-element.35, f32[1,128]{1,0:T(1,128)S(1)} %get-tuple-element.38, f32[1,128]{1,0:T(1,128)S(1)} %get-tuple-element.37, f32[1,128]{1,0:T(1,128)S(1)} %get-tuple-element.36, f32[1,128]{1,0:T(1,128)S(1)} %get-tuple-element.34, f32[1,128]{1,0:T(1,128)S(1)} %get-tuple-element.33, ...), dimensions={0} | concatenate | bytes 32768 | tf_op jit(solution)/shard_map/stack | solution.py:125
  88.2 3.9 %fusion.21.t_ref = f32[2,128,1024]{2,1,0:T(8,128)} fusion(f32[2,128,1024]{2,1,0:T(8,128)S(1)} %fusion.17, f32[2,128,4]{2,1,0:T(8,128)S(1)} %collective-permute-done.1, f32[2,128,4]{2,1,0:T(8,128)S(1)} %collective-permute-done, f32[1024]{0:T(1024)S(1)} %get-tuple-element.27, f32[1024]{0:T(1024)S(1)} %get-tuple-element.28, f32[1024]{0:T(1024)S(1)} %get-tuple-element.21, ...), kind=kLoop, calls=%fused_computation.37 | loop fusion | flops 7077888 | bytes 2142208 | tf_op jit(solution)/shard_map/add | solution.py:182
  92.1 24.0 %shard_map.59 = (f32[2,6,1024]{2,1,0:T(8,128)}, f32[2,1024]{1,0:T(2,128)}) custom-call(f32[2,128,1024]{2,1,0:T(8,128)} %fusion.21.t_ref, f32[128,8]{1,0:T(8,128)} %scatter.4.clone.phit_ref, f32[32,128]{1,0:T(8,128)} %stack.20.psi_ref), custom_call_target="tpu_custom_call" | custom-call | tf_op jit(solution)/shard_map/pallas_call | solution.py:126
  116.1 1.5 %copy.24 = f32[2,6,1024]{2,0,1:T(2,128)} copy(f32[2,6,1024]{2,1,0:T(8,128)} %get-tuple-element.18) | data formatting | bytes 98304 | tf_op jit(solution)/shard_map/pallas_call | solution.py:126
  (33 shorter events, 0.6 us)
Async XLA Ops:
  3.3 0.8 copy-start.1
  3.8 1.9 %copy-start = (bf16[2048,3,256]{2,0,1:T(8,128)(2,1)S(1)}, bf16[2048,3,256]{2,0,1:T(8,128)(2,1)}, u32[]{:S(2)}) copy-start(bf16[2048,3,256]{2,0,1:T(8,128)(2,1)} %param.6) | copy-start | bytes 9437188
  20.6 11.5 %copy-start.2 = (s32[4,1024]{1,0:T(4,128)S(1)}, s32[4,1024]{1,0:T(4,128)}, u32[]{:S(2)}) copy-start(s32[4,1024]{1,0:T(4,128)} %param.9) | copy-start | bytes 49156
  20.6 45.8 %all-to-all-start = ((bf16[128,40,256]{2,1,0:T(8,128)(2,1)}), bf16[128,40,256]{2,1,0:T(8,128)(2,1)S(1)}, u32[]{:S(2)}, u32[]{:S(2)}) async-start(bf16[128,40,256]{2,1,0:T(8,128)(2,1)} %fusion.9), calls=%async_computation | async-start | bytes 5242880 | tf_op jit(solution)/shard_map/all_to_all | solution.py:165
  75.2 13.0 %collective-permute-start = (f32[2,128,4]{2,1,0:T(8,128)S(1)}, f32[2,128,4]{2,1,0:T(8,128)S(1)}, u32[]{:S(2)}, u32[]{:S(2)}) collective-permute-start(f32[2,128,4]{2,1,0:T(8,128)S(1)} %get-tuple-element.29), channel_id=1, source_target_pairs={{0,1},{1,2},{2,3},{3,4},{4,5},{5,6},{6,7},{7,8},{8,9},{9,10},{10,1... | collective-permute-start | bytes 12296 | tf_op jit(solution)/shard_map/ppermute | solution.py:22
  77.7 10.5 %collective-permute-start.1 = (f32[2,128,4]{2,1,0:T(8,128)S(1)}, f32[2,128,4]{2,1,0:T(8,128)S(1)}, u32[]{:S(2)}, u32[]{:S(2)}) collective-permute-start(f32[2,128,4]{2,1,0:T(8,128)S(1)} %get-tuple-element.30), channel_id=1, source_target_pairs={{1,0},{2,1},{3,2},{4,3},{5,4},{6,5},{7,6},{8,7},{9,8},{10,9},{11,1... | collective-permute-start | bytes 12296 | tf_op jit(solution)/shard_map/ppermute | solution.py:25
where the time goes:
time: 118 us
  waiting for transfers between devices  33.5 us (28%)
  Pallas kernels  24 us (20%)
  starting transfers between devices  20.2 us (17%)
  matrix products  13.8 us (12%)
  local copies, waits for them, and re-layouts  13.6 us (12%)
  other arithmetic  11.6 us (10%)
    all_to_all x1, waiting for transfers between devices, body(): lax.all_to_all(message, ('cell', 'own'), split_axis=0, concat_axis=0, til...  33.5 us
    pallas_call x1, Pallas kernels, fit_all(): pl.pallas_call(fit_kernel, out_shape=(jax.ShapeDtypeStruct((spec, count,...  24 us
    all_to_all x1, starting transfers between devices, body(): lax.all_to_all(message, ('cell', 'own'), split_axis=0, concat_axis=0, til...  10.4 us
    dot_general x1, matrix products, body(): sent = jnp.dot(place, payload, preferred_element_type=jnp.float32)  10.4 us
    ppermute x1, starting transfers between devices, with_halo(): lax.ppermute(lax.slice_in_dim(block, 0, width, axis=dim), axis, backward)  7.29 us
    add x1, other arithmetic, body(): target + weight[None, None, :] * lax.slice_in_dim(rimmed, W + shift, W +...  3.88 us
    dot_general x1, matrix products, body(): lax.dot_general(recv_rows, select, (((0,), (0,)), ((), ())), preferred_el...  3.38 us
    dot_general x1, local copies, waits for them, and re-layouts, body(): lax.dot_general(recv_rows, select, (((0,), (0,)), ((), ())), preferred_el...  2.91 us
  transfers between devices with their start and end apart: 3, of which 1 were waited for; matrix products, arithmetic and copies ran while one was open for 4% of the time, Pallas kernels for 0%

commit v1 on v0

--- a/solution.py
+++ b/solution.py
@@ -1,5 +1,6 @@
 import jax
 import jax.numpy as jnp
+import numpy as np
 from jax import lax
 from jax.experimental import pallas as pl
 from jax.experimental.pallas import tpu as pltpu
@@ -69,68 +70,90 @@
     return backward
 
 
+def newton_step(got, moments, lam, count):
+    pairs = pair_list(count)
+    norm = got[count : count + 1]
+    first = [got[m : m + 1] / norm for m in range(count)]
+    hess = [[None] * count for _ in range(count)]
+    for k, (row, col) in enumerate(pairs):
+        second = got[count + 1 + k : count + 2 + k] / norm
+        value = second - first[row] * first[col]
+        if row == col:
+            value = value + 0.01
+        hess[row][col] = value
+    rhs = [first[m] - moments[m] for m in range(count)]
+    delta = chol_solve(hess, rhs, count)
+    return [lam[m : m + 1] - 0.5 * delta[m] for m in range(count)]
+
+
 def fit_kernel(t_ref, phit_ref, psi_ref, lam_ref, fit_ref, lam_s):
     spec, levels, cells = t_ref.shape
     count = lam_ref.shape[1]
     highest = lax.Precision.HIGHEST
-    pairs = pair_list(count)
-    phit = phit_ref[...]
-    psi = psi_ref[...]
 
     def contract(a, b):
         return jnp.dot(a, b, precision=highest, preferred_element_type=jnp.float32)
 
+    moments = []
+    for s in range(spec):
+        got = contract(psi_ref[...], t_ref[s])
+        total = got[count : count + 1]
+        moments.append([got[m : m + 1] / total for m in range(count)])
+    lam_s[...] = jnp.zeros(lam_s.shape, jnp.float32)
+
+    def step(_, carry):
+        for s in range(spec):
+            lam = lam_s[s]
+            expo = jnp.exp(contract(phit_ref[...], lam))
+            got = contract(psi_ref[...], expo)
+            new = newton_step(got, moments[s], lam, count)
+            for m in range(count):
+                lam_s[s, m : m + 1, :] = new[m]
+        return carry
+
+    lax.fori_loop(0, NEWTON, step, 0)
     for s in range(spec):
         target = t_ref[s]
-        got = contract(psi, target)
-        total = got[count : count + 1]
-        moments = [got[m : m + 1] / total for m in range(count)]
-        lam_s[...] = jnp.zeros(lam_s.shape, jnp.float32)
-        lam = [jnp.zeros((1, cells), jnp.float32) for _ in range(count)]
-        for step in range(NEWTON):
-            expo = jnp.exp(contract(phit, lam_s[...]))
-            got = contract(psi, expo)
-            norm = got[count : count + 1]
-            first = [got[m : m + 1] / norm for m in range(count)]
-            hess = [[None] * count for _ in range(count)]
-            for k, (row, col) in enumerate(pairs):
-                second = got[count + 1 + k : count + 2 + k] / norm
-                value = second - first[row] * first[col]
-                if row == col:
-                    value = value + 0.01
-                hess[row][col] = value
-            rhs = [first[m] - moments[m] for m in range(count)]
-            delta = chol_solve(hess, rhs, count)
-            for m in range(count):
-                lam[m] = lam[m] - 0.5 * delta[m]
-                lam_s[m : m + 1, :] = lam[m]
-        exponent = contract(phit, lam_s[...])
+        exponent = contract(phit_ref[...], lam_s[s])
         log_norm = jnp.log(jnp.sum(jnp.exp(exponent), axis=0, keepdims=True))
         whole = jnp.sum(target, axis=0, keepdims=True)
         ratio = jnp.log(target / whole) - (exponent - log_norm)
         fit_ref[s : s + 1, :] = 2.0 * jnp.sum(target * ratio, axis=0, keepdims=True) / levels
-        lam_ref[s] = lam_s[0:count, :]
+        lam_ref[s] = lam_s[s, 0:count, :]
+
+
+def legendre_numpy(levels, count):
+    xpos = (2.0 * np.arange(levels, dtype=np.float64) + 1.0) / levels - 1.0
+    prev = np.ones_like(xpos)
+    curr = xpos
+    table = [curr]
+    for order in range(1, count):
+        nxt = ((2 * order + 1) * xpos * curr - order * prev) / (order + 1)
+        prev, curr = (curr, nxt)
+        table.append(curr)
+    return np.stack(table, axis=0).astype(np.float32)
 
 
 def fit_all(target, count):
     spec, levels, cells = target.shape
-    phi = legendre_table(levels, count)
+    phi = legendre_numpy(levels, count)
     pairs = pair_list(count)
     width = 8
-    phit = jnp.zeros((levels, width), jnp.float32).at[:, :count].set(phi.T)
-    rows = [phi[m] for m in range(count)] + [jnp.ones((levels,), jnp.float32)]
+    phit = np.zeros((levels, width), np.float32)
+    phit[:, :count] = phi.T
+    rows = [phi[m] for m in range(count)] + [np.ones((levels,), np.float32)]
     rows += [phi[r] * phi[c] for r, c in pairs]
     height = -(-len(rows) // 8) * 8
-    rows += [jnp.zeros((levels,), jnp.float32)] * (height - len(rows))
-    psi = jnp.stack(rows, axis=0)
+    rows += [np.zeros((levels,), np.float32)] * (height - len(rows))
+    psi = np.stack(rows, axis=0)
     return pl.pallas_call(
         fit_kernel,
         out_shape=(
             jax.ShapeDtypeStruct((spec, count, cells), jnp.float32),
             jax.ShapeDtypeStruct((spec, cells), jnp.float32),
         ),
-        scratch_shapes=[pltpu.VMEM((width, cells), jnp.float32)],
-    )(target, phit, psi)
+        scratch_shapes=[pltpu.VMEM((spec, width, cells), jnp.float32)],
+    )(target, jnp.asarray(phit), jnp.asarray(psi))
 
 
 def smooth_levels(field):

time: 118 us -> 114 us (0.966)
  blocking collectives: 0 us -> 45.6 us
  waiting for transfers between devices: 33.5 us -> 2.38 us
  starting transfers between devices: 20.2 us -> 9.78 us
  local copies, waits for them, and re-layouts: 13.6 us -> 10.4 us
  other arithmetic: 11.6 us -> 8.46 us
  Pallas kernels: 24 us -> 21.7 us
    all_to_all x0 -> x1, blocking collectives: none -> 45.6 us  [body(): lax.all_to_all(message, ('cell', 'own'), split_axis=0, concat_axis=0, til...]
    all_to_all x1 -> x0, waiting for transfers between devices: 33.5 us -> none  [body(): lax.all_to_all(message, ('cell', 'own'), split_axis=0, concat_axis=0, til...]
    all_to_all x1 -> x0, starting transfers between devices: 10.4 us -> none  [body(): lax.all_to_all(message, ('cell', 'own'), split_axis=0, concat_axis=0, til...]
    another operation x6 -> x2, local copies, waits for them, and re-layouts: 2.46 us -> 0.01 us  [the longest x2 2.43 us: fit_all(): psi = jnp.stack(rows, axis=0)]
    pallas_call x1, Pallas kernels: 24 us -> 21.7 us  [fit_all(): pl.pallas_call(fit_kernel, out_shape=(jax.ShapeDtypeStruct((spec, count,...]
    ppermute x1, waiting for transfers between devices: 0.01 us -> 1.79 us  [with_halo(): lax.ppermute(lax.slice_in_dim(block, 0, width, axis=dim), axis, backward)]
    concatenate x1, other arithmetic: 1.78 us -> 0.27 us  [body(): message = jnp.concatenate([send_rows, code_rows], axis=1)]
    another operation x5 -> x3, other arithmetic: 2.37 us -> 1.08 us
  transfers between devices with their start and end apart: 3 -> 2, of which waited for: 1 -> 2; matrix products, arithmetic and copies ran while one was open for 4% -> 0% of each run, Pallas kernels for 0% -> 0%
where the time goes in v1:
time: 114 us; the launch traced here: 113 us
  blocking collectives  45.6 us (40%)
  Pallas kernels  21.7 us (19%)
  matrix products  13.8 us (12%)
  local copies, waits for them, and re-layouts  10.4 us (9%)
  starting transfers between devices  9.78 us (9%)
  other arithmetic  8.46 us (7%)
  waiting for transfers between devices  2.38 us (2%)
    all_to_all x1, blocking collectives, body(): lax.all_to_all(message, ('cell', 'own'), split_axis=0, concat_axis=0, til...  45.6 us
    pallas_call x1, Pallas kernels, fit_all(): pl.pallas_call(fit_kernel, out_shape=(jax.ShapeDtypeStruct((spec, count,...  21.7 us
    dot_general x1, matrix products, body(): sent = jnp.dot(place, payload, preferred_element_type=jnp.float32)  10.4 us
    ppermute x1, starting transfers between devices, with_halo(): lax.ppermute(lax.slice_in_dim(block, 0, width, axis=dim), axis, backward)  7.29 us
    add x1, other arithmetic, body(): target + weight[None, None, :] * lax.slice_in_dim(rimmed, W + shift, W +...  3.88 us
    dot_general x1, matrix products, body(): lax.dot_general(recv_rows, select, (((0,), (0,)), ((), ())), preferred_el...  3.37 us
    dot_general x1, local copies, waits for them, and re-layouts, body(): lax.dot_general(recv_rows, select, (((0,), (0,)), ((), ())), preferred_el...  2.91 us
    ppermute x1, starting transfers between devices, with_halo(): lax.ppermute(lax.slice_in_dim(block, block.shape[dim] - width, None, axis...  2.5 us
  transfers between devices with their start and end apart: 2, of which 2 were waited for; matrix products, arithmetic and copies ran while one was open for 0% of the time, Pallas kernels for 0%

profile of v1, /device:TPU:8, one launch (start us, length us, event | category | flops | bytes accessed | tf_op | source)
XLA Modules:
  0.0 112.9 jit_solution(282340694886314079)
XLA Ops:
  0.6 0.7 fusion.49
  1.4 0.8 copy.18
  2.2 1.1 copy.24
  3.3 0.3 fusion.42
  3.7 0.1 add_add_fusion
  3.8 0.0 copy-start
  3.8 0.3 copy.19
  4.1 0.6 fusion.41
  4.8 0.9 copy-done
  5.6 1.7 %reduce_sum.103 = bf16[2048,256]{1,0:T(8,128)(2,1)} reduce(bf16[2048,3,256]{2,0,1:T(8,128)(2,1)S(1)} %copy-done, bf16[]{:T(256)} %constant.32.clone.1), dimensions={1}, to_apply=%region_3.4 | reduce | flops 1048576 | bytes 4194306 | tf_op jit(solution)/shard_map/reduce_sum | solution.py:171
  7.4 10.4 %fusion.6 = bf16[4096,384]{1,0:T(8,128)(2,1)S(1)} fusion(s32[2048]{0:T(1024)S(1)} %multiply_add_fusion, bf16[2048,2]{1,0:T(8,128)(2,1)} %copy.24, bf16[2048,256]{1,0:T(8,128)(2,1)} %reduce_sum.103), kind=kOutput, calls=%fused_computation.7 | convolution fusion | flops 6457131008 | bytes 4210688 | tf_op jit(solution)/shard_map/dot_general | solution.py:182
  17.8 0.1 slice.89
  17.9 0.1 slice.88
  18.0 0.8 copy.21
  18.9 0.3 fusion.9
  19.1 45.6 %all_to_all.5 = bf16[128,40,256]{2,1,0:T(8,128)(2,1)S(1)} all-to-all(bf16[128,40,256]{2,1,0:T(8,128)(2,1)S(1)} %fusion.9), channel_id=1, replica_groups=mesh['cell'=32,'own'=4] {'cell','own'}, dimensions={0} | all-to-all | bytes 5242880 | tf_op jit(solution)/shard_map/all_to_all | solution.py:188
  64.7 0.4 fusion.46
  65.1 0.1 reshape.81
  65.2 1.6 %slice.90 = bf16[128,32,256]{2,1,0:T(8,128)(2,1)} slice(bf16[128,40,256]{2,1,0:T(8,128)(2,1)S(1)} %all_to_all.5), slice={[0:128], [0:32], [0:256]} | slice | bytes 4194304 | tf_op jit(solution)/shard_map/slice | solution.py:189
  66.8 2.9 %copy.22 = bf16[256,4096]{1,0:T(8,128)(2,1)S(1)} copy(bf16[256,4096]{0,1:T(8,128)(2,1)} %bitcast.22) | data formatting | bytes 4194304 | tf_op jit(solution)/shard_map/dot_general | solution.py:196
  69.7 3.4 %fusion.3 = f32[2,128,1024]{2,1,0:T(8,128)S(1)} fusion(bf16[2,128,4096]{2,1,0:T(8,128)(2,1)S(1)} %bitcast.24, s32[4096]{0:T(1024)S(1)} %reshape.81), kind=kOutput, calls=%fused_computation.5 | convolution fusion | flops 2151677952 | bytes 3162112 | tf_op jit(solution)/shard_map/dot_general | solution.py:196
  73.1 0.0 copy-start.2
  73.1 0.3 fusion.17
  73.4 0.1 fusion.56
  73.5 2.5 %collective-permute-start = (f32[2,128,4]{2,1,0:T(8,128)S(1)}, f32[2,128,4]{2,1,0:T(8,128)S(1)}, u32[]{:S(2)}, u32[]{:S(2)}) collective-permute-start(f32[2,128,4]{2,1,0:T(8,128)S(1)} %get-tuple-element.17), channel_id=1, source_target_pairs={{0,1},{1,2},{2,3},{3,4},{4,5},{5,6},{6,7},{7,8},{8,9},{9,10},{10,1... | collective-permute-start | bytes 12296 | tf_op jit(solution)/shard_map/ppermute | solution.py:23
  76.0 7.3 %collective-permute-start.1 = (f32[2,128,4]{2,1,0:T(8,128)S(1)}, f32[2,128,4]{2,1,0:T(8,128)S(1)}, u32[]{:S(2)}, u32[]{:S(2)}) collective-permute-start(f32[2,128,4]{2,1,0:T(8,128)S(1)} %get-tuple-element.18), channel_id=1, source_target_pairs={{1,0},{2,1},{3,2},{4,3},{5,4},{6,5},{7,6},{8,7},{9,8},{10,9},{11,1... | collective-permute-start | bytes 12296 | tf_op jit(solution)/shard_map/ppermute | solution.py:26
  83.3 0.1 convert_reduce_fusion.8
  83.4 0.6 collective-permute-done
  84.0 1.8 %collective-permute-done.1 = f32[2,128,4]{2,1,0:T(8,128)S(1)} collective-permute-done((f32[2,128,4]{2,1,0:T(8,128)S(1)}, f32[2,128,4]{2,1,0:T(8,128)S(1)}, u32[]{:S(2)}, u32[]{:S(2)}) %collective-permute-start.1) | collective-permute-done | bytes 4128 | tf_op jit(solution)/shard_map/ppermute | solution.py:26
  85.8 3.9 %fusion.21.t_ref = f32[2,128,1024]{2,1,0:T(8,128)} fusion(f32[2,128,1024]{2,1,0:T(8,128)S(1)} %fusion.17, f32[2,128,4]{2,1,0:T(8,128)S(1)} %collective-permute-done.1, f32[2,128,4]{2,1,0:T(8,128)S(1)} %collective-permute-done, f32[1024]{0:T(1024)S(1)} %get-tuple-element.15, f32[1024]{0:T(1024)S(1)} %get-tuple-element.16, f32[1024]{0:T(1024)S(1)} %get-tuple-element.9, ...), kind=kLoop, calls=%fused_computation.37 | loop fusion | flops 7077888 | bytes 2142208 | tf_op jit(solution)/shard_map/add | solution.py:205
  89.7 21.7 %shard_map.77 = (f32[2,6,1024]{2,1,0:T(8,128)}, f32[2,1024]{1,0:T(2,128)}) custom-call(f32[2,128,1024]{2,1,0:T(8,128)} %fusion.21.t_ref, f32[128,8]{1,0:T(8,128)} %constant.73.clone.phit_ref, f32[32,128]{1,0:T(8,128)} %constant.74.clone.psi_ref), custom_call_target="tpu_custom_call" | custom-call | tf_op jit(solution)/shard_map/pallas_call | solution.py:149
  111.4 1.5 %copy.23 = f32[2,6,1024]{2,0,1:T(2,128)} copy(f32[2,6,1024]{2,1,0:T(8,128)} %get-tuple-element.6) | data formatting | bytes 98304 | tf_op jit(solution)/shard_map/pallas_call | solution.py:149
  (10 shorter events, 0.1 us)
Async XLA Ops:
  3.3 0.8 copy-start.1
  3.8 1.9 %copy-start = (bf16[2048,3,256]{2,0,1:T(8,128)(2,1)S(1)}, bf16[2048,3,256]{2,0,1:T(8,128)(2,1)}, u32[]{:S(2)}) copy-start(bf16[2048,3,256]{2,0,1:T(8,128)(2,1)} %param.6) | copy-start | bytes 9437188
  73.1 10.2 %copy-start.2 = (s32[4,1024]{1,0:T(4,128)S(1)}, s32[4,1024]{1,0:T(4,128)}, u32[]{:S(2)}) copy-start(s32[4,1024]{1,0:T(4,128)} %param.9) | copy-start | bytes 49156
  73.5 10.5 %collective-permute-start = (f32[2,128,4]{2,1,0:T(8,128)S(1)}, f32[2,128,4]{2,1,0:T(8,128)S(1)}, u32[]{:S(2)}, u32[]{:S(2)}) collective-permute-start(f32[2,128,4]{2,1,0:T(8,128)S(1)} %get-tuple-element.17), channel_id=1, source_target_pairs={{0,1},{1,2},{2,3},{3,4},{4,5},{5,6},{6,7},{7,8},{8,9},{9,10},{10,1... | collective-permute-start | bytes 12296 | tf_op jit(solution)/shard_map/ppermute | solution.py:23
  76.0 9.8 %collective-permute-start.1 = (f32[2,128,4]{2,1,0:T(8,128)S(1)}, f32[2,128,4]{2,1,0:T(8,128)S(1)}, u32[]{:S(2)}, u32[]{:S(2)}) collective-permute-start(f32[2,128,4]{2,1,0:T(8,128)S(1)} %get-tuple-element.18), channel_id=1, source_target_pairs={{1,0},{2,1},{3,2},{4,3},{5,4},{6,5},{7,6},{8,7},{9,8},{10,9},{11,1... | collective-permute-start | bytes 12296 | tf_op jit(solution)/shard_map/ppermute | solution.py:26

commit v2 on v1

--- a/solution.py
+++ b/solution.py
@@ -9,35 +9,9 @@
 SPEC = 2
 MOM = 6
 NEWTON = 8
-NEIGH = 4
 W = 4
 CODE = 32
 EXTRA = 8
-
-
-def with_halo(block, sides, width):
-    for axis, dim in sides:
-        count = lax.axis_size(axis)
-        forward = [(i, i + 1) for i in range(count - 1)]
-        backward = [(target, source) for source, target in forward]
-        low = lax.ppermute(
-            lax.slice_in_dim(block, block.shape[dim] - width, None, axis=dim), axis, forward
-        )
-        high = lax.ppermute(lax.slice_in_dim(block, 0, width, axis=dim), axis, backward)
-        block = jnp.concatenate([low, block, high], axis=dim)
-    return block
-
-
-def legendre_table(levels, count):
-    xpos = (2.0 * jnp.arange(levels, dtype=jnp.float32) + 1.0) / levels - 1.0
-    prev = jnp.ones_like(xpos)
-    curr = xpos
-    table = [curr]
-    for order in range(1, count):
-        nxt = ((2 * order + 1) * xpos * curr - order * prev) / (order + 1)
-        prev, curr = (curr, nxt)
-        table.append(curr)
-    return jnp.stack(table, axis=0)
 
 
 def pair_list(count):
@@ -87,7 +61,7 @@
 
 
 def fit_kernel(t_ref, phit_ref, psi_ref, lam_ref, fit_ref, lam_s):
-    spec, levels, cells = t_ref.shape
+    spec, levels, _ = t_ref.shape
     count = lam_ref.shape[1]
     highest = lax.Precision.HIGHEST
 
@@ -161,7 +135,7 @@
     return 0.5 * field + 0.25 * (padded[:, :-2, :] + padded[:, 2:, :])
 
 
-def body(hist, dest, cell_in, offsets):
+def body_inner(hist, dest, cell_in, offsets):
     rows = hist.shape[0]
     width = hist.shape[2]
     cells = offsets.shape[1]
@@ -186,10 +160,25 @@
     code_rows = jnp.pad(code_rows, ((0, 0), (0, EXTRA - 2), (0, width - capacity)))
     message = jnp.concatenate([send_rows, code_rows], axis=1)
     got = lax.all_to_all(message, ("cell", "own"), split_axis=0, concat_axis=0, tiled=True)
-    recv_rows = got[:, :capacity, :].reshape(slots, width)
-    high = got[:, capacity, :capacity].astype(jnp.int32).reshape(slots)
-    low = got[:, capacity + 1, :capacity].astype(jnp.int32).reshape(slots)
+    lanes = capacity + EXTRA
+    recv_rows = got.reshape(devices * lanes, width)
+    high = got[:, capacity, :capacity].astype(jnp.int32)
+    low = got[:, capacity + 1, :capacity].astype(jnp.int32)
     recv_cells = jnp.where(high > 0, (high - 1) * CODE + low, -1)
+    recv_cells = jnp.pad(recv_cells, ((0, 0), (0, EXTRA)), constant_values=-1).reshape(devices * lanes)
+    edges = jnp.concatenate(
+        [jnp.arange(W, dtype=jnp.int32), jnp.arange(cells - W, cells, dtype=jnp.int32)]
+    )
+    edge_select = (recv_cells[:, None] == edges[None, :]).astype(jnp.bfloat16)
+    edge_sum = lax.dot_general(
+        recv_rows, edge_select, (((0,), (0,)), ((), ())), preferred_element_type=jnp.float32
+    )
+    edge_lev = smooth_levels(edge_sum.reshape(SPEC, width // SPEC, 2 * W))
+    count = devices
+    forward = [(i, i + 1) for i in range(count - 1)]
+    backward = [(target, source) for source, target in forward]
+    below = lax.ppermute(edge_lev[:, :, W:], ("cell", "own"), forward)
+    above = lax.ppermute(edge_lev[:, :, :W], ("cell", "own"), backward)
     select = (recv_cells[:, None] == jnp.arange(cells, dtype=jnp.int32)[None, :]).astype(
         jnp.bfloat16
     )
@@ -198,7 +187,7 @@
     )
     cellhist = summed.reshape(SPEC, width // SPEC, cells)
     levelled = smooth_levels(cellhist)
-    rimmed = with_halo(levelled, ((("cell", "own"), 2),), W)
+    rimmed = jnp.concatenate([below, levelled, above], axis=2)
     target = 1.0 + levelled
     for shift in range(-W, W + 1):
         weight = jnp.sum((offsets == shift).astype(jnp.float32), axis=0)
@@ -216,7 +205,7 @@
         P(None, ("cell", "own")),
     )
     return jax.shard_map(
-        body,
+        body_inner,
         mesh=mesh,
         in_specs=placed,
         out_specs=(P(None, None, ("cell", "own")), P(None, ("cell", "own"))),

time: 114 us -> 117 us (1.026)
  blocking collectives: 45.6 us -> 0 us
  waiting for transfers between devices: 2.38 us -> 42.8 us
  starting transfers between devices: 9.78 us -> 16.3 us
  matrix products: 13.8 us -> 17.4 us
  local copies, waits for them, and re-layouts: 10.4 us -> 7.81 us
    all_to_all x1 -> x0, blocking collectives: 45.6 us -> none  [body(): lax.all_to_all(message, ('cell', 'own'), split_axis=0, concat_axis=0, til...]
    all_to_all x0 -> x1, waiting for transfers between devices: none -> 35.1 us  [body_inner(): lax.all_to_all(message, ('cell', 'own'), split_axis=0, concat_axis=0, til...]
    all_to_all x0 -> x1, starting transfers between devices: none -> 10.4 us  [body_inner(): lax.all_to_all(message, ('cell', 'own'), split_axis=0, concat_axis=0, til...]
    ppermute x2, waiting for transfers between devices: 2.38 us -> 7.67 us  [the longest x1 6.14 us: body_inner(): below = lax.ppermute(edge_lev[:, :, W:], ('cell', 'own'), forward)]
    ppermute x2, starting transfers between devices: 9.78 us -> 5.84 us  [the longest x1 3.29 us: body_inner(): above = lax.ppermute(edge_lev[:, :, :W], ('cell', 'own'), backward)]
    dot_general x2 -> x3, matrix products: 13.8 us -> 17.4 us  [the longest x1 10.4 us: body_inner(): sent = jnp.dot(place, payload, preferred_element_type=jnp.float32)]
    slice x4 -> x3, local copies, waits for them, and re-layouts: 1.95 us -> 0.3 us  [the longest x1 0.14 us: body_inner(): sent[:, :width].astype(jnp.bfloat16).reshape(devices, capacity, width)]
    concatenate x1 -> x2, other arithmetic: 0.27 us -> 1.85 us  [the longest x1 1.78 us: body_inner(): message = jnp.concatenate([send_rows, code_rows], axis=1)]
  transfers between devices with their start and end apart: 2 -> 3, of which waited for: 2 -> 3; matrix products, arithmetic and copies ran while one was open for 0% -> 0% of each run, Pallas kernels for 0% -> 0%
where the time goes in v2:
time: 117 us; the launch traced here: 116 us
  waiting for transfers between devices  42.8 us (37%)
  Pallas kernels  21.7 us (19%)
  matrix products  17.4 us (15%)
  starting transfers between devices  16.3 us (14%)
  other arithmetic  9.22 us (8%)
  local copies, waits for them, and re-layouts  7.81 us (7%)
    all_to_all x1, waiting for transfers between devices, body_inner(): lax.all_to_all(message, ('cell', 'own'), split_axis=0, concat_axis=0, til...  35.1 us
    pallas_call x1, Pallas kernels, fit_all(): pl.pallas_call(fit_kernel, out_shape=(jax.ShapeDtypeStruct((spec, count,...  21.7 us
    all_to_all x1, starting transfers between devices, body_inner(): lax.all_to_all(message, ('cell', 'own'), split_axis=0, concat_axis=0, til...  10.4 us
    dot_general x1, matrix products, body_inner(): sent = jnp.dot(place, payload, preferred_element_type=jnp.float32)  10.4 us
    ppermute x1, waiting for transfers between devices, body_inner(): below = lax.ppermute(edge_lev[:, :, W:], ('cell', 'own'), forward)  6.14 us
    dot_general x1, matrix products, body_inner(): lax.dot_general(recv_rows, select, (((0,), (0,)), ((), ())), preferred_el...  6.05 us
    add x1, other arithmetic, body_inner(): target + weight[None, None, :] * lax.slice_in_dim(rimmed, W + shift, W +...  3.87 us
    ppermute x1, starting transfers between devices, body_inner(): above = lax.ppermute(edge_lev[:, :, :W], ('cell', 'own'), backward)  3.29 us
  transfers between devices with their start and end apart: 3, of which 3 were waited for; matrix products, arithmetic and copies ran while one was open for 0% of the time, Pallas kernels for 0%

profile of v2, /device:TPU:8, one launch (start us, length us, event | category | flops | bytes accessed | tf_op | source)
XLA Modules:
  0.0 116.1 jit_solution(15323233487127972792)
XLA Ops:
  0.6 0.8 copy.30
  1.4 0.3 fusion.42
  1.8 0.1 add_add_fusion
  1.9 0.0 copy-start
  1.9 0.3 copy.31
  2.3 0.0 copy-done.2
  2.3 0.6 fusion.41
  3.0 1.1 copy.40
  4.1 1.7 %reduce_sum.103 = bf16[2048,256]{1,0:T(8,128)(2,1)} reduce(bf16[2048,3,256]{2,0,1:T(8,128)(2,1)S(1)} %copy-done, bf16[]{:T(256)} %constant.30.clone.1), dimensions={1}, to_apply=%region_3.4 | reduce | flops 1048576 | bytes 4194306 | tf_op jit(solution)/shard_map/reduce_sum | solution.py:145
  5.9 10.4 %fusion.6 = bf16[4096,384]{1,0:T(8,128)(2,1)S(1)} fusion(s32[2048]{0:T(1024)S(1)} %multiply_add_fusion, bf16[2048,2]{1,0:T(8,128)(2,1)} %copy.40, bf16[2048,256]{1,0:T(8,128)(2,1)} %reduce_sum.103), kind=kOutput, calls=%fused_computation.7 | convolution fusion | flops 6457131008 | bytes 4210688 | tf_op jit(solution)/shard_map/dot_general | solution.py:156
  16.3 0.1 slice.93
  16.4 0.1 slice.92
  16.5 0.8 copy.33
  17.3 1.8 %fusion.9 = bf16[128,40,256]{2,1,0:T(8,128)(2,1)} fusion(bf16[128,2,32]{2,1,0:T(2,128)(2,1)S(1)} %bitcast.31, bf16[128,32,256]{2,1,0:T(8,128)(2,1)S(1)} %bitcast.27), kind=kLoop, calls=%fused_computation.12 | loop fusion | flops 7864320 | bytes 4734976 | tf_op jit(solution)/shard_map/concatenate | solution.py:161
  19.1 10.4 %all-to-all-start = ((bf16[128,40,256]{2,1,0:T(8,128)(2,1)}), bf16[128,40,256]{2,1,0:T(8,128)(2,1)S(1)}, u32[]{:S(2)}, u32[]{:S(2)}) async-start(bf16[128,40,256]{2,1,0:T(8,128)(2,1)} %fusion.9), calls=%async_computation | async-start | bytes 5242880 | tf_op jit(solution)/shard_map/all_to_all | solution.py:162
  29.6 0.1 pad_add_fusion
  29.7 0.1 convert_reduce_fusion.8
  29.8 35.1 %all-to-all-done = bf16[128,40,256]{2,1,0:T(8,128)(2,1)S(1)} async-done(((bf16[128,40,256]{2,1,0:T(8,128)(2,1)}), bf16[128,40,256]{2,1,0:T(8,128)(2,1)S(1)}, u32[]{:S(2)}, u32[]{:S(2)}) %all-to-all-start) | async-done | bytes 2621472 | tf_op jit(solution)/shard_map/all_to_all | solution.py:162
  64.9 2.8 %copy.34 = bf16[256,5120]{1,0:T(8,128)(2,1)} copy(bf16[256,5120]{0,1:T(8,128)(2,1)S(1)} %bitcast.26) | data formatting | bytes 5242880 | tf_op jit(solution)/shard_map/dot_general | solution.py:185
  67.7 0.2 compare_select_fusion
  67.9 0.1 eq.130
  68.0 6.1 %fusion.2 = f32[2,128,1024]{2,1,0:T(8,128)S(1)} fusion(bf16[2,128,5120]{2,1,0:T(8,128)(2,1)} %bitcast.29, s32[5120]{0:T(1024)S(1)} %eq.130), kind=kOutput, calls=%fused_computation.4 | convolution fusion | flops 2689597440 | bytes 3690496 | tf_op jit(solution)/shard_map/dot_general | solution.py:185
  74.1 0.9 fusion.46
  75.0 0.1 fusion.63
  75.1 3.3 %collective-permute-start.1 = (f32[2,128,4]{2,1,0:T(8,128)S(1)}, f32[2,128,4]{2,1,0:T(8,128)S(1)}, u32[]{:S(2)}, u32[]{:S(2)}) collective-permute-start(f32[2,128,4]{2,1,0:T(8,128)S(1)} %get-tuple-element.20), channel_id=1, source_target_pairs={{1,0},{2,1},{3,2},{4,3},{5,4},{6,5},{7,6},{8,7},{9,8},{10,9},{11,1... | collective-permute-start | bytes 12296 | tf_op jit(solution)/shard_map/ppermute | solution.py:181
  78.5 2.5 %collective-permute-start = (f32[2,128,4]{2,1,0:T(8,128)S(1)}, f32[2,128,4]{2,1,0:T(8,128)S(1)}, u32[]{:S(2)}, u32[]{:S(2)}) collective-permute-start(f32[2,128,4]{2,1,0:T(8,128)S(1)} %get-tuple-element.19), channel_id=1, source_target_pairs={{0,1},{1,2},{2,3},{3,4},{4,5},{5,6},{6,7},{7,8},{8,9},{9,10},{10,1... | collective-permute-start | bytes 12296 | tf_op jit(solution)/shard_map/ppermute | solution.py:180
  81.0 0.3 fusion.17
  81.3 1.5 %collective-permute-done.1 = f32[2,128,4]{2,1,0:T(8,128)S(1)} collective-permute-done((f32[2,128,4]{2,1,0:T(8,128)S(1)}, f32[2,128,4]{2,1,0:T(8,128)S(1)}, u32[]{:S(2)}, u32[]{:S(2)}) %collective-permute-start.1) | collective-permute-done | bytes 4128 | tf_op jit(solution)/shard_map/ppermute | solution.py:181
  82.8 6.1 %collective-permute-done = f32[2,128,4]{2,1,0:T(8,128)S(1)} collective-permute-done((f32[2,128,4]{2,1,0:T(8,128)S(1)}, f32[2,128,4]{2,1,0:T(8,128)S(1)}, u32[]{:S(2)}, u32[]{:S(2)}) %collective-permute-start) | collective-permute-done | bytes 4128 | tf_op jit(solution)/shard_map/ppermute | solution.py:180
  89.0 3.9 %fusion.21.t_ref = f32[2,128,1024]{2,1,0:T(8,128)} fusion(f32[2,128,1024]{2,1,0:T(8,128)S(1)} %fusion.17, f32[2,128,4]{2,1,0:T(8,128)S(1)} %collective-permute-done.1, f32[2,128,4]{2,1,0:T(8,128)S(1)} %collective-permute-done, f32[1024]{0:T(1024)S(1)} %get-tuple-element.17, f32[1024]{0:T(1024)S(1)} %get-tuple-element.18, f32[1024]{0:T(1024)S(1)} %get-tuple-element.11, ...), kind=kLoop, calls=%fused_computation.37 | loop fusion | flops 7077888 | bytes 2142208 | tf_op jit(solution)/shard_map/add | solution.py:194
  92.8 21.7 %shard_map.77 = (f32[2,6,1024]{2,1,0:T(8,128)}, f32[2,1024]{1,0:T(2,128)}) custom-call(f32[2,128,1024]{2,1,0:T(8,128)} %fusion.21.t_ref, f32[128,8]{1,0:T(8,128)} %constant.77.clone.phit_ref, f32[32,128]{1,0:T(8,128)} %constant.78.clone.psi_ref), custom_call_target="tpu_custom_call" | custom-call | tf_op jit(solution)/shard_map/pallas_call | solution.py:123
  114.6 1.5 %copy.38 = f32[2,6,1024]{2,0,1:T(2,128)} copy(f32[2,6,1024]{2,1,0:T(8,128)} %get-tuple-element.8) | data formatting | bytes 98304 | tf_op jit(solution)/shard_map/pallas_call | solution.py:123
  (20 shorter events, 0.2 us)
Async XLA Ops:
  1.4 0.9 copy-start.2
  1.8 1.1 copy-start.4
  1.9 2.2 %copy-start = (bf16[2048,3,256]{2,0,1:T(8,128)(2,1)S(1)}, bf16[2048,3,256]{2,0,1:T(8,128)(2,1)}, u32[]{:S(2)}) copy-start(bf16[2048,3,256]{2,0,1:T(8,128)(2,1)} %param.6) | copy-start | bytes 9437188
  19.1 10.6 %copy-start.3 = (s32[4,1024]{1,0:T(4,128)S(1)}, s32[4,1024]{1,0:T(4,128)}, u32[]{:S(2)}) copy-start(s32[4,1024]{1,0:T(4,128)} %param.9) | copy-start | bytes 49156
  19.1 45.8 %all-to-all-start = ((bf16[128,40,256]{2,1,0:T(8,128)(2,1)}), bf16[128,40,256]{2,1,0:T(8,128)(2,1)S(1)}, u32[]{:S(2)}, u32[]{:S(2)}) async-start(bf16[128,40,256]{2,1,0:T(8,128)(2,1)} %fusion.9), calls=%async_computation | async-start | bytes 5242880 | tf_op jit(solution)/shard_map/all_to_all | solution.py:162
  68.0 6.1 %copy-start.1 = (bf16[256,5120]{1,0:T(8,128)(2,1)S(1)}, bf16[256,5120]{1,0:T(8,128)(2,1)}, u32[]{:S(2)}) copy-start(bf16[256,5120]{1,0:T(8,128)(2,1)} %copy.34) | copy-start | bytes 7864324
  75.1 7.7 %collective-permute-start.1 = (f32[2,128,4]{2,1,0:T(8,128)S(1)}, f32[2,128,4]{2,1,0:T(8,128)S(1)}, u32[]{:S(2)}, u32[]{:S(2)}) collective-permute-start(f32[2,128,4]{2,1,0:T(8,128)S(1)} %get-tuple-element.20), channel_id=1, source_target_pairs={{1,0},{2,1},{3,2},{4,3},{5,4},{6,5},{7,6},{8,7},{9,8},{10,9},{11,1... | collective-permute-start | bytes 12296 | tf_op jit(solution)/shard_map/ppermute | solution.py:181
  78.5 10.5 %collective-permute-start = (f32[2,128,4]{2,1,0:T(8,128)S(1)}, f32[2,128,4]{2,1,0:T(8,128)S(1)}, u32[]{:S(2)}, u32[]{:S(2)}) collective-permute-start(f32[2,128,4]{2,1,0:T(8,128)S(1)} %get-tuple-element.19), channel_id=1, source_target_pairs={{0,1},{1,2},{2,3},{3,4},{4,5},{5,6},{6,7},{7,8},{8,9},{9,10},{10,1... | collective-permute-start | bytes 12296 | tf_op jit(solution)/shard_map/ppermute | solution.py:180

commit v3 on v2

--- a/solution.py
+++ b/solution.py
@@ -46,46 +46,62 @@
 
 def newton_step(got, moments, lam, count):
     pairs = pair_list(count)
-    norm = got[count : count + 1]
-    first = [got[m : m + 1] / norm for m in range(count)]
+    norm = got[count]
+    first = [got[m] / norm for m in range(count)]
     hess = [[None] * count for _ in range(count)]
     for k, (row, col) in enumerate(pairs):
-        second = got[count + 1 + k : count + 2 + k] / norm
+        second = got[count + 1 + k] / norm
         value = second - first[row] * first[col]
         if row == col:
             value = value + 0.01
         hess[row][col] = value
     rhs = [first[m] - moments[m] for m in range(count)]
     delta = chol_solve(hess, rhs, count)
-    return [lam[m : m + 1] - 0.5 * delta[m] for m in range(count)]
-
-
-def fit_kernel(t_ref, phit_ref, psi_ref, lam_ref, fit_ref, lam_s):
-    spec, levels, _ = t_ref.shape
+    return [lam[m] - 0.5 * delta[m] for m in range(count)]
+
+
+def fit_kernel(t_ref, phit_ref, psi_ref, lam_ref, fit_ref, lam_s, dense_ref):
+    spec, levels, cells = t_ref.shape
     count = lam_ref.shape[1]
+    used = count + 1 + len(pair_list(count))
+    groups = 8 // spec
+    part = cells // groups
     highest = lax.Precision.HIGHEST
 
     def contract(a, b):
         return jnp.dot(a, b, precision=highest, preferred_element_type=jnp.float32)
 
-    moments = []
-    for s in range(spec):
-        got = contract(psi_ref[...], t_ref[s])
-        total = got[count : count + 1]
-        moments.append([got[m : m + 1] / total for m in range(count)])
+    def densify(gots):
+        for s in range(spec):
+            for j in range(groups):
+                piece = gots[s][:, j * part : (j + 1) * part]
+                row = s * groups + j
+                for k in range(used):
+                    dense_ref[k, row : row + 1, :] = piece[k : k + 1, :]
+        return [dense_ref[k] for k in range(used)]
+
+    def spread(values):
+        for m in range(count):
+            for s in range(spec):
+                for j in range(groups):
+                    row = s * groups + j
+                    lam_s[s, m : m + 1, j * part : (j + 1) * part] = values[m][row : row + 1, :]
+
+    got = densify([contract(psi_ref[...], t_ref[s]) for s in range(spec)])
+    moments = [got[m] / got[count] for m in range(count)]
     lam_s[...] = jnp.zeros(lam_s.shape, jnp.float32)
-
-    def step(_, carry):
+    zero = jnp.zeros((8, part), jnp.float32)
+
+    def step(_, lam):
+        gots = []
         for s in range(spec):
-            lam = lam_s[s]
-            expo = jnp.exp(contract(phit_ref[...], lam))
-            got = contract(psi_ref[...], expo)
-            new = newton_step(got, moments[s], lam, count)
-            for m in range(count):
-                lam_s[s, m : m + 1, :] = new[m]
-        return carry
-
-    lax.fori_loop(0, NEWTON, step, 0)
+            expo = jnp.exp(contract(phit_ref[...], lam_s[s]))
+            gots.append(contract(psi_ref[...], expo))
+        new = newton_step(densify(gots), moments, list(lam), count)
+        spread(new)
+        return tuple(new)
+
+    lax.fori_loop(0, NEWTON, step, tuple([zero] * count))
     for s in range(spec):
         target = t_ref[s]
         exponent = contract(phit_ref[...], lam_s[s])
@@ -126,7 +142,10 @@
             jax.ShapeDtypeStruct((spec, count, cells), jnp.float32),
             jax.ShapeDtypeStruct((spec, cells), jnp.float32),
         ),
-        scratch_shapes=[pltpu.VMEM((spec, width, cells), jnp.float32)],
+        scratch_shapes=[
+            pltpu.VMEM((spec, width, cells), jnp.float32),
+            pltpu.VMEM((height, 8, cells * spec // 8), jnp.float32),
+        ],
     )(target, jnp.asarray(phit), jnp.asarray(psi))
 
 

time: 117 us -> 112 us (0.957)
  Pallas kernels: 21.7 us -> 16.9 us
    pallas_call x1, Pallas kernels: 21.7 us -> 16.9 us  [fit_all(): pl.pallas_call(fit_kernel, out_shape=(jax.ShapeDtypeStruct((spec, count,...]
where the time goes in v3:
time: 112 us; the launch traced here: 111 us
  waiting for transfers between devices  42.8 us (38%)
  matrix products  17.4 us (16%)
  Pallas kernels  16.9 us (15%)
  starting transfers between devices  16.3 us (15%)
  other arithmetic  9.22 us (8%)
  local copies, waits for them, and re-layouts  7.81 us (7%)
    all_to_all x1, waiting for transfers between devices, body_inner(): lax.all_to_all(message, ('cell', 'own'), split_axis=0, concat_axis=0, til...  35.1 us
    pallas_call x1, Pallas kernels, fit_all(): pl.pallas_call(fit_kernel, out_shape=(jax.ShapeDtypeStruct((spec, count,...  16.9 us
    all_to_all x1, starting transfers between devices, body_inner(): lax.all_to_all(message, ('cell', 'own'), split_axis=0, concat_axis=0, til...  10.4 us
    dot_general x1, matrix products, body_inner(): sent = jnp.dot(place, payload, preferred_element_type=jnp.float32)  10.4 us
    ppermute x1, waiting for transfers between devices, body_inner(): below = lax.ppermute(edge_lev[:, :, W:], ('cell', 'own'), forward)  6.14 us
    dot_general x1, matrix products, body_inner(): lax.dot_general(recv_rows, select, (((0,), (0,)), ((), ())), preferred_el...  6.05 us
    add x1, other arithmetic, body_inner(): target + weight[None, None, :] * lax.slice_in_dim(rimmed, W + shift, W +...  3.87 us
    ppermute x1, starting transfers between devices, body_inner(): above = lax.ppermute(edge_lev[:, :, :W], ('cell', 'own'), backward)  3.29 us
  transfers between devices with their start and end apart: 3, of which 3 were waited for; matrix products, arithmetic and copies ran while one was open for 0% of the time, Pallas kernels for 0%

profile of v3, /device:TPU:8, one launch (start us, length us, event | category | flops | bytes accessed | tf_op | source)
XLA Modules:
  0.0 111.2 jit_solution(13608735719532311346)
XLA Ops:
  0.6 0.8 copy.30
  1.4 0.3 fusion.42
  1.8 0.1 add_add_fusion
  1.9 0.0 copy-start
  1.9 0.3 copy.31
  2.3 0.0 copy-done.2
  2.3 0.6 fusion.41
  3.0 1.1 copy.40
  4.1 1.7 %reduce_sum.103 = bf16[2048,256]{1,0:T(8,128)(2,1)} reduce(bf16[2048,3,256]{2,0,1:T(8,128)(2,1)S(1)} %copy-done, bf16[]{:T(256)} %constant.30.clone.1), dimensions={1}, to_apply=%region_3.4 | reduce | flops 1048576 | bytes 4194306 | tf_op jit(solution)/shard_map/reduce_sum | solution.py:164
  5.9 10.4 %fusion.6 = bf16[4096,384]{1,0:T(8,128)(2,1)S(1)} fusion(s32[2048]{0:T(1024)S(1)} %multiply_add_fusion, bf16[2048,2]{1,0:T(8,128)(2,1)} %copy.40, bf16[2048,256]{1,0:T(8,128)(2,1)} %reduce_sum.103), kind=kOutput, calls=%fused_computation.7 | convolution fusion | flops 6457131008 | bytes 4210688 | tf_op jit(solution)/shard_map/dot_general | solution.py:175
  16.3 0.1 slice.93
  16.4 0.1 slice.92
  16.5 0.8 copy.33
  17.3 1.8 %fusion.9 = bf16[128,40,256]{2,1,0:T(8,128)(2,1)} fusion(bf16[128,2,32]{2,1,0:T(2,128)(2,1)S(1)} %bitcast.31, bf16[128,32,256]{2,1,0:T(8,128)(2,1)S(1)} %bitcast.27), kind=kLoop, calls=%fused_computation.12 | loop fusion | flops 7864320 | bytes 4734976 | tf_op jit(solution)/shard_map/concatenate | solution.py:180
  19.1 10.4 %all-to-all-start = ((bf16[128,40,256]{2,1,0:T(8,128)(2,1)}), bf16[128,40,256]{2,1,0:T(8,128)(2,1)S(1)}, u32[]{:S(2)}, u32[]{:S(2)}) async-start(bf16[128,40,256]{2,1,0:T(8,128)(2,1)} %fusion.9), calls=%async_computation | async-start | bytes 5242880 | tf_op jit(solution)/shard_map/all_to_all | solution.py:181
  29.6 0.1 pad_add_fusion
  29.7 0.1 convert_reduce_fusion.8
  29.8 35.1 %all-to-all-done = bf16[128,40,256]{2,1,0:T(8,128)(2,1)S(1)} async-done(((bf16[128,40,256]{2,1,0:T(8,128)(2,1)}), bf16[128,40,256]{2,1,0:T(8,128)(2,1)S(1)}, u32[]{:S(2)}, u32[]{:S(2)}) %all-to-all-start) | async-done | bytes 2621472 | tf_op jit(solution)/shard_map/all_to_all | solution.py:181
  64.9 2.8 %copy.34 = bf16[256,5120]{1,0:T(8,128)(2,1)} copy(bf16[256,5120]{0,1:T(8,128)(2,1)S(1)} %bitcast.26) | data formatting | bytes 5242880 | tf_op jit(solution)/shard_map/dot_general | solution.py:204
  67.7 0.2 compare_select_fusion
  67.9 0.1 eq.130
  68.0 6.1 %fusion.2 = f32[2,128,1024]{2,1,0:T(8,128)S(1)} fusion(bf16[2,128,5120]{2,1,0:T(8,128)(2,1)} %bitcast.29, s32[5120]{0:T(1024)S(1)} %eq.130), kind=kOutput, calls=%fused_computation.4 | convolution fusion | flops 2689597440 | bytes 3690496 | tf_op jit(solution)/shard_map/dot_general | solution.py:204
  74.1 0.9 fusion.46
  75.0 0.1 fusion.63
  75.1 3.3 %collective-permute-start.1 = (f32[2,128,4]{2,1,0:T(8,128)S(1)}, f32[2,128,4]{2,1,0:T(8,128)S(1)}, u32[]{:S(2)}, u32[]{:S(2)}) collective-permute-start(f32[2,128,4]{2,1,0:T(8,128)S(1)} %get-tuple-element.20), channel_id=1, source_target_pairs={{1,0},{2,1},{3,2},{4,3},{5,4},{6,5},{7,6},{8,7},{9,8},{10,9},{11,1... | collective-permute-start | bytes 12296 | tf_op jit(solution)/shard_map/ppermute | solution.py:200
  78.5 2.5 %collective-permute-start = (f32[2,128,4]{2,1,0:T(8,128)S(1)}, f32[2,128,4]{2,1,0:T(8,128)S(1)}, u32[]{:S(2)}, u32[]{:S(2)}) collective-permute-start(f32[2,128,4]{2,1,0:T(8,128)S(1)} %get-tuple-element.19), channel_id=1, source_target_pairs={{0,1},{1,2},{2,3},{3,4},{4,5},{5,6},{6,7},{7,8},{8,9},{9,10},{10,1... | collective-permute-start | bytes 12296 | tf_op jit(solution)/shard_map/ppermute | solution.py:199
  81.0 0.3 fusion.17
  81.3 1.5 %collective-permute-done.1 = f32[2,128,4]{2,1,0:T(8,128)S(1)} collective-permute-done((f32[2,128,4]{2,1,0:T(8,128)S(1)}, f32[2,128,4]{2,1,0:T(8,128)S(1)}, u32[]{:S(2)}, u32[]{:S(2)}) %collective-permute-start.1) | collective-permute-done | bytes 4128 | tf_op jit(solution)/shard_map/ppermute | solution.py:200
  82.8 6.1 %collective-permute-done = f32[2,128,4]{2,1,0:T(8,128)S(1)} collective-permute-done((f32[2,128,4]{2,1,0:T(8,128)S(1)}, f32[2,128,4]{2,1,0:T(8,128)S(1)}, u32[]{:S(2)}, u32[]{:S(2)}) %collective-permute-start) | collective-permute-done | bytes 4128 | tf_op jit(solution)/shard_map/ppermute | solution.py:199
  89.0 3.9 %fusion.21.t_ref = f32[2,128,1024]{2,1,0:T(8,128)} fusion(f32[2,128,1024]{2,1,0:T(8,128)S(1)} %fusion.17, f32[2,128,4]{2,1,0:T(8,128)S(1)} %collective-permute-done.1, f32[2,128,4]{2,1,0:T(8,128)S(1)} %collective-permute-done, f32[1024]{0:T(1024)S(1)} %get-tuple-element.17, f32[1024]{0:T(1024)S(1)} %get-tuple-element.18, f32[1024]{0:T(1024)S(1)} %get-tuple-element.11, ...), kind=kLoop, calls=%fused_computation.37 | loop fusion | flops 7077888 | bytes 2142208 | tf_op jit(solution)/shard_map/add | solution.py:213
  92.8 16.9 %shard_map.77 = (f32[2,6,1024]{2,1,0:T(8,128)}, f32[2,1024]{1,0:T(2,128)}) custom-call(f32[2,128,1024]{2,1,0:T(8,128)} %fusion.21.t_ref, f32[128,8]{1,0:T(8,128)} %constant.77.clone.phit_ref, f32[32,128]{1,0:T(8,128)} %constant.78.clone.psi_ref), custom_call_target="tpu_custom_call" | custom-call | tf_op jit(solution)/shard_map/pallas_call | solution.py:139
  109.7 1.5 %copy.38 = f32[2,6,1024]{2,0,1:T(2,128)} copy(f32[2,6,1024]{2,1,0:T(8,128)} %get-tuple-element.8) | data formatting | bytes 98304 | tf_op jit(solution)/shard_map/pallas_call | solution.py:139
  (20 shorter events, 0.2 us)
Async XLA Ops:
  1.4 0.9 copy-start.2
  1.8 1.1 copy-start.4
  1.9 2.2 %copy-start = (bf16[2048,3,256]{2,0,1:T(8,128)(2,1)S(1)}, bf16[2048,3,256]{2,0,1:T(8,128)(2,1)}, u32[]{:S(2)}) copy-start(bf16[2048,3,256]{2,0,1:T(8,128)(2,1)} %param.6) | copy-start | bytes 9437188
  19.1 10.6 %copy-start.3 = (s32[4,1024]{1,0:T(4,128)S(1)}, s32[4,1024]{1,0:T(4,128)}, u32[]{:S(2)}) copy-start(s32[4,1024]{1,0:T(4,128)} %param.9) | copy-start | bytes 49156
  19.1 45.8 %all-to-all-start = ((bf16[128,40,256]{2,1,0:T(8,128)(2,1)}), bf16[128,40,256]{2,1,0:T(8,128)(2,1)S(1)}, u32[]{:S(2)}, u32[]{:S(2)}) async-start(bf16[128,40,256]{2,1,0:T(8,128)(2,1)} %fusion.9), calls=%async_computation | async-start | bytes 5242880 | tf_op jit(solution)/shard_map/all_to_all | solution.py:181
  68.0 6.1 %copy-start.1 = (bf16[256,5120]{1,0:T(8,128)(2,1)S(1)}, bf16[256,5120]{1,0:T(8,128)(2,1)}, u32[]{:S(2)}) copy-start(bf16[256,5120]{1,0:T(8,128)(2,1)} %copy.34) | copy-start | bytes 7864324
  75.1 7.7 %collective-permute-start.1 = (f32[2,128,4]{2,1,0:T(8,128)S(1)}, f32[2,128,4]{2,1,0:T(8,128)S(1)}, u32[]{:S(2)}, u32[]{:S(2)}) collective-permute-start(f32[2,128,4]{2,1,0:T(8,128)S(1)} %get-tuple-element.20), channel_id=1, source_target_pairs={{1,0},{2,1},{3,2},{4,3},{5,4},{6,5},{7,6},{8,7},{9,8},{10,9},{11,1... | collective-permute-start | bytes 12296 | tf_op jit(solution)/shard_map/ppermute | solution.py:200
  78.5 10.5 %collective-permute-start = (f32[2,128,4]{2,1,0:T(8,128)S(1)}, f32[2,128,4]{2,1,0:T(8,128)S(1)}, u32[]{:S(2)}, u32[]{:S(2)}) collective-permute-start(f32[2,128,4]{2,1,0:T(8,128)S(1)} %get-tuple-element.19), channel_id=1, source_target_pairs={{0,1},{1,2},{2,3},{3,4},{4,5},{5,6},{6,7},{7,8},{8,9},{9,10},{10,1... | collective-permute-start | bytes 12296 | tf_op jit(solution)/shard_map/ppermute | solution.py:199

commit v4 on v3

--- a/solution.py
+++ b/solution.py
@@ -12,6 +12,7 @@
 W = 4
 CODE = 32
 EXTRA = 8
+LOOP_PRECISION = lax.Precision.HIGH
 
 
 def pair_list(count):
@@ -68,8 +69,8 @@
     part = cells // groups
     highest = lax.Precision.HIGHEST
 
-    def contract(a, b):
-        return jnp.dot(a, b, precision=highest, preferred_element_type=jnp.float32)
+    def contract(a, b, precision=highest):
+        return jnp.dot(a, b, precision=precision, preferred_element_type=jnp.float32)
 
     def densify(gots):
         for s in range(spec):
@@ -95,8 +96,8 @@
     def step(_, lam):
         gots = []
         for s in range(spec):
-            expo = jnp.exp(contract(phit_ref[...], lam_s[s]))
-            gots.append(contract(psi_ref[...], expo))
+            expo = jnp.exp(contract(phit_ref[...], lam_s[s], LOOP_PRECISION))
+            gots.append(contract(psi_ref[...], expo, LOOP_PRECISION))
         new = newton_step(densify(gots), moments, list(lam), count)
         spread(new)
         return tuple(new)

time: 112 us -> 107 us (0.955)
  Pallas kernels: 16.9 us -> 12 us
    pallas_call x1, Pallas kernels: 16.9 us -> 12 us  [fit_all(): pl.pallas_call(fit_kernel, out_shape=(jax.ShapeDtypeStruct((spec, count,...]
where the time goes in v4:
time: 107 us; the launch traced here: 106 us
  waiting for transfers between devices  42.8 us (40%)
  matrix products  17.4 us (16%)
  starting transfers between devices  16.3 us (15%)
  Pallas kernels  12 us (11%)
  other arithmetic  9.22 us (9%)
  local copies, waits for them, and re-layouts  7.81 us (7%)
    all_to_all x1, waiting for transfers between devices, body_inner(): lax.all_to_all(message, ('cell', 'own'), split_axis=0, concat_axis=0, til...  35.1 us
    pallas_call x1, Pallas kernels, fit_all(): pl.pallas_call(fit_kernel, out_shape=(jax.ShapeDtypeStruct((spec, count,...  12 us
    all_to_all x1, starting transfers between devices, body_inner(): lax.all_to_all(message, ('cell', 'own'), split_axis=0, concat_axis=0, til...  10.4 us
    dot_general x1, matrix products, body_inner(): sent = jnp.dot(place, payload, preferred_element_type=jnp.float32)  10.4 us
    ppermute x1, waiting for transfers between devices, body_inner(): below = lax.ppermute(edge_lev[:, :, W:], ('cell', 'own'), forward)  6.14 us
    dot_general x1, matrix products, body_inner(): lax.dot_general(recv_rows, select, (((0,), (0,)), ((), ())), preferred_el...  6.05 us
    add x1, other arithmetic, body_inner(): target + weight[None, None, :] * lax.slice_in_dim(rimmed, W + shift, W +...  3.87 us
    ppermute x1, starting transfers between devices, body_inner(): above = lax.ppermute(edge_lev[:, :, :W], ('cell', 'own'), backward)  3.29 us
  transfers between devices with their start and end apart: 3, of which 3 were waited for; matrix products, arithmetic and copies ran while one was open for 0% of the time, Pallas kernels for 0%

profile of v4, /device:TPU:8, one launch (start us, length us, event | category | flops | bytes accessed | tf_op | source)
XLA Modules:
  0.0 106.3 jit_solution(61883631789049863)
XLA Ops:
  0.6 0.8 copy.30
  1.4 0.3 fusion.42
  1.8 0.1 add_add_fusion
  1.9 0.0 copy-start
  1.9 0.3 copy.31
  2.3 0.0 copy-done.2
  2.3 0.6 fusion.41
  3.0 1.1 %copy.40 = bf16[2048,2]{1,0:T(8,128)(2,1)} copy(bf16[2048,2]{0,1:T(2,128)(2,1)S(1)} %pad_maximum_fusion.2) | data formatting | bytes 16384
  4.1 1.7 %reduce_sum.103 = bf16[2048,256]{1,0:T(8,128)(2,1)} reduce(bf16[2048,3,256]{2,0,1:T(8,128)(2,1)S(1)} %copy-done, bf16[]{:T(256)} %constant.30.clone.1), dimensions={1}, to_apply=%region_3.4 | reduce | flops 1048576 | bytes 4194306 | tf_op jit(solution)/shard_map/reduce_sum | solution.py:165
  5.9 10.4 %fusion.6 = bf16[4096,384]{1,0:T(8,128)(2,1)S(1)} fusion(s32[2048]{0:T(1024)S(1)} %multiply_add_fusion, bf16[2048,2]{1,0:T(8,128)(2,1)} %copy.40, bf16[2048,256]{1,0:T(8,128)(2,1)} %reduce_sum.103), kind=kOutput, calls=%fused_computation.7 | convolution fusion | flops 6457131008 | bytes 4210688 | tf_op jit(solution)/shard_map/dot_general | solution.py:176
  16.3 0.1 slice.93
  16.4 0.1 slice.92
  16.5 0.8 copy.33
  17.3 1.8 %fusion.9 = bf16[128,40,256]{2,1,0:T(8,128)(2,1)} fusion(bf16[128,2,32]{2,1,0:T(2,128)(2,1)S(1)} %bitcast.31, bf16[128,32,256]{2,1,0:T(8,128)(2,1)S(1)} %bitcast.27), kind=kLoop, calls=%fused_computation.12 | loop fusion | flops 7864320 | bytes 4734976 | tf_op jit(solution)/shard_map/concatenate | solution.py:181
  19.1 10.4 %all-to-all-start = ((bf16[128,40,256]{2,1,0:T(8,128)(2,1)}), bf16[128,40,256]{2,1,0:T(8,128)(2,1)S(1)}, u32[]{:S(2)}, u32[]{:S(2)}) async-start(bf16[128,40,256]{2,1,0:T(8,128)(2,1)} %fusion.9), calls=%async_computation | async-start | bytes 5242880 | tf_op jit(solution)/shard_map/all_to_all | solution.py:182
  29.6 0.1 pad_add_fusion
  29.7 0.1 convert_reduce_fusion.8
  29.8 35.1 %all-to-all-done = bf16[128,40,256]{2,1,0:T(8,128)(2,1)S(1)} async-done(((bf16[128,40,256]{2,1,0:T(8,128)(2,1)}), bf16[128,40,256]{2,1,0:T(8,128)(2,1)S(1)}, u32[]{:S(2)}, u32[]{:S(2)}) %all-to-all-start) | async-done | bytes 2621472 | tf_op jit(solution)/shard_map/all_to_all | solution.py:182
  64.9 2.8 %copy.34 = bf16[256,5120]{1,0:T(8,128)(2,1)} copy(bf16[256,5120]{0,1:T(8,128)(2,1)S(1)} %bitcast.26) | data formatting | bytes 5242880 | tf_op jit(solution)/shard_map/dot_general | solution.py:205
  67.7 0.2 compare_select_fusion
  67.9 0.1 eq.130
  68.0 6.1 %fusion.2 = f32[2,128,1024]{2,1,0:T(8,128)S(1)} fusion(bf16[2,128,5120]{2,1,0:T(8,128)(2,1)} %bitcast.29, s32[5120]{0:T(1024)S(1)} %eq.130), kind=kOutput, calls=%fused_computation.4 | convolution fusion | flops 2689597440 | bytes 3690496 | tf_op jit(solution)/shard_map/dot_general | solution.py:205
  74.1 0.9 fusion.46
  75.0 0.1 fusion.63
  75.1 3.3 %collective-permute-start.1 = (f32[2,128,4]{2,1,0:T(8,128)S(1)}, f32[2,128,4]{2,1,0:T(8,128)S(1)}, u32[]{:S(2)}, u32[]{:S(2)}) collective-permute-start(f32[2,128,4]{2,1,0:T(8,128)S(1)} %get-tuple-element.20), channel_id=1, source_target_pairs={{1,0},{2,1},{3,2},{4,3},{5,4},{6,5},{7,6},{8,7},{9,8},{10,9},{11,1... | collective-permute-start | bytes 12296 | tf_op jit(solution)/shard_map/ppermute | solution.py:201
  78.5 2.5 %collective-permute-start = (f32[2,128,4]{2,1,0:T(8,128)S(1)}, f32[2,128,4]{2,1,0:T(8,128)S(1)}, u32[]{:S(2)}, u32[]{:S(2)}) collective-permute-start(f32[2,128,4]{2,1,0:T(8,128)S(1)} %get-tuple-element.19), channel_id=1, source_target_pairs={{0,1},{1,2},{2,3},{3,4},{4,5},{5,6},{6,7},{7,8},{8,9},{9,10},{10,1... | collective-permute-start | bytes 12296 | tf_op jit(solution)/shard_map/ppermute | solution.py:200
  81.0 0.3 fusion.17
  81.3 1.5 %collective-permute-done.1 = f32[2,128,4]{2,1,0:T(8,128)S(1)} collective-permute-done((f32[2,128,4]{2,1,0:T(8,128)S(1)}, f32[2,128,4]{2,1,0:T(8,128)S(1)}, u32[]{:S(2)}, u32[]{:S(2)}) %collective-permute-start.1) | collective-permute-done | bytes 4128 | tf_op jit(solution)/shard_map/ppermute | solution.py:201
  82.8 6.1 %collective-permute-done = f32[2,128,4]{2,1,0:T(8,128)S(1)} collective-permute-done((f32[2,128,4]{2,1,0:T(8,128)S(1)}, f32[2,128,4]{2,1,0:T(8,128)S(1)}, u32[]{:S(2)}, u32[]{:S(2)}) %collective-permute-start) | collective-permute-done | bytes 4128 | tf_op jit(solution)/shard_map/ppermute | solution.py:200
  89.0 3.9 %fusion.21.t_ref = f32[2,128,1024]{2,1,0:T(8,128)} fusion(f32[2,128,1024]{2,1,0:T(8,128)S(1)} %fusion.17, f32[2,128,4]{2,1,0:T(8,128)S(1)} %collective-permute-done.1, f32[2,128,4]{2,1,0:T(8,128)S(1)} %collective-permute-done, f32[1024]{0:T(1024)S(1)} %get-tuple-element.17, f32[1024]{0:T(1024)S(1)} %get-tuple-element.18, f32[1024]{0:T(1024)S(1)} %get-tuple-element.11, ...), kind=kLoop, calls=%fused_computation.37 | loop fusion | flops 7077888 | bytes 2142208 | tf_op jit(solution)/shard_map/add | solution.py:214
  92.8 12.0 %shard_map.77 = (f32[2,6,1024]{2,1,0:T(8,128)}, f32[2,1024]{1,0:T(2,128)}) custom-call(f32[2,128,1024]{2,1,0:T(8,128)} %fusion.21.t_ref, f32[128,8]{1,0:T(8,128)} %constant.77.clone.phit_ref, f32[32,128]{1,0:T(8,128)} %constant.78.clone.psi_ref), custom_call_target="tpu_custom_call" | custom-call | tf_op jit(solution)/shard_map/pallas_call | solution.py:140
  104.8 1.5 %copy.38 = f32[2,6,1024]{2,0,1:T(2,128)} copy(f32[2,6,1024]{2,1,0:T(8,128)} %get-tuple-element.8) | data formatting | bytes 98304 | tf_op jit(solution)/shard_map/pallas_call | solution.py:140
  (20 shorter events, 0.2 us)
Async XLA Ops:
  1.4 0.9 copy-start.2
  1.8 1.1 %copy-start.4 = (s32[2048]{0:T(1024)S(1)}, s32[2048]{0:T(1024)}, u32[]{:S(2)}) copy-start(s32[2048]{0:T(1024)} %param.8) | copy-start | bytes 24580
  1.9 2.2 %copy-start = (bf16[2048,3,256]{2,0,1:T(8,128)(2,1)S(1)}, bf16[2048,3,256]{2,0,1:T(8,128)(2,1)}, u32[]{:S(2)}) copy-start(bf16[2048,3,256]{2,0,1:T(8,128)(2,1)} %param.6) | copy-start | bytes 9437188
  19.1 10.6 %copy-start.3 = (s32[4,1024]{1,0:T(4,128)S(1)}, s32[4,1024]{1,0:T(4,128)}, u32[]{:S(2)}) copy-start(s32[4,1024]{1,0:T(4,128)} %param.9) | copy-start | bytes 49156
  19.1 45.8 %all-to-all-start = ((bf16[128,40,256]{2,1,0:T(8,128)(2,1)}), bf16[128,40,256]{2,1,0:T(8,128)(2,1)S(1)}, u32[]{:S(2)}, u32[]{:S(2)}) async-start(bf16[128,40,256]{2,1,0:T(8,128)(2,1)} %fusion.9), calls=%async_computation | async-start | bytes 5242880 | tf_op jit(solution)/shard_map/all_to_all | solution.py:182
  68.0 6.1 %copy-start.1 = (bf16[256,5120]{1,0:T(8,128)(2,1)S(1)}, bf16[256,5120]{1,0:T(8,128)(2,1)}, u32[]{:S(2)}) copy-start(bf16[256,5120]{1,0:T(8,128)(2,1)} %copy.34) | copy-start | bytes 7864324
  75.1 7.7 %collective-permute-start.1 = (f32[2,128,4]{2,1,0:T(8,128)S(1)}, f32[2,128,4]{2,1,0:T(8,128)S(1)}, u32[]{:S(2)}, u32[]{:S(2)}) collective-permute-start(f32[2,128,4]{2,1,0:T(8,128)S(1)} %get-tuple-element.20), channel_id=1, source_target_pairs={{1,0},{2,1},{3,2},{4,3},{5,4},{6,5},{7,6},{8,7},{9,8},{10,9},{11,1... | collective-permute-start | bytes 12296 | tf_op jit(solution)/shard_map/ppermute | solution.py:201
  78.5 10.5 %collective-permute-start = (f32[2,128,4]{2,1,0:T(8,128)S(1)}, f32[2,128,4]{2,1,0:T(8,128)S(1)}, u32[]{:S(2)}, u32[]{:S(2)}) collective-permute-start(f32[2,128,4]{2,1,0:T(8,128)S(1)} %get-tuple-element.19), channel_id=1, source_target_pairs={{0,1},{1,2},{2,3},{3,4},{4,5},{5,6},{6,7},{7,8},{8,9},{9,10},{10,1... | collective-permute-start | bytes 12296 | tf_op jit(solution)/shard_map/ppermute | solution.py:200

commit v5 on v4

--- a/solution.py
+++ b/solution.py
@@ -186,26 +186,29 @@
     low = got[:, capacity + 1, :capacity].astype(jnp.int32)
     recv_cells = jnp.where(high > 0, (high - 1) * CODE + low, -1)
     recv_cells = jnp.pad(recv_cells, ((0, 0), (0, EXTRA)), constant_values=-1).reshape(devices * lanes)
+    tile = 128
     edges = jnp.concatenate(
-        [jnp.arange(W, dtype=jnp.int32), jnp.arange(cells - W, cells, dtype=jnp.int32)]
+        [jnp.arange(tile, dtype=jnp.int32), jnp.arange(cells - tile, cells, dtype=jnp.int32)]
     )
     edge_select = (recv_cells[:, None] == edges[None, :]).astype(jnp.bfloat16)
     edge_sum = lax.dot_general(
         recv_rows, edge_select, (((0,), (0,)), ((), ())), preferred_element_type=jnp.float32
-    )
-    edge_lev = smooth_levels(edge_sum.reshape(SPEC, width // SPEC, 2 * W))
+    ).reshape(SPEC, width // SPEC, 2 * tile)
+    edge_lev = smooth_levels(edge_sum)
     count = devices
     forward = [(i, i + 1) for i in range(count - 1)]
     backward = [(target, source) for source, target in forward]
-    below = lax.ppermute(edge_lev[:, :, W:], ("cell", "own"), forward)
+    below = lax.ppermute(edge_lev[:, :, 2 * tile - W :], ("cell", "own"), forward)
     above = lax.ppermute(edge_lev[:, :, :W], ("cell", "own"), backward)
-    select = (recv_cells[:, None] == jnp.arange(cells, dtype=jnp.int32)[None, :]).astype(
-        jnp.bfloat16
-    )
+    middle = jnp.arange(tile, cells - tile, dtype=jnp.int32)
+    select = (recv_cells[:, None] == middle[None, :]).astype(jnp.bfloat16)
     summed = lax.dot_general(
         recv_rows, select, (((0,), (0,)), ((), ())), preferred_element_type=jnp.float32
     )
-    cellhist = summed.reshape(SPEC, width // SPEC, cells)
+    cellhist = jnp.concatenate(
+        [edge_sum[:, :, :tile], summed.reshape(SPEC, width // SPEC, cells - 2 * tile), edge_sum[:, :, tile:]],
+        axis=2,
+    )
     levelled = smooth_levels(cellhist)
     rimmed = jnp.concatenate([below, levelled, above], axis=2)
     target = 1.0 + levelled

time: 107 us -> 107 us (level)
    dot_general x1, matrix products: 0.87 us -> 4.7 us  [body_inner(): lax.dot_general(recv_rows, edge_select, (((0,), (0,)), ((), ())), preferr...]
    dot_general x1, matrix products: 6.05 us -> 2.68 us  [body_inner(): lax.dot_general(recv_rows, select, (((0,), (0,)), ((), ())), preferred_el...]
where the time goes in v5:
time: 107 us
  waiting for transfers between devices  42.7 us (40%)
  matrix products  17.8 us (17%)
  starting transfers between devices  16.3 us (15%)
  Pallas kernels  12 us (11%)
  other arithmetic  9.31 us (9%)
  local copies, waits for them, and re-layouts  7.83 us (7%)
    all_to_all x1, waiting for transfers between devices, body_inner(): lax.all_to_all(message, ('cell', 'own'), split_axis=0, concat_axis=0, til...  35.2 us
    pallas_call x1, Pallas kernels, fit_all(): pl.pallas_call(fit_kernel, out_shape=(jax.ShapeDtypeStruct((spec, count,...  12 us
    all_to_all x1, starting transfers between devices, body_inner(): lax.all_to_all(message, ('cell', 'own'), split_axis=0, concat_axis=0, til...  10.4 us
    dot_general x1, matrix products, body_inner(): sent = jnp.dot(place, payload, preferred_element_type=jnp.float32)  10.4 us
    ppermute x1, waiting for transfers between devices, body_inner(): lax.ppermute(edge_lev[:, :, 2 * tile - W:], ('cell', 'own'), forward)  6.15 us
    dot_general x1, matrix products, body_inner(): lax.dot_general(recv_rows, edge_select, (((0,), (0,)), ((), ())), preferr...  4.7 us
    add x1, other arithmetic, body_inner(): target + weight[None, None, :] * lax.slice_in_dim(rimmed, W + shift, W +...  3.87 us
    ppermute x1, starting transfers between devices, body_inner(): above = lax.ppermute(edge_lev[:, :, :W], ('cell', 'own'), backward)  3.3 us
  transfers between devices with their start and end apart: 3, of which 3 were waited for; matrix products, arithmetic and copies ran while one was open for 0% of the time, Pallas kernels for 0%

profile of v5, /device:TPU:8, one launch (start us, length us, event | category | flops | bytes accessed | tf_op | source)
XLA Modules:
  0.0 106.8 jit_solution(12771070913928155618)
XLA Ops:
  0.6 0.8 copy.18
  1.4 0.3 fusion.48
  1.8 0.1 add_add_fusion
  1.9 0.0 copy-start
  1.9 0.3 copy.19
  2.3 0.6 fusion.47
  3.0 1.1 %copy.24 = bf16[2048,2]{1,0:T(8,128)(2,1)} copy(bf16[2048,2]{0,1:T(2,128)(2,1)S(1)} %pad_maximum_fusion.3) | data formatting | bytes 16384
  4.1 1.7 %reduce_sum.103 = bf16[2048,256]{1,0:T(8,128)(2,1)} reduce(bf16[2048,3,256]{2,0,1:T(8,128)(2,1)S(1)} %copy-done, bf16[]{:T(256)} %constant.30.clone.1), dimensions={1}, to_apply=%region_3.4 | reduce | flops 1048576 | bytes 4194306 | tf_op jit(solution)/shard_map/reduce_sum | solution.py:165
  5.9 10.4 %fusion.7 = bf16[4096,384]{1,0:T(8,128)(2,1)S(1)} fusion(s32[2048]{0:T(1024)S(1)} %multiply_add_fusion, bf16[2048,2]{1,0:T(8,128)(2,1)} %copy.24, bf16[2048,256]{1,0:T(8,128)(2,1)} %reduce_sum.103), kind=kOutput, calls=%fused_computation.8 | convolution fusion | flops 6457131008 | bytes 4210688 | tf_op jit(solution)/shard_map/dot_general | solution.py:176
  16.3 0.1 slice.101
  16.4 0.1 slice.100
  16.5 0.8 copy.21
  17.3 1.8 %fusion.13 = bf16[128,40,256]{2,1,0:T(8,128)(2,1)} fusion(bf16[128,2,32]{2,1,0:T(2,128)(2,1)S(1)} %bitcast.31, bf16[128,32,256]{2,1,0:T(8,128)(2,1)S(1)} %bitcast.27), kind=kLoop, calls=%fused_computation.16 | loop fusion | flops 7864320 | bytes 4734976 | tf_op jit(solution)/shard_map/concatenate | solution.py:181
  19.1 10.4 %all-to-all-start = ((bf16[128,40,256]{2,1,0:T(8,128)(2,1)}), bf16[128,40,256]{2,1,0:T(8,128)(2,1)S(1)}, u32[]{:S(2)}, u32[]{:S(2)}) async-start(bf16[128,40,256]{2,1,0:T(8,128)(2,1)} %fusion.13), calls=%async_computation | async-start | bytes 5242880 | tf_op jit(solution)/shard_map/all_to_all | solution.py:182
  29.6 0.1 convert_reduce_fusion.8
  29.7 35.2 %all-to-all-done = bf16[128,40,256]{2,1,0:T(8,128)(2,1)S(1)} async-done(((bf16[128,40,256]{2,1,0:T(8,128)(2,1)}), bf16[128,40,256]{2,1,0:T(8,128)(2,1)S(1)}, u32[]{:S(2)}, u32[]{:S(2)}) %all-to-all-start) | async-done | bytes 2621472 | tf_op jit(solution)/shard_map/all_to_all | solution.py:182
  64.9 2.8 %copy.22 = bf16[256,5120]{1,0:T(8,128)(2,1)} copy(bf16[256,5120]{0,1:T(8,128)(2,1)S(1)} %bitcast.26) | data formatting | bytes 5242880 | tf_op jit(solution)/shard_map/dot_general | solution.py:194
  67.7 0.2 compare_select_fusion
  67.9 0.1 eq.130
  68.0 4.7 %fusion.9 = f32[2,128,256]{2,1,0:T(8,128)S(1)} fusion(bf16[2,128,5120]{2,1,0:T(8,128)(2,1)} %bitcast.29, s32[256]{0:T(256)S(1)} %pad_add_fusion, s32[5120]{0:T(1024)S(1)} %eq.130), kind=kOutput, calls=%fused_computation.11 | convolution fusion | flops 672399360 | bytes 2905088 | tf_op jit(solution)/shard_map/dot_general | solution.py:194
  72.8 0.1 fusion.54
  72.9 2.7 %fusion.2 = f32[2,128,768]{2,1,0:T(8,128)S(1)} fusion(bf16[2,128,5120]{2,1,0:T(8,128)(2,1)S(1)} %bitcast.30, s32[768]{0:T(1024)S(1)} %iota_add_fusion, s32[5120]{0:T(1024)S(1)} %eq.130), kind=kOutput, calls=%fused_computation.3 | convolution fusion | flops 2017198080 | bytes 3431424 | tf_op jit(solution)/shard_map/dot_general | solution.py:205
  75.6 0.1 fusion.64
  75.7 3.3 %collective-permute-start.1 = (f32[2,128,4]{2,1,0:T(8,128)S(1)}, f32[2,128,4]{2,1,0:T(8,128)S(1)}, u32[]{:S(2)}, u32[]{:S(2)}) collective-permute-start(f32[2,128,4]{2,1,0:T(8,128)S(1)} %get-tuple-element.18), channel_id=1, source_target_pairs={{1,0},{2,1},{3,2},{4,3},{5,4},{6,5},{7,6},{8,7},{9,8},{10,9},{11,1... | collective-permute-start | bytes 12296 | tf_op jit(solution)/shard_map/ppermute | solution.py:202
  79.0 2.5 %collective-permute-start = (f32[2,128,4]{2,1,0:T(8,128)S(1)}, f32[2,128,4]{2,1,0:T(8,128)S(1)}, u32[]{:S(2)}, u32[]{:S(2)}) collective-permute-start(f32[2,128,4]{2,1,0:T(8,128)S(1)} %get-tuple-element.17), channel_id=1, source_target_pairs={{0,1},{1,2},{2,3},{3,4},{4,5},{5,6},{6,7},{7,8},{8,9},{9,10},{10,1... | collective-permute-start | bytes 12296 | tf_op jit(solution)/shard_map/ppermute | solution.py:201
  81.5 0.1 pad_maximum_fusion.2
  81.6 0.3 fusion.23
  81.9 1.4 %collective-permute-done.1 = f32[2,128,4]{2,1,0:T(8,128)S(1)} collective-permute-done((f32[2,128,4]{2,1,0:T(8,128)S(1)}, f32[2,128,4]{2,1,0:T(8,128)S(1)}, u32[]{:S(2)}, u32[]{:S(2)}) %collective-permute-start.1) | collective-permute-done | bytes 4128 | tf_op jit(solution)/shard_map/ppermute | solution.py:202
  83.3 6.1 %collective-permute-done = f32[2,128,4]{2,1,0:T(8,128)S(1)} collective-permute-done((f32[2,128,4]{2,1,0:T(8,128)S(1)}, f32[2,128,4]{2,1,0:T(8,128)S(1)}, u32[]{:S(2)}, u32[]{:S(2)}) %collective-permute-start) | collective-permute-done | bytes 4128 | tf_op jit(solution)/shard_map/ppermute | solution.py:201
  89.5 3.9 %fusion.27.t_ref = f32[2,128,1024]{2,1,0:T(8,128)} fusion(f32[2,128,1024]{2,1,0:T(8,128)S(1)} %fusion.23, f32[2,128,4]{2,1,0:T(8,128)S(1)} %collective-permute-done.1, f32[2,128,4]{2,1,0:T(8,128)S(1)} %collective-permute-done, f32[1024]{0:T(1024)S(1)} %get-tuple-element.15, f32[1024]{0:T(1024)S(1)} %get-tuple-element.16, f32[1024]{0:T(1024)S(1)} %get-tuple-element.9, ...), kind=kLoop, calls=%fused_computation.43 | loop fusion | flops 7077888 | bytes 2142208 | tf_op jit(solution)/shard_map/add | solution.py:217
  93.3 12.0 %shard_map.77 = (f32[2,6,1024]{2,1,0:T(8,128)}, f32[2,1024]{1,0:T(2,128)}) custom-call(f32[2,128,1024]{2,1,0:T(8,128)} %fusion.27.t_ref, f32[128,8]{1,0:T(8,128)} %constant.79.clone.phit_ref, f32[32,128]{1,0:T(8,128)} %constant.80.clone.psi_ref), custom_call_target="tpu_custom_call" | custom-call | tf_op jit(solution)/shard_map/pallas_call | solution.py:140
  105.3 1.5 %copy.23 = f32[2,6,1024]{2,0,1:T(2,128)} copy(f32[2,6,1024]{2,1,0:T(8,128)} %get-tuple-element.6) | data formatting | bytes 98304 | tf_op jit(solution)/shard_map/pallas_call | solution.py:140
  (23 shorter events, 0.2 us)
Async XLA Ops:
  1.4 0.9 copy-start.2
  1.8 1.1 %copy-start.4 = (s32[2048]{0:T(1024)S(1)}, s32[2048]{0:T(1024)}, u32[]{:S(2)}) copy-start(s32[2048]{0:T(1024)} %param.8) | copy-start | bytes 24580
  1.9 2.2 %copy-start = (bf16[2048,3,256]{2,0,1:T(8,128)(2,1)S(1)}, bf16[2048,3,256]{2,0,1:T(8,128)(2,1)}, u32[]{:S(2)}) copy-start(bf16[2048,3,256]{2,0,1:T(8,128)(2,1)} %param.6) | copy-start | bytes 9437188
  19.1 10.5 %copy-start.3 = (s32[4,1024]{1,0:T(4,128)S(1)}, s32[4,1024]{1,0:T(4,128)}, u32[]{:S(2)}) copy-start(s32[4,1024]{1,0:T(4,128)} %param.9) | copy-start | bytes 49156
  19.1 45.8 %all-to-all-start = ((bf16[128,40,256]{2,1,0:T(8,128)(2,1)}), bf16[128,40,256]{2,1,0:T(8,128)(2,1)S(1)}, u32[]{:S(2)}, u32[]{:S(2)}) async-start(bf16[128,40,256]{2,1,0:T(8,128)(2,1)} %fusion.13), calls=%async_computation | async-start | bytes 5242880 | tf_op jit(solution)/shard_map/all_to_all | solution.py:182
  68.0 4.8 %copy-start.1 = (bf16[256,5120]{1,0:T(8,128)(2,1)S(1)}, bf16[256,5120]{1,0:T(8,128)(2,1)}, u32[]{:S(2)}) copy-start(bf16[256,5120]{1,0:T(8,128)(2,1)} %copy.22) | copy-start | bytes 7864324
  75.7 7.7 %collective-permute-start.1 = (f32[2,128,4]{2,1,0:T(8,128)S(1)}, f32[2,128,4]{2,1,0:T(8,128)S(1)}, u32[]{:S(2)}, u32[]{:S(2)}) collective-permute-start(f32[2,128,4]{2,1,0:T(8,128)S(1)} %get-tuple-element.18), channel_id=1, source_target_pairs={{1,0},{2,1},{3,2},{4,3},{5,4},{6,5},{7,6},{8,7},{9,8},{10,9},{11,1... | collective-permute-start | bytes 12296 | tf_op jit(solution)/shard_map/ppermute | solution.py:202
  79.0 10.5 %collective-permute-start = (f32[2,128,4]{2,1,0:T(8,128)S(1)}, f32[2,128,4]{2,1,0:T(8,128)S(1)}, u32[]{:S(2)}, u32[]{:S(2)}) collective-permute-start(f32[2,128,4]{2,1,0:T(8,128)S(1)} %get-tuple-element.17), channel_id=1, source_target_pairs={{0,1},{1,2},{2,3},{3,4},{4,5},{5,6},{6,7},{7,8},{8,9},{9,10},{10,1... | collective-permute-start | bytes 12296 | tf_op jit(solution)/shard_map/ppermute | solution.py:201

commit v6 on v4

--- a/solution.py
+++ b/solution.py
@@ -169,14 +169,19 @@
     )
     ranks = jnp.sum((jnp.cumsum(member, axis=0) - 1) * member, axis=1)
     position = target_block * capacity + ranks
-    codes = jnp.stack([cell_in // CODE + 1, cell_in % CODE], axis=1).astype(jnp.bfloat16)
-    codes = jnp.pad(codes, ((0, 0), (0, 128 - 2)))
-    payload = jnp.concatenate([packed, codes], axis=1)
     place = (jnp.arange(slots, dtype=jnp.int32)[:, None] == position[None, :]).astype(jnp.bfloat16)
-    sent = jnp.dot(place, payload, preferred_element_type=jnp.float32)
-    send_rows = sent[:, :width].astype(jnp.bfloat16).reshape(devices, capacity, width)
-    code_rows = sent[:, width : width + 2].reshape(devices, capacity, 2)
-    code_rows = jnp.swapaxes(code_rows, 1, 2).astype(jnp.bfloat16)
+    send_rows = jnp.dot(place, packed, preferred_element_type=jnp.float32)
+    send_rows = send_rows.astype(jnp.bfloat16).reshape(devices, capacity, width)
+    in_rank = (ranks[:, None] == jnp.arange(capacity, dtype=jnp.int32)[None, :]).astype(jnp.bfloat16)
+    high_code = (cell_in // CODE + 1).astype(jnp.bfloat16)[:, None] * in_rank
+    low_code = (cell_in % CODE).astype(jnp.bfloat16)[:, None] * in_rank
+    code_rows = lax.dot_general(
+        member.astype(jnp.bfloat16),
+        jnp.concatenate([high_code, low_code], axis=1),
+        (((0,), (0,)), ((), ())),
+        preferred_element_type=jnp.float32,
+    )
+    code_rows = code_rows.astype(jnp.bfloat16).reshape(devices, 2, capacity)
     code_rows = jnp.pad(code_rows, ((0, 0), (0, EXTRA - 2), (0, width - capacity)))
     message = jnp.concatenate([send_rows, code_rows], axis=1)
     got = lax.all_to_all(message, ("cell", "own"), split_axis=0, concat_axis=0, tiled=True)

time: 107 us -> 109 us (1.019)
  waiting for transfers between devices: 42.8 us -> 37 us
  other arithmetic: 9.22 us -> 14 us
  starting transfers between devices: 16.3 us -> 20.6 us
  matrix products: 17.4 us -> 15.5 us
    ppermute x1, waiting for transfers between devices: 6.14 us -> 0.43 us  [body_inner(): below = lax.ppermute(edge_lev[:, :, W:], ('cell', 'own'), forward)]
    ppermute x1, starting transfers between devices: 3.29 us -> 7.3 us  [body_inner(): above = lax.ppermute(edge_lev[:, :, :W], ('cell', 'own'), backward)]
    dot_general x1 -> x2, matrix products: 10.4 us -> 8.53 us  [the longest x1 7.66 us: body_inner(): send_rows = jnp.dot(place, packed, preferred_element_type=jnp.float32)]
    mul x0 -> x1, other arithmetic: none -> 1.62 us  [body_inner(): high_code = (cell_in // CODE + 1).astype(jnp.bfloat16)[:, None] * in_rank]
    dot_general x1, local copies, waits for them, and re-layouts: 2.83 us -> 4.42 us  [body_inner(): lax.dot_general(recv_rows, select, (((0,), (0,)), ((), ())), preferred_el...]
    sub x1, other arithmetic: 0.07 us -> 1.3 us  [body_inner(): ranks = jnp.sum((jnp.cumsum(member, axis=0) - 1) * member, axis=1)]
where the time goes in v6:
time: 109 us; the launch traced here: 108 us
  waiting for transfers between devices  37 us (34%)
  starting transfers between devices  20.6 us (19%)
  matrix products  15.5 us (14%)
  other arithmetic  14 us (13%)
  Pallas kernels  12 us (11%)
  local copies, waits for them, and re-layouts  8.46 us (8%)
    all_to_all x1, waiting for transfers between devices, body_inner(): lax.all_to_all(message, ('cell', 'own'), split_axis=0, concat_axis=0, til...  34.8 us
    pallas_call x1, Pallas kernels, fit_all(): pl.pallas_call(fit_kernel, out_shape=(jax.ShapeDtypeStruct((spec, count,...  12 us
    all_to_all x1, starting transfers between devices, body_inner(): lax.all_to_all(message, ('cell', 'own'), split_axis=0, concat_axis=0, til...  10.8 us
    dot_general x1, matrix products, body_inner(): send_rows = jnp.dot(place, packed, preferred_element_type=jnp.float32)  7.66 us
    ppermute x1, starting transfers between devices, body_inner(): above = lax.ppermute(edge_lev[:, :, :W], ('cell', 'own'), backward)  7.3 us
    dot_general x1, matrix products, body_inner(): lax.dot_general(recv_rows, select, (((0,), (0,)), ((), ())), preferred_el...  6.04 us
    dot_general x1, local copies, waits for them, and re-layouts, body_inner(): lax.dot_general(recv_rows, select, (((0,), (0,)), ((), ())), preferred_el...  4.42 us
    add x1, other arithmetic, body_inner(): target + weight[None, None, :] * lax.slice_in_dim(rimmed, W + shift, W +...  3.87 us
  transfers between devices with their start and end apart: 3, of which 3 were waited for; matrix products, arithmetic and copies ran while one was open for 0% of the time, Pallas kernels for 0%

profile of v6, /device:TPU:8, one launch (start us, length us, event | category | flops | bytes accessed | tf_op | source)
XLA Modules:
  0.0 108.4 jit_solution(10536648179610295824)
XLA Ops:
  0.6 0.0 copy-start
  0.6 0.9 fusion.55
  1.5 0.9 copy.28
  2.4 0.3 fusion.38
  2.8 1.0 copy-done.1
  3.8 1.3 %add_add_fusion = s32[128,16,128]{0,1,2:T(8,128)S(1)} fusion(s32[128,16,128]{0,1,2:T(8,128)} %copy-done.1, s32[128,16]{0,1:T(8,128)S(1)} %slice.81), kind=kLoop, calls=%fused_computation.60 | loop fusion | flops 524288 | bytes 2105344 | tf_op jit(solution)/shard_map/sub | solution.py:170
  5.1 0.3 copy.29
  5.4 0.6 fusion.35
  6.1 1.6 %fusion.37 = (bf16[2048,32]{1,0:T(8,128)(2,1)S(1)}, bf16[2048,32]{1,0:T(8,128)(2,1)S(1)}) fusion(s32[2048]{0:T(1024)S(1)} %fusion.35, bf16[2048]{0:T(1024)(128)(2,1)S(1)} %get-tuple-element.23, bf16[2048]{0:T(1024)(128)(2,1)S(1)} %get-tuple-element.24), kind=kLoop, calls=%fused_computation.58 | loop fusion | flops 196608 | bytes 278528 | tf_op jit(solution)/shard_map/mul | solution.py:176
  7.7 0.9 convolution_convert_fusion
  8.6 0.1 copy.30
  8.7 1.7 %reduce_sum.103 = bf16[2048,256]{1,0:T(8,128)(2,1)} reduce(bf16[2048,3,256]{2,0,1:T(8,128)(2,1)S(1)} %copy-done, bf16[]{:T(256)} %constant.34.clone.1), dimensions={1}, to_apply=%region_3.4 | reduce | flops 1048576 | bytes 4194306 | tf_op jit(solution)/shard_map/reduce_sum | solution.py:165
  10.5 7.7 %fusion.7 = bf16[4096,256]{1,0:T(8,128)(2,1)S(1)} fusion(bf16[2048,256]{1,0:T(8,128)(2,1)} %reduce_sum.103, s32[2048]{0:T(1024)S(1)} %multiply_add_fusion), kind=kOutput, calls=%fused_computation.9 | convolution fusion | flops 4304404480 | bytes 3153920 | tf_op jit(solution)/shard_map/dot_general | solution.py:173
  18.1 1.8 %fusion.8 = bf16[128,40,256]{2,1,0:T(8,128)(2,1)} fusion(bf16[128,2,32]{2,1,0:T(2,128)(2,1)S(1)} %copy.30, bf16[128,32,256]{2,1,0:T(8,128)(2,1)S(1)} %bitcast.28), kind=kLoop, calls=%fused_computation.10 | loop fusion | flops 7864320 | bytes 4734976 | tf_op jit(solution)/shard_map/concatenate | solution.py:186
  20.0 10.8 %all-to-all-start = ((bf16[128,40,256]{2,1,0:T(8,128)(2,1)}), bf16[128,40,256]{2,1,0:T(8,128)(2,1)}, u32[]{:S(2)}, u32[]{:S(2)}) async-start(bf16[128,40,256]{2,1,0:T(8,128)(2,1)} %fusion.8), calls=%async_computation | async-start | bytes 5242880 | tf_op jit(solution)/shard_map/all_to_all | solution.py:187
  30.8 0.1 pad_add_fusion
  30.9 0.1 convert_reduce_fusion.8
  31.0 34.8 %all-to-all-done = bf16[128,40,256]{2,1,0:T(8,128)(2,1)} async-done(((bf16[128,40,256]{2,1,0:T(8,128)(2,1)}), bf16[128,40,256]{2,1,0:T(8,128)(2,1)}, u32[]{:S(2)}, u32[]{:S(2)}) %all-to-all-start) | async-done | bytes 2621472 | tf_op jit(solution)/shard_map/all_to_all | solution.py:187
  65.8 1.3 %compare_select_fusion = s32[128,1,32]{2,1,0:T(1,128)S(1)} fusion(bf16[128,40,256]{2,1,0:T(8,128)(2,1)} %all-to-all-done), kind=kLoop, calls=%fused_computation.70 | loop fusion | flops 28672 | bytes 32768 | tf_op jit(solution)/shard_map/jit(_where)/select_n | solution.py:192
  67.1 0.1 eq.146
  67.2 4.4 %copy.31 = bf16[256,5120]{1,0:T(8,128)(2,1)} copy(bf16[256,5120]{0,1:T(8,128)(2,1)} %bitcast.8) | data formatting | bytes 5242880 | tf_op jit(solution)/shard_map/dot_general | solution.py:210
  71.6 6.0 %fusion.2 = f32[2,128,1024]{2,1,0:T(8,128)S(1)} fusion(bf16[2,128,5120]{2,1,0:T(8,128)(2,1)} %bitcast.26, s32[5120]{0:T(1024)S(1)} %eq.146), kind=kOutput, calls=%fused_computation.4 | convolution fusion | flops 2689597440 | bytes 3690496 | tf_op jit(solution)/shard_map/dot_general | solution.py:210
  77.7 0.9 fusion.45
  78.6 0.1 fusion.60
  78.7 2.5 %collective-permute-start = (f32[2,128,4]{2,1,0:T(8,128)S(1)}, f32[2,128,4]{2,1,0:T(8,128)S(1)}, u32[]{:S(2)}, u32[]{:S(2)}) collective-permute-start(f32[2,128,4]{2,1,0:T(8,128)S(1)} %get-tuple-element.19), channel_id=1, source_target_pairs={{0,1},{1,2},{2,3},{3,4},{4,5},{5,6},{6,7},{7,8},{8,9},{9,10},{10,1... | collective-permute-start | bytes 12296 | tf_op jit(solution)/shard_map/ppermute | solution.py:205
  81.2 7.3 %collective-permute-start.1 = (f32[2,128,4]{2,1,0:T(8,128)S(1)}, f32[2,128,4]{2,1,0:T(8,128)S(1)}, u32[]{:S(2)}, u32[]{:S(2)}) collective-permute-start(f32[2,128,4]{2,1,0:T(8,128)S(1)} %get-tuple-element.20), channel_id=1, source_target_pairs={{1,0},{2,1},{3,2},{4,3},{5,4},{6,5},{7,6},{8,7},{9,8},{10,9},{11,1... | collective-permute-start | bytes 12296 | tf_op jit(solution)/shard_map/ppermute | solution.py:206
  88.5 0.3 fusion.11
  88.8 0.4 collective-permute-done
  89.2 1.8 %collective-permute-done.1 = f32[2,128,4]{2,1,0:T(8,128)S(1)} collective-permute-done((f32[2,128,4]{2,1,0:T(8,128)S(1)}, f32[2,128,4]{2,1,0:T(8,128)S(1)}, u32[]{:S(2)}, u32[]{:S(2)}) %collective-permute-start.1) | collective-permute-done | bytes 4128 | tf_op jit(solution)/shard_map/ppermute | solution.py:206
  91.0 3.9 %fusion.15.t_ref = f32[2,128,1024]{2,1,0:T(8,128)} fusion(f32[2,128,1024]{2,1,0:T(8,128)S(1)} %fusion.11, f32[2,128,4]{2,1,0:T(8,128)S(1)} %collective-permute-done.1, f32[2,128,4]{2,1,0:T(8,128)S(1)} %collective-permute-done, f32[1024]{0:T(1024)S(1)} %get-tuple-element.17, f32[1024]{0:T(1024)S(1)} %get-tuple-element.18, f32[1024]{0:T(1024)S(1)} %get-tuple-element.11, ...), kind=kLoop, calls=%fused_computation.32 | loop fusion | flops 7077888 | bytes 2142208 | tf_op jit(solution)/shard_map/add | solution.py:219
  94.9 12.0 %shard_map.77 = (f32[2,6,1024]{2,1,0:T(8,128)}, f32[2,1024]{1,0:T(2,128)}) custom-call(f32[2,128,1024]{2,1,0:T(8,128)} %fusion.15.t_ref, f32[128,8]{1,0:T(8,128)} %constant.79.clone.phit_ref, f32[32,128]{1,0:T(8,128)} %constant.80.clone.psi_ref), custom_call_target="tpu_custom_call" | custom-call | tf_op jit(solution)/shard_map/pallas_call | solution.py:140
  106.9 1.5 %copy.35 = f32[2,6,1024]{2,0,1:T(2,128)} copy(f32[2,6,1024]{2,1,0:T(8,128)} %get-tuple-element.8) | data formatting | bytes 98304 | tf_op jit(solution)/shard_map/pallas_call | solution.py:140
  (16 shorter events, 0.1 us)
Async XLA Ops:
  0.6 8.1 %copy-start = (bf16[2048,3,256]{2,0,1:T(8,128)(2,1)S(1)}, bf16[2048,3,256]{2,0,1:T(8,128)(2,1)}, u32[]{:S(2)}) copy-start(bf16[2048,3,256]{2,0,1:T(8,128)(2,1)} %param.6) | copy-start | bytes 9437188
  2.4 3.0 %copy-start.3 = (s32[2048,1]{0,1:T(1,128)S(1)}, s32[2048,1]{0,1:T(1,128)}, u32[]{:S(2)}) copy-start(s32[2048,1]{0,1:T(1,128)} %param.7) | copy-start | bytes 24580
  2.7 1.0 copy-start.1
  20.0 11.0 %copy-start.4 = (s32[4,1024]{1,0:T(4,128)S(1)}, s32[4,1024]{1,0:T(4,128)}, u32[]{:S(2)}) copy-start(s32[4,1024]{1,0:T(4,128)} %param.9) | copy-start | bytes 49156
  20.0 45.9 %all-to-all-start = ((bf16[128,40,256]{2,1,0:T(8,128)(2,1)}), bf16[128,40,256]{2,1,0:T(8,128)(2,1)}, u32[]{:S(2)}, u32[]{:S(2)}) async-start(bf16[128,40,256]{2,1,0:T(8,128)(2,1)} %fusion.8), calls=%async_computation | async-start | bytes 5242880 | tf_op jit(solution)/shard_map/all_to_all | solution.py:187
  71.6 6.1 %copy-start.2 = (bf16[256,5120]{1,0:T(8,128)(2,1)S(1)}, bf16[256,5120]{1,0:T(8,128)(2,1)}, u32[]{:S(2)}) copy-start(bf16[256,5120]{1,0:T(8,128)(2,1)} %copy.31) | copy-start | bytes 7864324
  78.7 10.5 %collective-permute-start = (f32[2,128,4]{2,1,0:T(8,128)S(1)}, f32[2,128,4]{2,1,0:T(8,128)S(1)}, u32[]{:S(2)}, u32[]{:S(2)}) collective-permute-start(f32[2,128,4]{2,1,0:T(8,128)S(1)} %get-tuple-element.19), channel_id=1, source_target_pairs={{0,1},{1,2},{2,3},{3,4},{4,5},{5,6},{6,7},{7,8},{8,9},{9,10},{10,1... | collective-permute-start | bytes 12296 | tf_op jit(solution)/shard_map/ppermute | solution.py:205
  81.2 9.8 %collective-permute-start.1 = (f32[2,128,4]{2,1,0:T(8,128)S(1)}, f32[2,128,4]{2,1,0:T(8,128)S(1)}, u32[]{:S(2)}, u32[]{:S(2)}) collective-permute-start(f32[2,128,4]{2,1,0:T(8,128)S(1)} %get-tuple-element.20), channel_id=1, source_target_pairs={{1,0},{2,1},{3,2},{4,3},{5,4},{6,5},{7,6},{8,7},{9,8},{10,9},{11,1... | collective-permute-start | bytes 12296 | tf_op jit(solution)/shard_map/ppermute | solution.py:206

commit v7 on v4

--- a/solution.py
+++ b/solution.py
@@ -179,6 +179,19 @@
     code_rows = jnp.swapaxes(code_rows, 1, 2).astype(jnp.bfloat16)
     code_rows = jnp.pad(code_rows, ((0, 0), (0, EXTRA - 2), (0, width - capacity)))
     message = jnp.concatenate([send_rows, code_rows], axis=1)
+    low_side = cell_in < W
+    high_side = cell_in >= cells - W
+    aimed = jnp.where(high_side, target_block + 1, target_block - 1)
+    aimed_ok = (low_side | high_side) & (aimed >= 0) & (aimed < devices)
+    spot = jnp.where(high_side, cell_in - (cells - W), W + cell_in)
+    halo_slot = jnp.where(aimed_ok, aimed * 2 * W + spot, -1)
+    halo_place = (
+        jnp.arange(devices * 2 * W, dtype=jnp.int32)[:, None] == halo_slot[None, :]
+    ).astype(jnp.bfloat16)
+    halo_part = jnp.dot(halo_place, packed, preferred_element_type=jnp.float32)
+    halo_sum = lax.psum_scatter(
+        halo_part.reshape(devices, 2 * W, width), ("cell", "own"), scatter_dimension=0, tiled=True
+    )
     got = lax.all_to_all(message, ("cell", "own"), split_axis=0, concat_axis=0, tiled=True)
     lanes = capacity + EXTRA
     recv_rows = got.reshape(devices * lanes, width)
@@ -186,19 +199,9 @@
     low = got[:, capacity + 1, :capacity].astype(jnp.int32)
     recv_cells = jnp.where(high > 0, (high - 1) * CODE + low, -1)
     recv_cells = jnp.pad(recv_cells, ((0, 0), (0, EXTRA)), constant_values=-1).reshape(devices * lanes)
-    edges = jnp.concatenate(
-        [jnp.arange(W, dtype=jnp.int32), jnp.arange(cells - W, cells, dtype=jnp.int32)]
-    )
-    edge_select = (recv_cells[:, None] == edges[None, :]).astype(jnp.bfloat16)
-    edge_sum = lax.dot_general(
-        recv_rows, edge_select, (((0,), (0,)), ((), ())), preferred_element_type=jnp.float32
-    )
-    edge_lev = smooth_levels(edge_sum.reshape(SPEC, width // SPEC, 2 * W))
-    count = devices
-    forward = [(i, i + 1) for i in range(count - 1)]
-    backward = [(target, source) for source, target in forward]
-    below = lax.ppermute(edge_lev[:, :, W:], ("cell", "own"), forward)
-    above = lax.ppermute(edge_lev[:, :, :W], ("cell", "own"), backward)
+    halo_lev = smooth_levels(halo_sum.reshape(2 * W, width).T.reshape(SPEC, width // SPEC, 2 * W))
+    below = halo_lev[:, :, :W]
+    above = halo_lev[:, :, W:]
     select = (recv_cells[:, None] == jnp.arange(cells, dtype=jnp.int32)[None, :]).astype(
         jnp.bfloat16
     )

time: 107 us -> 727 us (6.79)
  the two profiles are of different devices: /device:TPU:8 before, /device:TPU:0 now
where the time goes in v7:
time: 727 us; the launch traced here: 726 us
  waiting for transfers between devices  648 us (89%)
  matrix products  20.9 us (3%)
  between operations  14.3 us (2%)
  Pallas kernels  12 us (2%)
  starting transfers between devices  11.4 us (2%)
  other arithmetic  10.5 us (1%)
  local copies, waits for them, and re-layouts  8.6 us (1%)
    reduce_scatter x1, waiting for transfers between devices, body_inner(): lax.psum_scatter(halo_part.reshape(devices, 2 * W, width), ('cell', 'own'...  648 us
  transfers between devices with their start and end apart: 2, of which 1 were waited for; matrix products, arithmetic and copies ran while one was open for 1% of the time, Pallas kernels for 0%

profile of v7, /device:TPU:0, one launch (start us, length us, event | category | flops | bytes accessed | tf_op | source)
XLA Modules:
  0.0 726.1 jit_solution(7431258478001508117)
XLA Ops:
  7.2 0.8 copy.27
  8.0 0.3 fusion.45
  8.4 0.1 add_add_fusion
  8.5 0.0 copy-start
  8.5 0.3 copy.28
  8.8 0.6 fusion.43
  9.6 1.1 copy.37
  10.6 1.7 reduce_sum.103
  12.4 10.4 %fusion.8 = bf16[4096,384]{1,0:T(8,128)(2,1)S(1)} fusion(s32[2048]{0:T(1024)S(1)} %get-tuple-element.22, bf16[2048,2]{1,0:T(8,128)(2,1)} %copy.37, bf16[2048,256]{1,0:T(8,128)(2,1)} %reduce_sum.103), kind=kOutput, calls=%fused_computation.9 | convolution fusion | flops 6457131008 | bytes 4210688 | tf_op jit(solution)/shard_map/dot_general | solution.py:176
  22.8 0.1 slice.93
  22.9 0.1 slice.92
  23.0 0.8 copy.30
  23.8 1.8 fusion.11
  25.6 11.2 %all-to-all-start = ((bf16[128,40,256]{2,1,0:T(8,128)(2,1)}), bf16[128,40,256]{2,1,0:T(8,128)(2,1)S(1)}, u32[]{:S(2)}, u32[]{:S(2)}) async-start(bf16[128,40,256]{2,1,0:T(8,128)(2,1)} %fusion.11), calls=%async_computation | async-start | bytes 5242880 | tf_op jit(solution)/shard_map/all_to_all | solution.py:195
  36.8 0.2 reduce-scatter.2.cloned.1.call-start
  37.0 1.3 broadcast_compare_fusion
  38.4 0.0 copy-start.2
  38.4 4.6 fusion.6
  42.9 0.0 reduce-scatter.2.cloned.1.call-update
  43.0 0.1 convert_reduce_fusion.8
  43.1 648.5 %reduce-scatter.2.cloned.1.call-done = f32[1,8,256]{2,1,0:T(8,128)} async-done(((f32[128,8,256]{2,1,0:T(8,128)}), f32[1,8,256]{2,1,0:T(8,128)}) %reduce-scatter.2.cloned.1.call-update) | async-done | bytes 8208 | tf_op jit(solution)/shard_map/reduce_scatter | solution.py:192
  691.5 0.8 copy.33
  692.4 0.1 fusion.61
  692.5 0.0 all-to-all-done
  692.5 2.8 copy.31
  695.4 0.2 compare_select_fusion
  695.6 0.1 eq.137
  695.7 5.9 fusion.2
  701.6 0.3 fusion.19
  701.9 3.9 fusion.23.t_ref
  705.8 12.0 %shard_map.77 = (f32[2,6,1024]{2,1,0:T(8,128)}, f32[2,1024]{1,0:T(2,128)}) custom-call(f32[2,128,1024]{2,1,0:T(8,128)} %fusion.23.t_ref, f32[128,8]{1,0:T(8,128)} %constant.88.clone.phit_ref, f32[32,128]{1,0:T(8,128)} %constant.89.clone.psi_ref), custom_call_target="tpu_custom_call" | custom-call | tf_op jit(solution)/shard_map/pallas_call | solution.py:140
  717.8 1.5 copy.34
  (16 shorter events, 0.2 us)
Async XLA Ops:
  8.0 0.9 copy-start.1
  8.4 1.1 copy-start.3
  8.5 2.2 copy-start
  25.6 666.9 %all-to-all-start = ((bf16[128,40,256]{2,1,0:T(8,128)(2,1)}), bf16[128,40,256]{2,1,0:T(8,128)(2,1)S(1)}, u32[]{:S(2)}, u32[]{:S(2)}) async-start(bf16[128,40,256]{2,1,0:T(8,128)(2,1)} %fusion.11), calls=%async_computation | async-start | bytes 5242880 | tf_op jit(solution)/shard_map/all_to_all | solution.py:195
  36.8 654.8 %reduce-scatter.2.cloned.1.call-start = ((), (), s32[]{:S(2)}) async-start(), calls=%async_computation.2 | async-start | bytes 1056768 | tf_op jit(solution)/shard_map/reduce_scatter | solution.py:192
  38.4 4.6 copy-start.2
Sparse Core Ops, SparseCore 0:
  43.1 648.4 reduce-scatter.1

commit v8 on v4

--- a/solution.py
+++ b/solution.py
@@ -186,26 +186,25 @@
     low = got[:, capacity + 1, :capacity].astype(jnp.int32)
     recv_cells = jnp.where(high > 0, (high - 1) * CODE + low, -1)
     recv_cells = jnp.pad(recv_cells, ((0, 0), (0, EXTRA)), constant_values=-1).reshape(devices * lanes)
-    edges = jnp.concatenate(
-        [jnp.arange(W, dtype=jnp.int32), jnp.arange(cells - W, cells, dtype=jnp.int32)]
-    )
-    edge_select = (recv_cells[:, None] == edges[None, :]).astype(jnp.bfloat16)
-    edge_sum = lax.dot_general(
-        recv_rows, edge_select, (((0,), (0,)), ((), ())), preferred_element_type=jnp.float32
-    )
-    edge_lev = smooth_levels(edge_sum.reshape(SPEC, width // SPEC, 2 * W))
-    count = devices
-    forward = [(i, i + 1) for i in range(count - 1)]
+    tile = 128
+
+    def cell_sums(first, count):
+        picked = (
+            recv_cells[:, None] == first + jnp.arange(count, dtype=jnp.int32)[None, :]
+        ).astype(jnp.bfloat16)
+        summed = lax.dot_general(
+            recv_rows, picked, (((0,), (0,)), ((), ())), preferred_element_type=jnp.float32
+        )
+        return summed.reshape(SPEC, width // SPEC, count)
+
+    bottom = cell_sums(0, tile)
+    top = cell_sums(cells - tile, tile)
+    forward = [(i, i + 1) for i in range(devices - 1)]
     backward = [(target, source) for source, target in forward]
-    below = lax.ppermute(edge_lev[:, :, W:], ("cell", "own"), forward)
-    above = lax.ppermute(edge_lev[:, :, :W], ("cell", "own"), backward)
-    select = (recv_cells[:, None] == jnp.arange(cells, dtype=jnp.int32)[None, :]).astype(
-        jnp.bfloat16
-    )
-    summed = lax.dot_general(
-        recv_rows, select, (((0,), (0,)), ((), ())), preferred_element_type=jnp.float32
-    )
-    cellhist = summed.reshape(SPEC, width // SPEC, cells)
+    below = lax.ppermute(smooth_levels(top)[:, :, tile - W :], ("cell", "own"), forward)
+    above = lax.ppermute(smooth_levels(bottom)[:, :, :W], ("cell", "own"), backward)
+    middle = cell_sums(tile, cells - 2 * tile)
+    cellhist = jnp.concatenate([bottom, middle, top], axis=2)
     levelled = smooth_levels(cellhist)
     rimmed = jnp.concatenate([below, levelled, above], axis=2)
     target = 1.0 + levelled

time: 107 us -> 107 us (level)
    dot_general x2 -> x3, matrix products: 6.93 us -> 6.4 us  [cell_sums(): lax.dot_general(recv_rows, picked, (((0,), (0,)), ((), ())), preferred_el...]
  transfers between devices with their start and end apart: 3 -> 3, of which waited for: 3 -> 3; matrix products, arithmetic and copies ran while one was open for 0% -> 1% of each run, Pallas kernels for 0% -> 0%
where the time goes in v8:
time: 107 us; the launch traced here: 106 us
  waiting for transfers between devices  42.8 us (40%)
  matrix products  16.8 us (16%)
  starting transfers between devices  16.3 us (15%)
  Pallas kernels  12 us (11%)
  other arithmetic  9.43 us (9%)
  local copies, waits for them, and re-layouts  7.76 us (7%)
    all_to_all x1, waiting for transfers between devices, body_inner(): lax.all_to_all(message, ('cell', 'own'), split_axis=0, concat_axis=0, til...  35.2 us
    pallas_call x1, Pallas kernels, fit_all(): pl.pallas_call(fit_kernel, out_shape=(jax.ShapeDtypeStruct((spec, count,...  12 us
    all_to_all x1, starting transfers between devices, body_inner(): lax.all_to_all(message, ('cell', 'own'), split_axis=0, concat_axis=0, til...  10.4 us
    dot_general x1, matrix products, body_inner(): sent = jnp.dot(place, payload, preferred_element_type=jnp.float32)  10.4 us
    dot_general x3, matrix products, cell_sums(): lax.dot_general(recv_rows, picked, (((0,), (0,)), ((), ())), preferred_el...  6.4 us
    ppermute x1, waiting for transfers between devices, body_inner(): lax.ppermute(smooth_levels(top)[:, :, tile - W:], ('cell', 'own'), forward)  6.33 us
    add x1, other arithmetic, body_inner(): target + weight[None, None, :] * lax.slice_in_dim(rimmed, W + shift, W +...  3.87 us
    ppermute x1, starting transfers between devices, body_inner(): lax.ppermute(smooth_levels(bottom)[:, :, :W], ('cell', 'own'), backward)  3.3 us
  transfers between devices with their start and end apart: 3, of which 3 were waited for; matrix products, arithmetic and copies ran while one was open for 1% of the time, Pallas kernels for 0%

profile of v8, /device:TPU:8, one launch (start us, length us, event | category | flops | bytes accessed | tf_op | source)
XLA Modules:
  0.0 106.1 jit_solution(5658788416480195613)
XLA Ops:
  0.6 0.8 copy.30
  1.4 0.3 fusion.52
  1.8 0.1 add_add_fusion
  1.9 0.0 copy-start
  1.9 0.3 copy.31
  2.3 0.6 fusion.51
  3.0 1.1 %copy.44 = bf16[2048,2]{1,0:T(8,128)(2,1)} copy(bf16[2048,2]{0,1:T(2,128)(2,1)S(1)} %pad_maximum_fusion.3) | data formatting | bytes 16384
  4.1 1.7 %reduce_sum.103 = bf16[2048,256]{1,0:T(8,128)(2,1)} reduce(bf16[2048,3,256]{2,0,1:T(8,128)(2,1)S(1)} %copy-done, bf16[]{:T(256)} %constant.30.clone.1), dimensions={1}, to_apply=%region_3.4 | reduce | flops 1048576 | bytes 4194306 | tf_op jit(solution)/shard_map/reduce_sum | solution.py:165
  5.9 10.4 %fusion.7 = bf16[4096,384]{1,0:T(8,128)(2,1)S(1)} fusion(s32[2048]{0:T(1024)S(1)} %multiply_add_fusion, bf16[2048,2]{1,0:T(8,128)(2,1)} %copy.44, bf16[2048,256]{1,0:T(8,128)(2,1)} %reduce_sum.103), kind=kOutput, calls=%fused_computation.8 | convolution fusion | flops 6457131008 | bytes 4210688 | tf_op jit(solution)/shard_map/dot_general | solution.py:176
  16.3 0.1 slice.101
  16.4 0.1 slice.100
  16.5 0.8 copy.33
  17.3 1.8 %fusion.10 = bf16[128,40,256]{2,1,0:T(8,128)(2,1)} fusion(bf16[128,2,32]{2,1,0:T(2,128)(2,1)S(1)} %bitcast.36, bf16[128,32,256]{2,1,0:T(8,128)(2,1)S(1)} %bitcast.31), kind=kLoop, calls=%fused_computation.13 | loop fusion | flops 7864320 | bytes 4734976 | tf_op jit(solution)/shard_map/concatenate | solution.py:181
  19.1 10.4 %all-to-all-start = ((bf16[128,40,256]{2,1,0:T(8,128)(2,1)}), bf16[128,40,256]{2,1,0:T(8,128)(2,1)S(1)}, u32[]{:S(2)}, u32[]{:S(2)}) async-start(bf16[128,40,256]{2,1,0:T(8,128)(2,1)} %fusion.10), calls=%async_computation | async-start | bytes 5242880 | tf_op jit(solution)/shard_map/all_to_all | solution.py:182
  29.6 0.1 convert_reduce_fusion.8
  29.7 35.2 %all-to-all-done = bf16[128,40,256]{2,1,0:T(8,128)(2,1)S(1)} async-done(((bf16[128,40,256]{2,1,0:T(8,128)(2,1)}), bf16[128,40,256]{2,1,0:T(8,128)(2,1)S(1)}, u32[]{:S(2)}, u32[]{:S(2)}) %all-to-all-start) | async-done | bytes 2621472 | tf_op jit(solution)/shard_map/all_to_all | solution.py:182
  64.9 2.8 %copy.34 = bf16[256,5120]{1,0:T(8,128)(2,1)} copy(bf16[256,5120]{0,1:T(8,128)(2,1)S(1)} %bitcast.30) | data formatting | bytes 5242880 | tf_op jit(solution)/shard_map/dot_general | solution.py:195
  67.7 0.2 compare_select_fusion
  68.0 0.1 eq.141
  68.0 2.8 %fusion.12 = f32[2,128,128]{2,1,0:T(8,128)S(1)} fusion(bf16[2,128,5120]{2,1,0:T(8,128)(2,1)} %bitcast.33, s32[5120]{0:T(1024)S(1)} %eq.141), kind=kOutput, calls=%fused_computation.16 | convolution fusion | flops 336199680 | bytes 2772992 | tf_op jit(solution)/shard_map/dot_general | solution.py:195
  70.9 0.9 fusion.14
  71.8 2.7 %fusion.2 = f32[2,128,768]{2,1,0:T(8,128)S(1)} fusion(bf16[2,128,5120]{2,1,0:T(8,128)(2,1)S(1)} %bitcast.35, s32[768]{0:T(1024)S(1)} %iota_add_fusion, s32[5120]{0:T(1024)S(1)} %eq.141), kind=kOutput, calls=%fused_computation.3 | convolution fusion | flops 2017198080 | bytes 3431424 | tf_op jit(solution)/shard_map/dot_general | solution.py:195
  74.5 0.1 pad_maximum_fusion.2
  74.7 3.3 %collective-permute-start.1 = (f32[2,128,4]{2,1,0:T(8,128)S(1)}, f32[2,128,4]{2,1,0:T(8,128)S(1)}, u32[]{:S(2)}, u32[]{:S(2)}) collective-permute-start(f32[2,128,4]{2,1,0:T(8,128)S(1)} %fusion.56), channel_id=1, source_target_pairs={{1,0},{2,1},{3,2},{4,3},{5,4},{6,5},{7,6},{8,7},{9,8},{10,9},{11,1... | collective-permute-start | bytes 12296 | tf_op jit(solution)/shard_map/ppermute | solution.py:205
  78.0 0.2 fusion.58
  78.2 2.5 %collective-permute-start = (f32[2,128,4]{2,1,0:T(8,128)S(1)}, f32[2,128,4]{2,1,0:T(8,128)S(1)}, u32[]{:S(2)}, u32[]{:S(2)}) collective-permute-start(f32[2,128,4]{2,1,0:T(8,128)S(1)} %fusion.58), channel_id=1, source_target_pairs={{0,1},{1,2},{2,3},{3,4},{4,5},{5,6},{6,7},{7,8},{8,9},{9,10},{10,1... | collective-permute-start | bytes 12296 | tf_op jit(solution)/shard_map/ppermute | solution.py:204
  80.7 0.3 fusion.27
  81.0 1.3 %collective-permute-done.1 = f32[2,128,4]{2,1,0:T(8,128)S(1)} collective-permute-done((f32[2,128,4]{2,1,0:T(8,128)S(1)}, f32[2,128,4]{2,1,0:T(8,128)S(1)}, u32[]{:S(2)}, u32[]{:S(2)}) %collective-permute-start.1) | collective-permute-done | bytes 4128 | tf_op jit(solution)/shard_map/ppermute | solution.py:205
  82.4 6.3 %collective-permute-done = f32[2,128,4]{2,1,0:T(8,128)S(1)} collective-permute-done((f32[2,128,4]{2,1,0:T(8,128)S(1)}, f32[2,128,4]{2,1,0:T(8,128)S(1)}, u32[]{:S(2)}, u32[]{:S(2)}) %collective-permute-start) | collective-permute-done | bytes 4128 | tf_op jit(solution)/shard_map/ppermute | solution.py:204
  88.7 3.9 %fusion.31.t_ref = f32[2,128,1024]{2,1,0:T(8,128)} fusion(f32[2,128,1024]{2,1,0:T(8,128)S(1)} %fusion.27, f32[2,128,4]{2,1,0:T(8,128)S(1)} %collective-permute-done.1, f32[2,128,4]{2,1,0:T(8,128)S(1)} %collective-permute-done, f32[1024]{0:T(1024)S(1)} %get-tuple-element.15, f32[1024]{0:T(1024)S(1)} %get-tuple-element.16, f32[1024]{0:T(1024)S(1)} %get-tuple-element.9, ...), kind=kLoop, calls=%fused_computation.47 | loop fusion | flops 7077888 | bytes 2142208 | tf_op jit(solution)/shard_map/add | solution.py:213
  92.6 12.0 %shard_map.77 = (f32[2,6,1024]{2,1,0:T(8,128)}, f32[2,1024]{1,0:T(2,128)}) custom-call(f32[2,128,1024]{2,1,0:T(8,128)} %fusion.31.t_ref, f32[128,8]{1,0:T(8,128)} %constant.79.clone.phit_ref, f32[32,128]{1,0:T(8,128)} %constant.80.clone.psi_ref), custom_call_target="tpu_custom_call" | custom-call | tf_op jit(solution)/shard_map/pallas_call | solution.py:140
  104.6 1.5 %copy.41 = f32[2,6,1024]{2,0,1:T(2,128)} copy(f32[2,6,1024]{2,1,0:T(8,128)} %get-tuple-element.6) | data formatting | bytes 98304 | tf_op jit(solution)/shard_map/pallas_call | solution.py:140
  (23 shorter events, 0.2 us)
Async XLA Ops:
  1.4 0.9 copy-start.2
  1.8 1.1 %copy-start.4 = (s32[2048]{0:T(1024)S(1)}, s32[2048]{0:T(1024)}, u32[]{:S(2)}) copy-start(s32[2048]{0:T(1024)} %param.8) | copy-start | bytes 24580
  1.9 2.2 %copy-start = (bf16[2048,3,256]{2,0,1:T(8,128)(2,1)S(1)}, bf16[2048,3,256]{2,0,1:T(8,128)(2,1)}, u32[]{:S(2)}) copy-start(bf16[2048,3,256]{2,0,1:T(8,128)(2,1)} %param.6) | copy-start | bytes 9437188
  19.1 10.5 %copy-start.3 = (s32[4,1024]{1,0:T(4,128)S(1)}, s32[4,1024]{1,0:T(4,128)}, u32[]{:S(2)}) copy-start(s32[4,1024]{1,0:T(4,128)} %param.9) | copy-start | bytes 49156
  19.1 45.8 %all-to-all-start = ((bf16[128,40,256]{2,1,0:T(8,128)(2,1)}), bf16[128,40,256]{2,1,0:T(8,128)(2,1)S(1)}, u32[]{:S(2)}, u32[]{:S(2)}) async-start(bf16[128,40,256]{2,1,0:T(8,128)(2,1)} %fusion.10), calls=%async_computation | async-start | bytes 5242880 | tf_op jit(solution)/shard_map/all_to_all | solution.py:182
  67.9 2.9 %copy-start.1 = (bf16[256,5120]{1,0:T(8,128)(2,1)S(1)}, bf16[256,5120]{1,0:T(8,128)(2,1)}, u32[]{:S(2)}) copy-start(bf16[256,5120]{1,0:T(8,128)(2,1)} %copy.34) | copy-start | bytes 7864324
  74.7 7.7 %collective-permute-start.1 = (f32[2,128,4]{2,1,0:T(8,128)S(1)}, f32[2,128,4]{2,1,0:T(8,128)S(1)}, u32[]{:S(2)}, u32[]{:S(2)}) collective-permute-start(f32[2,128,4]{2,1,0:T(8,128)S(1)} %fusion.56), channel_id=1, source_target_pairs={{1,0},{2,1},{3,2},{4,3},{5,4},{6,5},{7,6},{8,7},{9,8},{10,9},{11,1... | collective-permute-start | bytes 12296 | tf_op jit(solution)/shard_map/ppermute | solution.py:205
  78.2 10.5 %collective-permute-start = (f32[2,128,4]{2,1,0:T(8,128)S(1)}, f32[2,128,4]{2,1,0:T(8,128)S(1)}, u32[]{:S(2)}, u32[]{:S(2)}) collective-permute-start(f32[2,128,4]{2,1,0:T(8,128)S(1)} %fusion.58), channel_id=1, source_target_pairs={{0,1},{1,2},{2,3},{3,4},{4,5},{5,6},{6,7},{7,8},{8,9},{9,10},{10,1... | collective-permute-start | bytes 12296 | tf_op jit(solution)/shard_map/ppermute | solution.py:204

commit v9 on v4

--- a/solution.py
+++ b/solution.py
@@ -63,7 +63,7 @@
 
 def fit_kernel(t_ref, phit_ref, psi_ref, lam_ref, fit_ref, lam_s, dense_ref):
     spec, levels, cells = t_ref.shape
-    count = lam_ref.shape[1]
+    count = lam_ref.shape[0]
     used = count + 1 + len(pair_list(count))
     groups = 8 // spec
     part = cells // groups
@@ -110,7 +110,8 @@
         whole = jnp.sum(target, axis=0, keepdims=True)
         ratio = jnp.log(target / whole) - (exponent - log_norm)
         fit_ref[s : s + 1, :] = 2.0 * jnp.sum(target * ratio, axis=0, keepdims=True) / levels
-        lam_ref[s] = lam_s[s, 0:count, :]
+        for m in range(count):
+            lam_ref[m, s : s + 1, :] = lam_s[s, m : m + 1, :]
 
 
 def legendre_numpy(levels, count):
@@ -137,10 +138,10 @@
     height = -(-len(rows) // 8) * 8
     rows += [np.zeros((levels,), np.float32)] * (height - len(rows))
     psi = np.stack(rows, axis=0)
-    return pl.pallas_call(
+    lam, fit = pl.pallas_call(
         fit_kernel,
         out_shape=(
-            jax.ShapeDtypeStruct((spec, count, cells), jnp.float32),
+            jax.ShapeDtypeStruct((count, spec, cells), jnp.float32),
             jax.ShapeDtypeStruct((spec, cells), jnp.float32),
         ),
         scratch_shapes=[
@@ -148,6 +149,7 @@
             pltpu.VMEM((height, 8, cells * spec // 8), jnp.float32),
         ],
     )(target, jnp.asarray(phit), jnp.asarray(psi))
+    return jnp.transpose(lam, (1, 0, 2)), fit
 
 
 def smooth_levels(field):

time: 107 us -> 105 us (0.981)
  local copies, waits for them, and re-layouts: 7.81 us -> 6.31 us
    pallas_call x1 -> x0, local copies, waits for them, and re-layouts: 1.5 us -> none  [fit_all(): pl.pallas_call(fit_kernel, out_shape=(jax.ShapeDtypeStruct((spec, count,...]
where the time goes in v9:
time: 105 us
  waiting for transfers between devices  42.8 us (41%)
  matrix products  17.4 us (17%)
  starting transfers between devices  16.3 us (16%)
  Pallas kernels  12 us (11%)
  other arithmetic  9.22 us (9%)
  local copies, waits for them, and re-layouts  6.31 us (6%)
    all_to_all x1, waiting for transfers between devices, body_inner(): lax.all_to_all(message, ('cell', 'own'), split_axis=0, concat_axis=0, til...  35.1 us
    pallas_call x1, Pallas kernels, fit_all(): pl.pallas_call(fit_kernel, out_shape=(jax.ShapeDtypeStruct((count, spec,...  12 us
    all_to_all x1, starting transfers between devices, body_inner(): lax.all_to_all(message, ('cell', 'own'), split_axis=0, concat_axis=0, til...  10.4 us
    dot_general x1, matrix products, body_inner(): sent = jnp.dot(place, payload, preferred_element_type=jnp.float32)  10.4 us
    ppermute x1, waiting for transfers between devices, body_inner(): below = lax.ppermute(edge_lev[:, :, W:], ('cell', 'own'), forward)  6.14 us
    dot_general x1, matrix products, body_inner(): lax.dot_general(recv_rows, select, (((0,), (0,)), ((), ())), preferred_el...  6.05 us
    add x1, other arithmetic, body_inner(): target + weight[None, None, :] * lax.slice_in_dim(rimmed, W + shift, W +...  3.87 us
    ppermute x1, starting transfers between devices, body_inner(): above = lax.ppermute(edge_lev[:, :, :W], ('cell', 'own'), backward)  3.29 us
  transfers between devices with their start and end apart: 3, of which 3 were waited for; matrix products, arithmetic and copies ran while one was open for 0% of the time, Pallas kernels for 0%

profile of v9, /device:TPU:8, one launch (start us, length us, event | category | flops | bytes accessed | tf_op | source)
XLA Modules:
  0.0 104.8 jit_solution(3699644152402201540)
XLA Ops:
  0.6 0.8 copy.27
  1.4 0.3 fusion.42
  1.8 0.1 add_add_fusion
  1.9 0.0 copy-start
  1.9 0.3 copy.28
  2.3 0.0 copy-done.2
  2.3 0.6 fusion.41
  2.9 0.0 copy-done.4
  3.0 1.1 %copy.36 = bf16[2048,2]{1,0:T(8,128)(2,1)} copy(bf16[2048,2]{0,1:T(2,128)(2,1)S(1)} %pad_maximum_fusion.2) | data formatting | bytes 16384
  4.1 1.7 %reduce_sum.103 = bf16[2048,256]{1,0:T(8,128)(2,1)} reduce(bf16[2048,3,256]{2,0,1:T(8,128)(2,1)S(1)} %copy-done, bf16[]{:T(256)} %constant.30.clone.1), dimensions={1}, to_apply=%region_3.4 | reduce | flops 1048576 | bytes 4194306 | tf_op jit(solution)/shard_map/reduce_sum | solution.py:167
  5.9 10.4 %fusion.6 = bf16[4096,384]{1,0:T(8,128)(2,1)S(1)} fusion(s32[2048]{0:T(1024)S(1)} %multiply_add_fusion, bf16[2048,2]{1,0:T(8,128)(2,1)} %copy.36, bf16[2048,256]{1,0:T(8,128)(2,1)} %reduce_sum.103), kind=kOutput, calls=%fused_computation.7 | convolution fusion | flops 6457131008 | bytes 4210688 | tf_op jit(solution)/shard_map/dot_general | solution.py:178
  16.3 0.1 slice.93
  16.4 0.1 slice.92
  16.5 0.8 copy.30
  17.3 1.8 %fusion.9 = bf16[128,40,256]{2,1,0:T(8,128)(2,1)} fusion(bf16[128,2,32]{2,1,0:T(2,128)(2,1)S(1)} %bitcast.32, bf16[128,32,256]{2,1,0:T(8,128)(2,1)S(1)} %bitcast.28), kind=kLoop, calls=%fused_computation.12 | loop fusion | flops 7864320 | bytes 4734976 | tf_op jit(solution)/shard_map/concatenate | solution.py:183
  19.1 10.4 %all-to-all-start = ((bf16[128,40,256]{2,1,0:T(8,128)(2,1)}), bf16[128,40,256]{2,1,0:T(8,128)(2,1)S(1)}, u32[]{:S(2)}, u32[]{:S(2)}) async-start(bf16[128,40,256]{2,1,0:T(8,128)(2,1)} %fusion.9), calls=%async_computation | async-start | bytes 5242880 | tf_op jit(solution)/shard_map/all_to_all | solution.py:184
  29.6 0.1 pad_add_fusion
  29.7 0.1 convert_reduce_fusion.8
  29.8 35.1 %all-to-all-done = bf16[128,40,256]{2,1,0:T(8,128)(2,1)S(1)} async-done(((bf16[128,40,256]{2,1,0:T(8,128)(2,1)}), bf16[128,40,256]{2,1,0:T(8,128)(2,1)S(1)}, u32[]{:S(2)}, u32[]{:S(2)}) %all-to-all-start) | async-done | bytes 2621472 | tf_op jit(solution)/shard_map/all_to_all | solution.py:184
  64.9 2.8 %copy.31 = bf16[256,5120]{1,0:T(8,128)(2,1)} copy(bf16[256,5120]{0,1:T(8,128)(2,1)S(1)} %bitcast.27) | data formatting | bytes 5242880 | tf_op jit(solution)/shard_map/dot_general | solution.py:207
  67.7 0.2 compare_select_fusion
  67.9 0.1 eq.130
  68.0 6.1 %fusion.2 = f32[2,128,1024]{2,1,0:T(8,128)S(1)} fusion(bf16[2,128,5120]{2,1,0:T(8,128)(2,1)} %bitcast.30, s32[5120]{0:T(1024)S(1)} %eq.130), kind=kOutput, calls=%fused_computation.4 | convolution fusion | flops 2689597440 | bytes 3690496 | tf_op jit(solution)/shard_map/dot_general | solution.py:207
  74.1 0.9 fusion.46
  75.0 0.1 fusion.63
  75.1 3.3 %collective-permute-start.1 = (f32[2,128,4]{2,1,0:T(8,128)S(1)}, f32[2,128,4]{2,1,0:T(8,128)S(1)}, u32[]{:S(2)}, u32[]{:S(2)}) collective-permute-start(f32[2,128,4]{2,1,0:T(8,128)S(1)} %get-tuple-element.16), channel_id=1, source_target_pairs={{1,0},{2,1},{3,2},{4,3},{5,4},{6,5},{7,6},{8,7},{9,8},{10,9},{11,1... | collective-permute-start | bytes 12296 | tf_op jit(solution)/shard_map/ppermute | solution.py:203
  78.5 2.5 %collective-permute-start = (f32[2,128,4]{2,1,0:T(8,128)S(1)}, f32[2,128,4]{2,1,0:T(8,128)S(1)}, u32[]{:S(2)}, u32[]{:S(2)}) collective-permute-start(f32[2,128,4]{2,1,0:T(8,128)S(1)} %get-tuple-element.15), channel_id=1, source_target_pairs={{0,1},{1,2},{2,3},{3,4},{4,5},{5,6},{6,7},{7,8},{8,9},{9,10},{10,1... | collective-permute-start | bytes 12296 | tf_op jit(solution)/shard_map/ppermute | solution.py:202
  81.0 0.3 fusion.17
  81.3 1.5 %collective-permute-done.1 = f32[2,128,4]{2,1,0:T(8,128)S(1)} collective-permute-done((f32[2,128,4]{2,1,0:T(8,128)S(1)}, f32[2,128,4]{2,1,0:T(8,128)S(1)}, u32[]{:S(2)}, u32[]{:S(2)}) %collective-permute-start.1) | collective-permute-done | bytes 4128 | tf_op jit(solution)/shard_map/ppermute | solution.py:203
  82.8 6.1 %collective-permute-done = f32[2,128,4]{2,1,0:T(8,128)S(1)} collective-permute-done((f32[2,128,4]{2,1,0:T(8,128)S(1)}, f32[2,128,4]{2,1,0:T(8,128)S(1)}, u32[]{:S(2)}, u32[]{:S(2)}) %collective-permute-start) | collective-permute-done | bytes 4128 | tf_op jit(solution)/shard_map/ppermute | solution.py:202
  89.0 3.9 %fusion.21.t_ref = f32[2,128,1024]{2,1,0:T(8,128)} fusion(f32[2,128,1024]{2,1,0:T(8,128)S(1)} %fusion.17, f32[2,128,4]{2,1,0:T(8,128)S(1)} %collective-permute-done.1, f32[2,128,4]{2,1,0:T(8,128)S(1)} %collective-permute-done, f32[1024]{0:T(1024)S(1)} %get-tuple-element.13, f32[1024]{0:T(1024)S(1)} %get-tuple-element.14, f32[1024]{0:T(1024)S(1)} %get-tuple-element.7, ...), kind=kLoop, calls=%fused_computation.37 | loop fusion | flops 7077888 | bytes 2142208 | tf_op jit(solution)/shard_map/add | solution.py:216
  92.8 12.0 %shard_map.77 = (f32[6,2,1024]{2,1,0:T(2,128)}, f32[2,1024]{1,0:T(2,128)}) custom-call(f32[2,128,1024]{2,1,0:T(8,128)} %fusion.21.t_ref, f32[128,8]{1,0:T(8,128)} %constant.77.clone.phit_ref, f32[32,128]{1,0:T(8,128)} %constant.78.clone.psi_ref), custom_call_target="tpu_custom_call" | custom-call | tf_op jit(solution)/shard_map/pallas_call | solution.py:141
  (19 shorter events, 0.2 us)
Async XLA Ops:
  1.4 0.9 copy-start.2
  1.8 1.1 %copy-start.4 = (s32[2048]{0:T(1024)S(1)}, s32[2048]{0:T(1024)}, u32[]{:S(2)}) copy-start(s32[2048]{0:T(1024)} %param.8) | copy-start | bytes 24580
  1.9 2.2 %copy-start = (bf16[2048,3,256]{2,0,1:T(8,128)(2,1)S(1)}, bf16[2048,3,256]{2,0,1:T(8,128)(2,1)}, u32[]{:S(2)}) copy-start(bf16[2048,3,256]{2,0,1:T(8,128)(2,1)} %param.6) | copy-start | bytes 9437188
  19.1 10.6 %copy-start.3 = (s32[4,1024]{1,0:T(4,128)S(1)}, s32[4,1024]{1,0:T(4,128)}, u32[]{:S(2)}) copy-start(s32[4,1024]{1,0:T(4,128)} %param.9) | copy-start | bytes 49156
  19.1 45.8 %all-to-all-start = ((bf16[128,40,256]{2,1,0:T(8,128)(2,1)}), bf16[128,40,256]{2,1,0:T(8,128)(2,1)S(1)}, u32[]{:S(2)}, u32[]{:S(2)}) async-start(bf16[128,40,256]{2,1,0:T(8,128)(2,1)} %fusion.9), calls=%async_computation | async-start | bytes 5242880 | tf_op jit(solution)/shard_map/all_to_all | solution.py:184
  68.0 6.1 %copy-start.1 = (bf16[256,5120]{1,0:T(8,128)(2,1)S(1)}, bf16[256,5120]{1,0:T(8,128)(2,1)}, u32[]{:S(2)}) copy-start(bf16[256,5120]{1,0:T(8,128)(2,1)} %copy.31) | copy-start | bytes 7864324
  75.1 7.7 %collective-permute-start.1 = (f32[2,128,4]{2,1,0:T(8,128)S(1)}, f32[2,128,4]{2,1,0:T(8,128)S(1)}, u32[]{:S(2)}, u32[]{:S(2)}) collective-permute-start(f32[2,128,4]{2,1,0:T(8,128)S(1)} %get-tuple-element.16), channel_id=1, source_target_pairs={{1,0},{2,1},{3,2},{4,3},{5,4},{6,5},{7,6},{8,7},{9,8},{10,9},{11,1... | collective-permute-start | bytes 12296 | tf_op jit(solution)/shard_map/ppermute | solution.py:203
  78.5 10.5 %collective-permute-start = (f32[2,128,4]{2,1,0:T(8,128)S(1)}, f32[2,128,4]{2,1,0:T(8,128)S(1)}, u32[]{:S(2)}, u32[]{:S(2)}) collective-permute-start(f32[2,128,4]{2,1,0:T(8,128)S(1)} %get-tuple-element.15), channel_id=1, source_target_pairs={{0,1},{1,2},{2,3},{3,4},{4,5},{5,6},{6,7},{7,8},{8,9},{9,10},{10,1... | collective-permute-start | bytes 12296 | tf_op jit(solution)/shard_map/ppermute | solution.py:202

commit v10 on v9

--- a/solution.py
+++ b/solution.py
@@ -61,8 +61,27 @@
     return [lam[m] - 0.5 * delta[m] for m in range(count)]
 
 
-def fit_kernel(t_ref, phit_ref, psi_ref, lam_ref, fit_ref, lam_s, dense_ref):
-    spec, levels, cells = t_ref.shape
+def fit_kernel(
+    h_ref, rim_ref, w_ref, phit_ref, psi_ref, lam_ref, fit_ref, lam_s, dense_ref, t_ref, ext_ref
+):
+    spec, levels, cells = h_ref.shape
+    pad = (ext_ref.shape[2] - cells) // 2
+    rim = rim_ref.shape[2] // 2
+    ext_ref[...] = jnp.zeros(ext_ref.shape, jnp.float32)
+    for s in range(spec):
+        field = h_ref[s]
+        t_ref[s] = field
+        lower = jnp.concatenate([jnp.zeros((1, cells), jnp.float32), t_ref[s, : levels - 1, :]], axis=0)
+        upper = jnp.concatenate([t_ref[s, 1:, :], jnp.zeros((1, cells), jnp.float32)], axis=0)
+        levelled = 0.5 * field + 0.25 * (lower + upper)
+        ext_ref[s, :, pad : pad + cells] = levelled
+        ext_ref[s, :, pad - rim : pad] = rim_ref[s, :, :rim]
+        ext_ref[s, :, pad + cells : pad + cells + rim] = rim_ref[s, :, rim:]
+        target = 1.0 + levelled
+        for k in range(w_ref.shape[0]):
+            shift = k - w_ref.shape[0] // 2
+            target = target + w_ref[k : k + 1, :] * ext_ref[s, :, pad + shift : pad + shift + cells]
+        t_ref[s] = target
     count = lam_ref.shape[0]
     used = count + 1 + len(pair_list(count))
     groups = 8 // spec
@@ -126,8 +145,8 @@
     return np.stack(table, axis=0).astype(np.float32)
 
 
-def fit_all(target, count):
-    spec, levels, cells = target.shape
+def fit_all(cellhist, rim, weights, count):
+    spec, levels, cells = cellhist.shape
     phi = legendre_numpy(levels, count)
     pairs = pair_list(count)
     width = 8
@@ -147,8 +166,10 @@
         scratch_shapes=[
             pltpu.VMEM((spec, width, cells), jnp.float32),
             pltpu.VMEM((height, 8, cells * spec // 8), jnp.float32),
+            pltpu.VMEM((spec, levels, cells), jnp.float32),
+            pltpu.VMEM((spec, levels, cells + 256), jnp.float32),
         ],
-    )(target, jnp.asarray(phit), jnp.asarray(psi))
+    )(cellhist, rim, weights, jnp.asarray(phit), jnp.asarray(psi))
     return jnp.transpose(lam, (1, 0, 2)), fit
 
 
@@ -208,15 +229,11 @@
         recv_rows, select, (((0,), (0,)), ((), ())), preferred_element_type=jnp.float32
     )
     cellhist = summed.reshape(SPEC, width // SPEC, cells)
-    levelled = smooth_levels(cellhist)
-    rimmed = jnp.concatenate([below, levelled, above], axis=2)
-    target = 1.0 + levelled
-    for shift in range(-W, W + 1):
-        weight = jnp.sum((offsets == shift).astype(jnp.float32), axis=0)
-        target = target + weight[None, None, :] * lax.slice_in_dim(
-            rimmed, W + shift, W + shift + cells, axis=2
-        )
-    return fit_all(target, MOM)
+    weights = jnp.stack(
+        [jnp.sum((offsets == shift).astype(jnp.float32), axis=0) for shift in range(-W, W + 1)]
+    )
+    rim = jnp.concatenate([below, above], axis=2)
+    return fit_all(cellhist, rim, weights, MOM)
 
 
 def solution(mesh):

time: 105 us -> 101 us (0.962)
  waiting for transfers between devices: 42.8 us -> 35.1 us
  local copies, waits for them, and re-layouts: 6.31 us -> 9.7 us
  other arithmetic: 9.22 us -> 6.41 us
  Pallas kernels: 12 us -> 14.7 us
    ppermute x1, waiting for transfers between devices: 6.14 us -> 1.25 us  [body_inner(): below = lax.ppermute(edge_lev[:, :, W:], ('cell', 'own'), forward)]
    add x1 -> x0, other arithmetic: 3.87 us -> none  [body_inner(): target + weight[None, None, :] * lax.slice_in_dim(rimmed, W + shift, W +...]
    pallas_call x1, Pallas kernels: 12 us -> 14.7 us  [fit_all(): pl.pallas_call(fit_kernel, out_shape=(jax.ShapeDtypeStruct((count, spec,...]
    dot_general x1, matrix products: 0.87 us -> 2.66 us  [body_inner(): lax.dot_general(recv_rows, edge_select, (((0,), (0,)), ((), ())), preferr...]
    ppermute x1, waiting for transfers between devices: 1.52 us -> 0.01 us  [body_inner(): above = lax.ppermute(edge_lev[:, :, :W], ('cell', 'own'), backward)]
    dot_general x1, matrix products: 10.4 us -> 9.04 us  [body_inner(): sent = jnp.dot(place, payload, preferred_element_type=jnp.float32)]
    reduce_sum x1, other arithmetic: 1.74 us -> 3.03 us  [body_inner(): packed = jnp.sum(hist, axis=1, dtype=jnp.float32).astype(jnp.bfloat16)]
    another operation x2 -> x3, local copies, waits for them, and re-layouts: 0.01 us -> 1.28 us  [the longest x1 1.27 us: body_inner(): jnp.stack([jnp.sum((offsets == shift).astype(jnp.float32), axis=0) for sh...]
  transfers between devices with their start and end apart: 3 -> 3, of which waited for: 3 -> 2; matrix products, arithmetic and copies ran while one was open for 0% -> 7% of each run, Pallas kernels for 0% -> 0%
where the time goes in v10:
time: 101 us; the launch traced here: 100 us
  waiting for transfers between devices  35.1 us (35%)
  matrix products  16.8 us (17%)
  starting transfers between devices  16.5 us (16%)
  Pallas kernels  14.7 us (15%)
  local copies, waits for them, and re-layouts  9.7 us (10%)
  other arithmetic  6.41 us (6%)
    all_to_all x1, waiting for transfers between devices, body_inner(): lax.all_to_all(message, ('cell', 'own'), split_axis=0, concat_axis=0, til...  33.9 us
    pallas_call x1, Pallas kernels, fit_all(): pl.pallas_call(fit_kernel, out_shape=(jax.ShapeDtypeStruct((count, spec,...  14.7 us
    all_to_all x1, starting transfers between devices, body_inner(): lax.all_to_all(message, ('cell', 'own'), split_axis=0, concat_axis=0, til...  10.4 us
    dot_general x1, matrix products, body_inner(): sent = jnp.dot(place, payload, preferred_element_type=jnp.float32)  9.04 us
    dot_general x1, matrix products, body_inner(): lax.dot_general(recv_rows, select, (((0,), (0,)), ((), ())), preferred_el...  5.15 us
    ppermute x1, starting transfers between devices, body_inner(): above = lax.ppermute(edge_lev[:, :, :W], ('cell', 'own'), backward)  3.31 us
    reduce_sum x1, other arithmetic, body_inner(): packed = jnp.sum(hist, axis=1, dtype=jnp.float32).astype(jnp.bfloat16)  3.03 us
    dot_general x1, local copies, waits for them, and re-layouts, body_inner(): lax.dot_general(recv_rows, select, (((0,), (0,)), ((), ())), preferred_el...  2.83 us
  transfers between devices with their start and end apart: 3, of which 2 were waited for; matrix products, arithmetic and copies ran while one was open for 7% of the time, Pallas kernels for 0%

profile of v10, /device:TPU:8, one launch (start us, length us, event | category | flops | bytes accessed | tf_op | source)
XLA Modules:
  0.0 100.1 jit_solution(10581221208036180547)
XLA Ops:
  0.6 0.8 copy.27
  1.4 0.3 fusion.16
  1.8 0.1 add_add_fusion
  1.9 0.3 copy.28
  2.3 0.0 copy-done.1
  2.3 0.6 fusion.15
  2.9 0.0 copy-done.3
  3.0 0.3 copy.33
  3.3 3.0 %reduce_sum.103 = bf16[2048,256]{1,0:T(8,128)(2,1)S(1)} reduce(bf16[2048,3,256]{2,0,1:T(8,128)(2,1)} %param.6, bf16[]{:T(256)} %constant.32.clone.1), dimensions={1}, to_apply=%region_3.4 | reduce | flops 1048576 | bytes 4194306 | tf_op jit(solution)/shard_map/reduce_sum | solution.py:188
  6.4 9.0 %fusion.6 = bf16[4096,384]{1,0:T(8,128)(2,1)S(1)} fusion(s32[2048]{0:T(1024)S(1)} %multiply_add_fusion, bf16[2048,2]{1,0:T(8,128)(2,1)S(1)} %copy.33, bf16[2048,256]{1,0:T(8,128)(2,1)S(1)} %reduce_sum.103), kind=kOutput, calls=%fused_computation.7 | convolution fusion | flops 6457131008 | bytes 4210688 | tf_op jit(solution)/shard_map/dot_general | solution.py:199
  15.4 1.1 %slice.45 = bf16[4096,2]{1,0:T(8,128)(2,1)} slice(bf16[4096,384]{1,0:T(8,128)(2,1)S(1)} %fusion.6), slice={[0:4096], [256:258]} | slice | bytes 32768 | tf_op jit(solution)/shard_map/slice | solution.py:201
  16.5 0.1 slice.44
  16.6 2.0 %copy.30 = bf16[128,32,2]{1,2,0:T(2,128)(2,1)S(1)} copy(bf16[128,32,2]{2,1,0:T(8,128)(2,1)} %bitcast.40) | data formatting | bytes 32768 | tf_op jit(solution)/shard_map/convert_element_type | solution.py:202
  18.6 1.8 %fusion.9 = bf16[128,40,256]{2,1,0:T(8,128)(2,1)} fusion(bf16[128,2,32]{2,1,0:T(2,128)(2,1)S(1)} %bitcast.41, bf16[128,32,256]{2,1,0:T(8,128)(2,1)S(1)} %bitcast.39), kind=kLoop, calls=%fused_computation.12 | loop fusion | flops 7864320 | bytes 4734976 | tf_op jit(solution)/shard_map/concatenate | solution.py:204
  20.4 10.4 %all-to-all-start = ((bf16[128,40,256]{2,1,0:T(8,128)(2,1)}), bf16[128,40,256]{2,1,0:T(8,128)(2,1)S(1)}, u32[]{:S(2)}, u32[]{:S(2)}) async-start(bf16[128,40,256]{2,1,0:T(8,128)(2,1)} %fusion.9), calls=%async_computation | async-start | bytes 5242880 | tf_op jit(solution)/shard_map/all_to_all | solution.py:205
  30.9 0.0 copy-done.2
  30.9 0.1 convert_reduce_fusion
  31.0 1.3 %stack.54.w_ref = f32[9,1024]{1,0:T(8,128)} concatenate(f32[1,1024]{1,0:T(1,128)S(1)} %bitcast.53, f32[1,1024]{1,0:T(1,128)S(1)} %bitcast.52, f32[1,1024]{1,0:T(1,128)S(1)} %bitcast.51, f32[1,1024]{1,0:T(1,128)S(1)} %bitcast.50, f32[1,1024]{1,0:T(1,128)S(1)} %bitcast.49, f32[1,1024]{1,0:T(1,128)S(1)} %bitcast.48, f32[1,1024]{1,0:T(1,128)S(1)} %bitcast.47, ...), dimensions={0} | concatenate | bytes 73728 | tf_op jit(solution)/shard_map/stack | solution.py:232
  32.3 0.1 pad_add_fusion
  32.4 33.9 %all-to-all-done = bf16[128,40,256]{2,1,0:T(8,128)(2,1)S(1)} async-done(((bf16[128,40,256]{2,1,0:T(8,128)(2,1)}), bf16[128,40,256]{2,1,0:T(8,128)(2,1)S(1)}, u32[]{:S(2)}, u32[]{:S(2)}) %all-to-all-start) | async-done | bytes 2621472 | tf_op jit(solution)/shard_map/all_to_all | solution.py:205
  66.2 2.8 %copy.31 = bf16[256,5120]{1,0:T(8,128)(2,1)} copy(bf16[256,5120]{0,1:T(8,128)(2,1)S(1)} %bitcast.36) | data formatting | bytes 5242880 | tf_op jit(solution)/shard_map/dot_general | solution.py:228
  69.0 0.2 compare_select_fusion
  69.3 0.1 eq.130
  69.4 2.7 %fusion.20 = f32[2,128,8]{1,2,0:T(8,128)S(1)} fusion(bf16[2,128,5120]{2,1,0:T(8,128)(2,1)} %bitcast.37, s32[5120]{0:T(1024)S(1)} %eq.130, s32[8]{0:T(128)S(1)} %pad_add_fusion), kind=kOutput, calls=%fused_computation.27 | convolution fusion | flops 21012480 | bytes 2650144 | tf_op jit(solution)/shard_map/dot_general | solution.py:216
  72.0 0.1 fusion.31
  72.1 3.3 %collective-permute-start.1 = (f32[2,128,4]{1,2,0:T(4,128)S(1)}, f32[2,128,4]{1,2,0:T(4,128)S(1)}, u32[]{:S(2)}, u32[]{:S(2)}) collective-permute-start(f32[2,128,4]{1,2,0:T(4,128)S(1)} %get-tuple-element.16), channel_id=1, source_target_pairs={{1,0},{2,1},{3,2},{4,3},{5,4},{6,5},{7,6},{8,7},{9,8},{10,9},{11,1... | collective-permute-start | bytes 12296 | tf_op jit(solution)/shard_map/ppermute | solution.py:224
  75.4 2.7 %collective-permute-start = (f32[2,128,4]{1,2,0:T(4,128)S(1)}, f32[2,128,4]{1,2,0:T(4,128)S(1)}, u32[]{:S(2)}, u32[]{:S(2)}) collective-permute-start(f32[2,128,4]{1,2,0:T(4,128)S(1)} %get-tuple-element.15), channel_id=1, source_target_pairs={{0,1},{1,2},{2,3},{3,4},{4,5},{5,6},{6,7},{7,8},{8,9},{9,10},{10,1... | collective-permute-start | bytes 12296 | tf_op jit(solution)/shard_map/ppermute | solution.py:223
  78.2 5.1 %fusion.2.h_ref = f32[2,128,1024]{2,1,0:T(8,128)} fusion(bf16[2,128,5120]{2,1,0:T(8,128)(2,1)S(1)} %bitcast.38, s32[5120]{0:T(1024)S(1)} %eq.130), kind=kOutput, calls=%fused_computation.4 | convolution fusion | flops 2689597440 | bytes 3690496 | tf_op jit(solution)/shard_map/dot_general | solution.py:228
  83.3 0.0 collective-permute-done.1
  83.3 1.3 %collective-permute-done = f32[2,128,4]{1,2,0:T(4,128)S(1)} collective-permute-done((f32[2,128,4]{1,2,0:T(4,128)S(1)}, f32[2,128,4]{1,2,0:T(4,128)S(1)}, u32[]{:S(2)}, u32[]{:S(2)}) %collective-permute-start) | collective-permute-done | bytes 4128 | tf_op jit(solution)/shard_map/ppermute | solution.py:223
  84.6 0.8 copy.32.rim_ref
  85.4 14.7 %shard_map.77 = (f32[6,2,1024]{2,1,0:T(2,128)}, f32[2,1024]{1,0:T(2,128)}) custom-call(f32[2,128,1024]{2,1,0:T(8,128)} %fusion.2.h_ref, f32[2,128,8]{2,1,0:T(8,128)} %copy.32.rim_ref, f32[9,1024]{1,0:T(8,128)} %stack.54.w_ref, f32[128,8]{1,0:T(8,128)} %constant.73.clone.phit_ref, f32[32,128]{1,0:T(8,128)} %constant.74.clone.psi_ref), custom_call_target="tpu_custom_call" | custom-call | tf_op jit(solution)/shard_map/pallas_call | solution.py:160
  (18 shorter events, 0.1 us)
Async XLA Ops:
  1.4 0.8 copy-start.1
  1.8 1.1 %copy-start.3 = (s32[2048]{0:T(1024)S(1)}, s32[2048]{0:T(1024)}, u32[]{:S(2)}) copy-start(s32[2048]{0:T(1024)} %param.8) | copy-start | bytes 24580
  20.4 10.5 %copy-start.2 = (s32[4,1024]{1,0:T(4,128)S(1)}, s32[4,1024]{1,0:T(4,128)}, u32[]{:S(2)}) copy-start(s32[4,1024]{1,0:T(4,128)} %param.9) | copy-start | bytes 49156
  20.4 45.8 %all-to-all-start = ((bf16[128,40,256]{2,1,0:T(8,128)(2,1)}), bf16[128,40,256]{2,1,0:T(8,128)(2,1)S(1)}, u32[]{:S(2)}, u32[]{:S(2)}) async-start(bf16[128,40,256]{2,1,0:T(8,128)(2,1)} %fusion.9), calls=%async_computation | async-start | bytes 5242880 | tf_op jit(solution)/shard_map/all_to_all | solution.py:205
  69.3 8.9 %copy-start = (bf16[256,5120]{1,0:T(8,128)(2,1)S(1)}, bf16[256,5120]{1,0:T(8,128)(2,1)}, u32[]{:S(2)}) copy-start(bf16[256,5120]{1,0:T(8,128)(2,1)} %copy.31) | copy-start | bytes 7864324
  72.1 11.2 %collective-permute-start.1 = (f32[2,128,4]{1,2,0:T(4,128)S(1)}, f32[2,128,4]{1,2,0:T(4,128)S(1)}, u32[]{:S(2)}, u32[]{:S(2)}) collective-permute-start(f32[2,128,4]{1,2,0:T(4,128)S(1)} %get-tuple-element.16), channel_id=1, source_target_pairs={{1,0},{2,1},{3,2},{4,3},{5,4},{6,5},{7,6},{8,7},{9,8},{10,9},{11,1... | collective-permute-start | bytes 12296 | tf_op jit(solution)/shard_map/ppermute | solution.py:224
  75.4 9.1 %collective-permute-start = (f32[2,128,4]{1,2,0:T(4,128)S(1)}, f32[2,128,4]{1,2,0:T(4,128)S(1)}, u32[]{:S(2)}, u32[]{:S(2)}) collective-permute-start(f32[2,128,4]{1,2,0:T(4,128)S(1)} %get-tuple-element.15), channel_id=1, source_target_pairs={{0,1},{1,2},{2,3},{3,4},{4,5},{5,6},{6,7},{7,8},{8,9},{9,10},{10,1... | collective-permute-start | bytes 12296 | tf_op jit(solution)/shard_map/ppermute | solution.py:223

commit v11 on v9

--- a/solution.py
+++ b/solution.py
@@ -171,8 +171,10 @@
     )
     ranks = jnp.sum((jnp.cumsum(member, axis=0) - 1) * member, axis=1)
     position = target_block * capacity + ranks
-    codes = jnp.stack([cell_in // CODE + 1, cell_in % CODE], axis=1).astype(jnp.bfloat16)
-    codes = jnp.pad(codes, ((0, 0), (0, 128 - 2)))
+    column = jnp.arange(128, dtype=jnp.int32)[None, :]
+    codes = jnp.where(
+        column == 0, cell_in[:, None] // CODE + 1, jnp.where(column == 1, cell_in[:, None] % CODE, 0)
+    ).astype(jnp.bfloat16)
     payload = jnp.concatenate([packed, codes], axis=1)
     place = (jnp.arange(slots, dtype=jnp.int32)[:, None] == position[None, :]).astype(jnp.bfloat16)
     sent = jnp.dot(place, payload, preferred_element_type=jnp.float32)

time: 105 us -> 106 us (level)
  other arithmetic: 9.22 us -> 10.5 us
    convert_element_type x0 -> x1, other arithmetic: none -> 1.29 us  [body_inner(): codes = jnp.where(column == 0, cell_in[:, None] // CODE + 1, jnp.where(co...]
where the time goes in v11:
time: 106 us
  waiting for transfers between devices  42.8 us (40%)
  matrix products  17.2 us (16%)
  starting transfers between devices  16.3 us (15%)
  Pallas kernels  12 us (11%)
  other arithmetic  10.5 us (10%)
  local copies, waits for them, and re-layouts  6.06 us (6%)
    all_to_all x1, waiting for transfers between devices, body_inner(): lax.all_to_all(message, ('cell', 'own'), split_axis=0, concat_axis=0, til...  35.1 us
    pallas_call x1, Pallas kernels, fit_all(): pl.pallas_call(fit_kernel, out_shape=(jax.ShapeDtypeStruct((count, spec,...  12 us
    all_to_all x1, starting transfers between devices, body_inner(): lax.all_to_all(message, ('cell', 'own'), split_axis=0, concat_axis=0, til...  10.4 us
    dot_general x1, matrix products, body_inner(): sent = jnp.dot(place, payload, preferred_element_type=jnp.float32)  10.3 us
    ppermute x1, waiting for transfers between devices, body_inner(): below = lax.ppermute(edge_lev[:, :, W:], ('cell', 'own'), forward)  6.16 us
    dot_general x1, matrix products, body_inner(): lax.dot_general(recv_rows, select, (((0,), (0,)), ((), ())), preferred_el...  6.05 us
    add x1, other arithmetic, body_inner(): target + weight[None, None, :] * lax.slice_in_dim(rimmed, W + shift, W +...  3.87 us
    ppermute x1, starting transfers between devices, body_inner(): above = lax.ppermute(edge_lev[:, :, :W], ('cell', 'own'), backward)  3.31 us
  transfers between devices with their start and end apart: 3, of which 3 were waited for; matrix products, arithmetic and copies ran while one was open for 0% of the time, Pallas kernels for 0%

profile of v11, /device:TPU:8, one launch (start us, length us, event | category | flops | bytes accessed | tf_op | source)
XLA Modules:
  0.0 105.7 jit_solution(5343567753672395555)
XLA Ops:
  0.6 0.8 copy.25
  1.4 0.3 fusion.39
  1.9 0.1 add_add_fusion
  1.9 0.0 copy-start
  1.9 0.3 copy.26
  2.3 0.6 fusion.38
  2.9 0.0 copy-done.4
  3.0 0.8 copy-done
  3.8 1.7 %reduce_sum.103 = bf16[2048,256]{1,0:T(8,128)(2,1)} reduce(bf16[2048,3,256]{2,0,1:T(8,128)(2,1)S(1)} %copy-done, bf16[]{:T(256)} %constant.29.clone.1), dimensions={1}, to_apply=%region_3.4 | reduce | flops 1048576 | bytes 4194306 | tf_op jit(solution)/shard_map/reduce_sum | solution.py:167
  5.6 1.3 %select_convert_fusion = bf16[2048,128]{1,0:T(8,128)(2,1)S(1)} fusion(s32[2048]{0:T(1024)S(1)} %get-tuple-element.18, s32[2048]{0:T(1024)S(1)} %get-tuple-element.17, pred[128]{0:T(512)(128)(4,1)S(1)} %get-tuple-element.19, pred[128]{0:T(512)(128)(4,1)S(1)} %get-tuple-element.20), kind=kLoop, calls=%fused_computation.58 | loop fusion | flops 786432 | bytes 540928 | tf_op jit(solution)/shard_map/convert_element_type | solution.py:177
  6.9 10.3 %fusion.6 = bf16[4096,384]{1,0:T(8,128)(2,1)S(1)} fusion(s32[2048]{0:T(1024)S(1)} %multiply_add_fusion, bf16[2048,128]{1,0:T(8,128)(2,1)S(1)} %select_convert_fusion, bf16[2048,256]{1,0:T(8,128)(2,1)} %reduce_sum.103), kind=kOutput, calls=%fused_computation.7 | convolution fusion | flops 6455558144 | bytes 4726784 | tf_op jit(solution)/shard_map/dot_general | solution.py:180
  17.2 0.1 slice.93
  17.2 0.1 slice.92
  17.4 0.8 copy.27
  18.2 1.8 %fusion.8 = bf16[128,40,256]{2,1,0:T(8,128)(2,1)} fusion(bf16[128,2,32]{2,1,0:T(2,128)(2,1)S(1)} %bitcast.32, bf16[128,32,256]{2,1,0:T(8,128)(2,1)S(1)} %bitcast.28), kind=kLoop, calls=%fused_computation.10 | loop fusion | flops 7864320 | bytes 4734976 | tf_op jit(solution)/shard_map/concatenate | solution.py:185
  20.0 10.4 %all-to-all-start = ((bf16[128,40,256]{2,1,0:T(8,128)(2,1)}), bf16[128,40,256]{2,1,0:T(8,128)(2,1)S(1)}, u32[]{:S(2)}, u32[]{:S(2)}) async-start(bf16[128,40,256]{2,1,0:T(8,128)(2,1)} %fusion.8), calls=%async_computation | async-start | bytes 5242880 | tf_op jit(solution)/shard_map/all_to_all | solution.py:186
  30.5 0.1 pad_add_fusion
  30.5 0.1 convert_reduce_fusion.8
  30.6 35.1 %all-to-all-done = bf16[128,40,256]{2,1,0:T(8,128)(2,1)S(1)} async-done(((bf16[128,40,256]{2,1,0:T(8,128)(2,1)}), bf16[128,40,256]{2,1,0:T(8,128)(2,1)S(1)}, u32[]{:S(2)}, u32[]{:S(2)}) %all-to-all-start) | async-done | bytes 2621472 | tf_op jit(solution)/shard_map/all_to_all | solution.py:186
  65.8 2.8 %copy.28 = bf16[256,5120]{1,0:T(8,128)(2,1)} copy(bf16[256,5120]{0,1:T(8,128)(2,1)S(1)} %bitcast.27) | data formatting | bytes 5242880 | tf_op jit(solution)/shard_map/dot_general | solution.py:209
  68.6 0.2 compare_select_fusion
  68.8 0.1 eq.156
  68.9 6.0 %fusion.2 = f32[2,128,1024]{2,1,0:T(8,128)S(1)} fusion(bf16[2,128,5120]{2,1,0:T(8,128)(2,1)} %bitcast.30, s32[5120]{0:T(1024)S(1)} %eq.156), kind=kOutput, calls=%fused_computation.4 | convolution fusion | flops 2689597440 | bytes 3690496 | tf_op jit(solution)/shard_map/dot_general | solution.py:209
  75.0 0.9 fusion.42
  75.9 0.1 fusion.55
  76.0 3.3 %collective-permute-start.1 = (f32[2,128,4]{2,1,0:T(8,128)S(1)}, f32[2,128,4]{2,1,0:T(8,128)S(1)}, u32[]{:S(2)}, u32[]{:S(2)}) collective-permute-start(f32[2,128,4]{2,1,0:T(8,128)S(1)} %get-tuple-element.16), channel_id=1, source_target_pairs={{1,0},{2,1},{3,2},{4,3},{5,4},{6,5},{7,6},{8,7},{9,8},{10,9},{11,1... | collective-permute-start | bytes 12296 | tf_op jit(solution)/shard_map/ppermute | solution.py:205
  79.3 2.5 %collective-permute-start = (f32[2,128,4]{2,1,0:T(8,128)S(1)}, f32[2,128,4]{2,1,0:T(8,128)S(1)}, u32[]{:S(2)}, u32[]{:S(2)}) collective-permute-start(f32[2,128,4]{2,1,0:T(8,128)S(1)} %get-tuple-element.15), channel_id=1, source_target_pairs={{0,1},{1,2},{2,3},{3,4},{4,5},{5,6},{6,7},{7,8},{8,9},{9,10},{10,1... | collective-permute-start | bytes 12296 | tf_op jit(solution)/shard_map/ppermute | solution.py:204
  81.9 0.3 fusion.14
  82.2 1.5 %collective-permute-done.1 = f32[2,128,4]{2,1,0:T(8,128)S(1)} collective-permute-done((f32[2,128,4]{2,1,0:T(8,128)S(1)}, f32[2,128,4]{2,1,0:T(8,128)S(1)}, u32[]{:S(2)}, u32[]{:S(2)}) %collective-permute-start.1) | collective-permute-done | bytes 4128 | tf_op jit(solution)/shard_map/ppermute | solution.py:205
  83.7 6.2 %collective-permute-done = f32[2,128,4]{2,1,0:T(8,128)S(1)} collective-permute-done((f32[2,128,4]{2,1,0:T(8,128)S(1)}, f32[2,128,4]{2,1,0:T(8,128)S(1)}, u32[]{:S(2)}, u32[]{:S(2)}) %collective-permute-start) | collective-permute-done | bytes 4128 | tf_op jit(solution)/shard_map/ppermute | solution.py:204
  89.8 3.9 %fusion.18.t_ref = f32[2,128,1024]{2,1,0:T(8,128)} fusion(f32[2,128,1024]{2,1,0:T(8,128)S(1)} %fusion.14, f32[2,128,4]{2,1,0:T(8,128)S(1)} %collective-permute-done.1, f32[2,128,4]{2,1,0:T(8,128)S(1)} %collective-permute-done, f32[1024]{0:T(1024)S(1)} %get-tuple-element.13, f32[1024]{0:T(1024)S(1)} %get-tuple-element.14, f32[1024]{0:T(1024)S(1)} %get-tuple-element.7, ...), kind=kLoop, calls=%fused_computation.34 | loop fusion | flops 7077888 | bytes 2142208 | tf_op jit(solution)/shard_map/add | solution.py:218
  93.7 12.0 %shard_map.77 = (f32[6,2,1024]{2,1,0:T(2,128)}, f32[2,1024]{1,0:T(2,128)}) custom-call(f32[2,128,1024]{2,1,0:T(8,128)} %fusion.18.t_ref, f32[128,8]{1,0:T(8,128)} %constant.79.clone.phit_ref, f32[32,128]{1,0:T(8,128)} %constant.80.clone.psi_ref), custom_call_target="tpu_custom_call" | custom-call | tf_op jit(solution)/shard_map/pallas_call | solution.py:141
  (17 shorter events, 0.1 us)
Async XLA Ops:
  1.4 0.9 copy-start.2
  1.8 1.1 %copy-start.4 = (s32[2048]{0:T(1024)S(1)}, s32[2048]{0:T(1024)}, u32[]{:S(2)}) copy-start(s32[2048]{0:T(1024)} %param.8) | copy-start | bytes 24580
  1.9 1.9 %copy-start = (bf16[2048,3,256]{2,0,1:T(8,128)(2,1)S(1)}, bf16[2048,3,256]{2,0,1:T(8,128)(2,1)}, u32[]{:S(2)}) copy-start(bf16[2048,3,256]{2,0,1:T(8,128)(2,1)} %param.6) | copy-start | bytes 9437188
  20.0 10.6 %copy-start.3 = (s32[4,1024]{1,0:T(4,128)S(1)}, s32[4,1024]{1,0:T(4,128)}, u32[]{:S(2)}) copy-start(s32[4,1024]{1,0:T(4,128)} %param.9) | copy-start | bytes 49156
  20.0 45.8 %all-to-all-start = ((bf16[128,40,256]{2,1,0:T(8,128)(2,1)}), bf16[128,40,256]{2,1,0:T(8,128)(2,1)S(1)}, u32[]{:S(2)}, u32[]{:S(2)}) async-start(bf16[128,40,256]{2,1,0:T(8,128)(2,1)} %fusion.8), calls=%async_computation | async-start | bytes 5242880 | tf_op jit(solution)/shard_map/all_to_all | solution.py:186
  68.9 6.1 %copy-start.1 = (bf16[256,5120]{1,0:T(8,128)(2,1)S(1)}, bf16[256,5120]{1,0:T(8,128)(2,1)}, u32[]{:S(2)}) copy-start(bf16[256,5120]{1,0:T(8,128)(2,1)} %copy.28) | copy-start | bytes 7864324
  76.0 7.7 %collective-permute-start.1 = (f32[2,128,4]{2,1,0:T(8,128)S(1)}, f32[2,128,4]{2,1,0:T(8,128)S(1)}, u32[]{:S(2)}, u32[]{:S(2)}) collective-permute-start(f32[2,128,4]{2,1,0:T(8,128)S(1)} %get-tuple-element.16), channel_id=1, source_target_pairs={{1,0},{2,1},{3,2},{4,3},{5,4},{6,5},{7,6},{8,7},{9,8},{10,9},{11,1... | collective-permute-start | bytes 12296 | tf_op jit(solution)/shard_map/ppermute | solution.py:205
  79.3 10.5 %collective-permute-start = (f32[2,128,4]{2,1,0:T(8,128)S(1)}, f32[2,128,4]{2,1,0:T(8,128)S(1)}, u32[]{:S(2)}, u32[]{:S(2)}) collective-permute-start(f32[2,128,4]{2,1,0:T(8,128)S(1)} %get-tuple-element.15), channel_id=1, source_target_pairs={{0,1},{1,2},{2,3},{3,4},{4,5},{5,6},{6,7},{7,8},{8,9},{9,10},{10,1... | collective-permute-start | bytes 12296 | tf_op jit(solution)/shard_map/ppermute | solution.py:204

commit v12 on v9

--- a/solution.py
+++ b/solution.py
@@ -179,15 +179,20 @@
     send_rows = sent[:, :width].astype(jnp.bfloat16).reshape(devices, capacity, width)
     code_rows = sent[:, width : width + 2].reshape(devices, capacity, 2)
     code_rows = jnp.swapaxes(code_rows, 1, 2).astype(jnp.bfloat16)
-    code_rows = jnp.pad(code_rows, ((0, 0), (0, EXTRA - 2), (0, width - capacity)))
-    message = jnp.concatenate([send_rows, code_rows], axis=1)
+    narrow = 128
+    split = width // narrow
+    code_rows = jnp.pad(code_rows, ((0, 0), (0, EXTRA - 2), (0, narrow - capacity)))
+    message = jnp.concatenate(
+        [send_rows.reshape(devices, capacity * split, narrow), code_rows], axis=1
+    )
     got = lax.all_to_all(message, ("cell", "own"), split_axis=0, concat_axis=0, tiled=True)
-    lanes = capacity + EXTRA
+    lanes = capacity + EXTRA // split
     recv_rows = got.reshape(devices * lanes, width)
-    high = got[:, capacity, :capacity].astype(jnp.int32)
-    low = got[:, capacity + 1, :capacity].astype(jnp.int32)
+    high = got[:, capacity * split, :capacity].astype(jnp.int32)
+    low = got[:, capacity * split + 1, :capacity].astype(jnp.int32)
     recv_cells = jnp.where(high > 0, (high - 1) * CODE + low, -1)
-    recv_cells = jnp.pad(recv_cells, ((0, 0), (0, EXTRA)), constant_values=-1).reshape(devices * lanes)
+    recv_cells = jnp.pad(recv_cells, ((0, 0), (0, lanes - capacity)), constant_values=-1)
+    recv_cells = recv_cells.reshape(devices * lanes)
     edges = jnp.concatenate(
         [jnp.arange(W, dtype=jnp.int32), jnp.arange(cells - W, cells, dtype=jnp.int32)]
     )

time: 105 us -> 110 us (1.048); the launches traced: 105 us -> 108 us
  local copies, waits for them, and re-layouts: 6.31 us -> 15.5 us
  waiting for transfers between devices: 42.8 us -> 34.5 us
  starting transfers between devices: 16.3 us -> 20.2 us
  matrix products: 17.4 us -> 15.5 us
    ppermute x1, waiting for transfers between devices: 6.14 us -> 0.43 us  [body_inner(): below = lax.ppermute(edge_lev[:, :, W:], ('cell', 'own'), forward)]
    ppermute x1, starting transfers between devices: 3.29 us -> 7.3 us  [body_inner(): above = lax.ppermute(edge_lev[:, :, :W], ('cell', 'own'), backward)]
    all_to_all x1, waiting for transfers between devices: 35.1 us -> 32.3 us  [body_inner(): lax.all_to_all(message, ('cell', 'own'), split_axis=0, concat_axis=0, til...]
    another operation x2 -> x3, local copies, waits for them, and re-layouts: 0.01 us -> 2.68 us  [the longest x1 2.67 us: body_inner(): send_rows.reshape(devices, capacity * split, narrow)]
    slice x1 -> x2, local copies, waits for them, and re-layouts: 0.14 us -> 2.7 us  [body_inner(): sent[:, :width].astype(jnp.bfloat16).reshape(devices, capacity, width)]
    reshape x0 -> x1, local copies, waits for them, and re-layouts: none -> 2.25 us  [body_inner(): recv_rows = got.reshape(devices * lanes, width)]
    dot_general x1, local copies, waits for them, and re-layouts: 2.83 us -> 4.3 us  [body_inner(): lax.dot_general(recv_rows, select, (((0,), (0,)), ((), ())), preferred_el...]
    dot_general x1, matrix products: 10.4 us -> 9.23 us  [body_inner(): sent = jnp.dot(place, payload, preferred_element_type=jnp.float32)]
where the time goes in v12:
time: 110 us; the launch traced here: 108 us
  waiting for transfers between devices  34.5 us (31%)
  starting transfers between devices  20.2 us (18%)
  local copies, waits for them, and re-layouts  15.5 us (14%)
  matrix products  15.5 us (14%)
  Pallas kernels  12 us (11%)
  other arithmetic  9.87 us (9%)
    all_to_all x1, waiting for transfers between devices, body_inner(): lax.all_to_all(message, ('cell', 'own'), split_axis=0, concat_axis=0, til...  32.3 us
    pallas_call x1, Pallas kernels, fit_all(): pl.pallas_call(fit_kernel, out_shape=(jax.ShapeDtypeStruct((count, spec,...  12 us
    all_to_all x1, starting transfers between devices, body_inner(): lax.all_to_all(message, ('cell', 'own'), split_axis=0, concat_axis=0, til...  10.5 us
    dot_general x1, matrix products, body_inner(): sent = jnp.dot(place, payload, preferred_element_type=jnp.float32)  9.23 us
    ppermute x1, starting transfers between devices, body_inner(): above = lax.ppermute(edge_lev[:, :, :W], ('cell', 'own'), backward)  7.3 us
    dot_general x1, matrix products, body_inner(): lax.dot_general(recv_rows, select, (((0,), (0,)), ((), ())), preferred_el...  5.49 us
    dot_general x1, local copies, waits for them, and re-layouts, body_inner(): lax.dot_general(recv_rows, select, (((0,), (0,)), ((), ())), preferred_el...  4.3 us
    add x1, other arithmetic, body_inner(): target + weight[None, None, :] * lax.slice_in_dim(rimmed, W + shift, W +...  3.87 us
  transfers between devices with their start and end apart: 3, of which 3 were waited for; matrix products, arithmetic and copies ran while one was open for 0% of the time, Pallas kernels for 0%

profile of v12, /device:TPU:8, one launch (start us, length us, event | category | flops | bytes accessed | tf_op | source)
XLA Modules:
  0.0 108.5 jit_solution(3718787186668952123)
XLA Ops:
  0.6 0.7 fusion.56
  1.4 0.8 copy.20
  2.2 1.1 copy.30
  3.3 0.3 fusion.42
  3.8 0.3 copy.21
  4.1 0.2 copy-done.2
  4.3 0.6 fusion.41
  5.0 0.7 copy-done
  5.7 1.7 %reduce_sum.103 = bf16[2048,256]{1,0:T(8,128)(2,1)} reduce(bf16[2048,3,256]{2,0,1:T(8,128)(2,1)S(1)} %copy-done, bf16[]{:T(256)} %constant.30.clone.1), dimensions={1}, to_apply=%region_3.4 | reduce | flops 1048576 | bytes 4194306 | tf_op jit(solution)/shard_map/reduce_sum | solution.py:167
  7.4 9.2 %fusion.6 = bf16[4096,384]{0,1:T(8,128)(2,1)S(1)} fusion(s32[2048]{0:T(1024)S(1)} %multiply_add_fusion, bf16[2048,2]{1,0:T(8,128)(2,1)} %copy.30, bf16[2048,256]{1,0:T(8,128)(2,1)} %reduce_sum.103), kind=kOutput, calls=%fused_computation.7 | convolution fusion | flops 6457131008 | bytes 4210688 | tf_op jit(solution)/shard_map/dot_general | solution.py:178
  16.7 0.2 slice.92
  16.9 2.5 %copy.23 = bf16[4096,256]{1,0:T(8,128)(2,1)} copy(bf16[4096,256]{0,1:T(8,128)(2,1)S(1)} %slice.92) | data formatting | bytes 4194304 | tf_op jit(solution)/shard_map/slice | solution.py:179
  19.4 2.7 %reshape_reshape.3 = bf16[128,64,128]{2,1,0:T(8,128)(2,1)S(1)} reshape(bf16[4096,256]{1,0:T(8,128)(2,1)} %copy.23) | data formatting | bytes 4194304 | tf_op jit(solution)/shard_map/reshape;reshape | solution.py:186
  22.1 0.1 convert_element_type.63
  22.2 1.7 %fusion.9 = bf16[128,72,128]{2,1,0:T(8,128)(2,1)} fusion(bf16[128,2,32]{2,1,0:T(2,128)(2,1)S(1)} %bitcast.30, bf16[128,64,128]{2,1,0:T(8,128)(2,1)S(1)} %reshape_reshape.3), kind=kLoop, calls=%fused_computation.12 | loop fusion | flops 7077888 | bytes 4472832 | tf_op jit(solution)/shard_map/concatenate | solution.py:185
  24.0 10.5 %all-to-all-start = ((bf16[128,72,128]{2,1,0:T(8,128)(2,1)}), bf16[128,72,128]{2,1,0:T(8,128)(2,1)S(1)}, u32[]{:S(2)}, u32[]{:S(2)}) async-start(bf16[128,72,128]{2,1,0:T(8,128)(2,1)} %fusion.9), calls=%async_computation | async-start | bytes 4718592 | tf_op jit(solution)/shard_map/all_to_all | solution.py:188
  34.5 0.1 convert_reduce_fusion.8
  34.6 32.3 %all-to-all-done = bf16[128,72,128]{2,1,0:T(8,128)(2,1)S(1)} async-done(((bf16[128,72,128]{2,1,0:T(8,128)(2,1)}), bf16[128,72,128]{2,1,0:T(8,128)(2,1)S(1)}, u32[]{:S(2)}, u32[]{:S(2)}) %all-to-all-start) | async-done | bytes 2359328 | tf_op jit(solution)/shard_map/all_to_all | solution.py:188
  66.9 2.2 %reshape.60 = bf16[4608,256]{1,0:T(8,128)(2,1)} reshape(bf16[128,72,128]{2,1,0:T(8,128)(2,1)S(1)} %all-to-all-done) | data formatting | bytes 4718592 | tf_op jit(solution)/shard_map/reshape | solution.py:190
  69.2 4.3 %copy.25 = bf16[256,4608]{1,0:T(8,128)(2,1)} copy(bf16[256,4608]{0,1:T(8,128)(2,1)} %bitcast.27) | data formatting | bytes 4718592 | tf_op jit(solution)/shard_map/dot_general | solution.py:212
  73.5 0.2 compare_select_fusion
  73.7 0.1 eq.130
  73.8 5.5 %fusion.2 = f32[2,128,1024]{2,1,0:T(8,128)S(1)} fusion(bf16[2,128,4608]{2,1,0:T(8,128)(2,1)} %bitcast.28, s32[4608]{0:T(1024)S(1)} %eq.130), kind=kOutput, calls=%fused_computation.4 | convolution fusion | flops 2420637696 | bytes 3426304 | tf_op jit(solution)/shard_map/dot_general | solution.py:212
  79.4 0.8 fusion.46
  80.2 0.1 fusion.63
  80.3 2.5 %collective-permute-start = (f32[2,128,4]{2,1,0:T(8,128)S(1)}, f32[2,128,4]{2,1,0:T(8,128)S(1)}, u32[]{:S(2)}, u32[]{:S(2)}) collective-permute-start(f32[2,128,4]{2,1,0:T(8,128)S(1)} %get-tuple-element.15), channel_id=1, source_target_pairs={{0,1},{1,2},{2,3},{3,4},{4,5},{5,6},{6,7},{7,8},{8,9},{9,10},{10,1... | collective-permute-start | bytes 12296 | tf_op jit(solution)/shard_map/ppermute | solution.py:207
  82.8 7.3 %collective-permute-start.1 = (f32[2,128,4]{2,1,0:T(8,128)S(1)}, f32[2,128,4]{2,1,0:T(8,128)S(1)}, u32[]{:S(2)}, u32[]{:S(2)}) collective-permute-start(f32[2,128,4]{2,1,0:T(8,128)S(1)} %get-tuple-element.16), channel_id=1, source_target_pairs={{1,0},{2,1},{3,2},{4,3},{5,4},{6,5},{7,6},{8,7},{9,8},{10,9},{11,1... | collective-permute-start | bytes 12296 | tf_op jit(solution)/shard_map/ppermute | solution.py:208
  90.1 0.3 fusion.17
  90.4 0.4 collective-permute-done
  90.8 1.8 %collective-permute-done.1 = f32[2,128,4]{2,1,0:T(8,128)S(1)} collective-permute-done((f32[2,128,4]{2,1,0:T(8,128)S(1)}, f32[2,128,4]{2,1,0:T(8,128)S(1)}, u32[]{:S(2)}, u32[]{:S(2)}) %collective-permute-start.1) | collective-permute-done | bytes 4128 | tf_op jit(solution)/shard_map/ppermute | solution.py:208
  92.6 3.9 %fusion.21.t_ref = f32[2,128,1024]{2,1,0:T(8,128)} fusion(f32[2,128,1024]{2,1,0:T(8,128)S(1)} %fusion.17, f32[2,128,4]{2,1,0:T(8,128)S(1)} %collective-permute-done.1, f32[2,128,4]{2,1,0:T(8,128)S(1)} %collective-permute-done, f32[1024]{0:T(1024)S(1)} %get-tuple-element.13, f32[1024]{0:T(1024)S(1)} %get-tuple-element.14, f32[1024]{0:T(1024)S(1)} %get-tuple-element.7, ...), kind=kLoop, calls=%fused_computation.37 | loop fusion | flops 7077888 | bytes 2142208 | tf_op jit(solution)/shard_map/add | solution.py:221
  96.5 12.0 %shard_map.77 = (f32[6,2,1024]{2,1,0:T(2,128)}, f32[2,1024]{1,0:T(2,128)}) custom-call(f32[2,128,1024]{2,1,0:T(8,128)} %fusion.21.t_ref, f32[128,8]{1,0:T(8,128)} %constant.77.clone.phit_ref, f32[32,128]{1,0:T(8,128)} %constant.78.clone.psi_ref), custom_call_target="tpu_custom_call" | custom-call | tf_op jit(solution)/shard_map/pallas_call | solution.py:141
  (21 shorter events, 0.4 us)
Async XLA Ops:
  3.6 0.7 copy-start.2
  3.8 1.9 %copy-start = (bf16[2048,3,256]{2,0,1:T(8,128)(2,1)S(1)}, bf16[2048,3,256]{2,0,1:T(8,128)(2,1)}, u32[]{:S(2)}) copy-start(bf16[2048,3,256]{2,0,1:T(8,128)(2,1)} %param.6) | copy-start | bytes 9437188
  24.0 10.6 %copy-start.3 = (s32[4,1024]{1,0:T(4,128)S(1)}, s32[4,1024]{1,0:T(4,128)}, u32[]{:S(2)}) copy-start(s32[4,1024]{1,0:T(4,128)} %param.9) | copy-start | bytes 49156
  24.0 43.0 %all-to-all-start = ((bf16[128,72,128]{2,1,0:T(8,128)(2,1)}), bf16[128,72,128]{2,1,0:T(8,128)(2,1)S(1)}, u32[]{:S(2)}, u32[]{:S(2)}) async-start(bf16[128,72,128]{2,1,0:T(8,128)(2,1)} %fusion.9), calls=%async_computation | async-start | bytes 4718592 | tf_op jit(solution)/shard_map/all_to_all | solution.py:188
  73.8 5.5 %copy-start.1 = (bf16[256,4608]{1,0:T(8,128)(2,1)S(1)}, bf16[256,4608]{1,0:T(8,128)(2,1)}, u32[]{:S(2)}) copy-start(bf16[256,4608]{1,0:T(8,128)(2,1)} %copy.25) | copy-start | bytes 7077892
  80.3 10.5 %collective-permute-start = (f32[2,128,4]{2,1,0:T(8,128)S(1)}, f32[2,128,4]{2,1,0:T(8,128)S(1)}, u32[]{:S(2)}, u32[]{:S(2)}) collective-permute-start(f32[2,128,4]{2,1,0:T(8,128)S(1)} %get-tuple-element.15), channel_id=1, source_target_pairs={{0,1},{1,2},{2,3},{3,4},{4,5},{5,6},{6,7},{7,8},{8,9},{9,10},{10,1... | collective-permute-start | bytes 12296 | tf_op jit(solution)/shard_map/ppermute | solution.py:207
  82.8 9.8 %collective-permute-start.1 = (f32[2,128,4]{2,1,0:T(8,128)S(1)}, f32[2,128,4]{2,1,0:T(8,128)S(1)}, u32[]{:S(2)}, u32[]{:S(2)}) collective-permute-start(f32[2,128,4]{2,1,0:T(8,128)S(1)} %get-tuple-element.16), channel_id=1, source_target_pairs={{1,0},{2,1},{3,2},{4,3},{5,4},{6,5},{7,6},{8,7},{9,8},{10,9},{11,1... | collective-permute-start | bytes 12296 | tf_op jit(solution)/shard_map/ppermute | solution.py:208

commit v13 on v9

--- a/solution.py
+++ b/solution.py
@@ -176,38 +176,45 @@
     payload = jnp.concatenate([packed, codes], axis=1)
     place = (jnp.arange(slots, dtype=jnp.int32)[:, None] == position[None, :]).astype(jnp.bfloat16)
     sent = jnp.dot(place, payload, preferred_element_type=jnp.float32)
-    send_rows = sent[:, :width].astype(jnp.bfloat16).reshape(devices, capacity, width)
+    narrow = width // SPEC
+    halves = [
+        sent[:, h * narrow : (h + 1) * narrow].astype(jnp.bfloat16).reshape(devices, capacity, narrow)
+        for h in range(SPEC)
+    ]
     code_rows = sent[:, width : width + 2].reshape(devices, capacity, 2)
     code_rows = jnp.swapaxes(code_rows, 1, 2).astype(jnp.bfloat16)
-    code_rows = jnp.pad(code_rows, ((0, 0), (0, EXTRA - 2), (0, width - capacity)))
-    message = jnp.concatenate([send_rows, code_rows], axis=1)
+    code_rows = jnp.pad(code_rows, ((0, 0), (0, EXTRA - 2), (0, narrow - capacity)))
+    message = jnp.concatenate(halves + [code_rows], axis=1)
     got = lax.all_to_all(message, ("cell", "own"), split_axis=0, concat_axis=0, tiled=True)
-    lanes = capacity + EXTRA
-    recv_rows = got.reshape(devices * lanes, width)
-    high = got[:, capacity, :capacity].astype(jnp.int32)
-    low = got[:, capacity + 1, :capacity].astype(jnp.int32)
+    recv_halves = [
+        got[:, h * capacity : (h + 1) * capacity, :].reshape(slots, narrow) for h in range(SPEC)
+    ]
+    high = got[:, SPEC * capacity, :capacity].astype(jnp.int32).reshape(slots)
+    low = got[:, SPEC * capacity + 1, :capacity].astype(jnp.int32).reshape(slots)
     recv_cells = jnp.where(high > 0, (high - 1) * CODE + low, -1)
-    recv_cells = jnp.pad(recv_cells, ((0, 0), (0, EXTRA)), constant_values=-1).reshape(devices * lanes)
+
+    def cell_sums(picked):
+        return jnp.stack(
+            [
+                lax.dot_general(
+                    part, picked, (((0,), (0,)), ((), ())), preferred_element_type=jnp.float32
+                )
+                for part in recv_halves
+            ]
+        )
+
     edges = jnp.concatenate(
         [jnp.arange(W, dtype=jnp.int32), jnp.arange(cells - W, cells, dtype=jnp.int32)]
     )
-    edge_select = (recv_cells[:, None] == edges[None, :]).astype(jnp.bfloat16)
-    edge_sum = lax.dot_general(
-        recv_rows, edge_select, (((0,), (0,)), ((), ())), preferred_element_type=jnp.float32
-    )
-    edge_lev = smooth_levels(edge_sum.reshape(SPEC, width // SPEC, 2 * W))
-    count = devices
-    forward = [(i, i + 1) for i in range(count - 1)]
+    edge_lev = smooth_levels(cell_sums((recv_cells[:, None] == edges[None, :]).astype(jnp.bfloat16)))
+    forward = [(i, i + 1) for i in range(devices - 1)]
     backward = [(target, source) for source, target in forward]
     below = lax.ppermute(edge_lev[:, :, W:], ("cell", "own"), forward)
     above = lax.ppermute(edge_lev[:, :, :W], ("cell", "own"), backward)
     select = (recv_cells[:, None] == jnp.arange(cells, dtype=jnp.int32)[None, :]).astype(
         jnp.bfloat16
     )
-    summed = lax.dot_general(
-        recv_rows, select, (((0,), (0,)), ((), ())), preferred_element_type=jnp.float32
-    )
-    cellhist = summed.reshape(SPEC, width // SPEC, cells)
+    cellhist = cell_sums(select)
     levelled = smooth_levels(cellhist)
     rimmed = jnp.concatenate([below, levelled, above], axis=2)
     target = 1.0 + levelled

time: 105 us -> 101 us (0.962)
  waiting for transfers between devices: 42.8 us -> 40 us
  local copies, waits for them, and re-layouts: 6.31 us -> 4.14 us
    dot_general x1 -> x0, local copies, waits for them, and re-layouts: 2.83 us -> none  [body_inner(): lax.dot_general(recv_rows, select, (((0,), (0,)), ((), ())), preferred_el...]
    all_to_all x1, waiting for transfers between devices: 35.1 us -> 32.3 us  [body_inner(): lax.all_to_all(message, ('cell', 'own'), split_axis=0, concat_axis=0, til...]
    dot_general x2 -> x4, matrix products: 6.93 us -> 7.13 us  [cell_sums(): lax.dot_general(part, picked, (((0,), (0,)), ((), ())), preferred_element...]
  transfers between devices with their start and end apart: 3 -> 3, of which waited for: 3 -> 3; matrix products, arithmetic and copies ran while one was open for 0% -> 1% of each run, Pallas kernels for 0% -> 0%
where the time goes in v13:
time: 101 us; the launch traced here: 100 us
  waiting for transfers between devices  40 us (40%)
  matrix products  17.5 us (17%)
  starting transfers between devices  16.3 us (16%)
  Pallas kernels  12 us (12%)
  other arithmetic  9.4 us (9%)
  local copies, waits for them, and re-layouts  4.14 us (4%)
    all_to_all x1, waiting for transfers between devices, body_inner(): lax.all_to_all(message, ('cell', 'own'), split_axis=0, concat_axis=0, til...  32.3 us
    pallas_call x1, Pallas kernels, fit_all(): pl.pallas_call(fit_kernel, out_shape=(jax.ShapeDtypeStruct((count, spec,...  12 us
    all_to_all x1, starting transfers between devices, body_inner(): lax.all_to_all(message, ('cell', 'own'), split_axis=0, concat_axis=0, til...  10.5 us
    dot_general x1, matrix products, body_inner(): sent = jnp.dot(place, payload, preferred_element_type=jnp.float32)  10.4 us
    dot_general x4, matrix products, cell_sums(): lax.dot_general(part, picked, (((0,), (0,)), ((), ())), preferred_element...  7.13 us
    ppermute x1, waiting for transfers between devices, body_inner(): below = lax.ppermute(edge_lev[:, :, W:], ('cell', 'own'), forward)  6.23 us
    add x1, other arithmetic, body_inner(): target + weight[None, None, :] * lax.slice_in_dim(rimmed, W + shift, W +...  3.87 us
    ppermute x1, starting transfers between devices, body_inner(): above = lax.ppermute(edge_lev[:, :, :W], ('cell', 'own'), backward)  3.38 us
  transfers between devices with their start and end apart: 3, of which 3 were waited for; matrix products, arithmetic and copies ran while one was open for 1% of the time, Pallas kernels for 0%

profile of v13, /device:TPU:8, one launch (start us, length us, event | category | flops | bytes accessed | tf_op | source)
XLA Modules:
  0.0 100.2 jit_solution(4813836924481952477)
XLA Ops:
  0.6 0.9 copy.40
  1.5 0.3 fusion.44
  2.0 0.3 copy.41
  2.4 0.6 fusion.43
  3.1 1.1 %copy.46 = bf16[2048,2]{1,0:T(8,128)(2,1)} copy(bf16[2048,2]{0,1:T(2,128)(2,1)S(1)} %pad_maximum_fusion.3) | data formatting | bytes 16384
  4.2 1.7 %reduce_sum.103 = bf16[2048,256]{1,0:T(8,128)(2,1)} reduce(bf16[2048,3,256]{2,0,1:T(8,128)(2,1)S(1)} %copy-done, bf16[]{:T(256)} %constant.30.clone.1), dimensions={1}, to_apply=%region_3.4 | reduce | flops 1048576 | bytes 4194306 | tf_op jit(solution)/shard_map/reduce_sum | solution.py:167
  5.9 10.4 %fusion.6 = bf16[4096,384]{1,0:T(8,128)(2,1)S(1)} fusion(s32[2048]{0:T(1024)S(1)} %multiply_add_fusion, bf16[2048,2]{1,0:T(8,128)(2,1)} %copy.46, bf16[2048,256]{1,0:T(8,128)(2,1)} %reduce_sum.103), kind=kOutput, calls=%fused_computation.8 | convolution fusion | flops 6457131008 | bytes 4210688 | tf_op jit(solution)/shard_map/dot_general | solution.py:178
  16.4 0.1 fusion.67
  16.6 0.8 copy.43
  17.4 1.7 %fusion.9 = bf16[128,72,128]{2,1,0:T(8,128)(2,1)} fusion(bf16[128,2,32]{2,1,0:T(2,128)(2,1)S(1)} %bitcast.36, bf16[128,32,128]{2,1,0:T(8,128)(2,1)S(1)} %bitcast.30, bf16[128,32,128]{2,1,0:T(8,128)(2,1)S(1)} %bitcast.29), kind=kLoop, calls=%fused_computation.13 | loop fusion | flops 9437184 | bytes 4472832 | tf_op jit(solution)/shard_map/concatenate | solution.py:187
  19.1 10.5 %all-to-all-start = ((bf16[128,72,128]{2,1,0:T(8,128)(2,1)}), bf16[128,72,128]{2,1,0:T(8,128)(2,1)S(1)}, u32[]{:S(2)}, u32[]{:S(2)}) async-start(bf16[128,72,128]{2,1,0:T(8,128)(2,1)} %fusion.9), calls=%async_computation | async-start | bytes 4718592 | tf_op jit(solution)/shard_map/all_to_all | solution.py:188
  29.6 0.1 pad_add_fusion
  29.6 0.1 convert_reduce_fusion.8
  29.7 32.3 %all-to-all-done = bf16[128,72,128]{2,1,0:T(8,128)(2,1)S(1)} async-done(((bf16[128,72,128]{2,1,0:T(8,128)(2,1)}), bf16[128,72,128]{2,1,0:T(8,128)(2,1)S(1)}, u32[]{:S(2)}, u32[]{:S(2)}) %all-to-all-start) | async-done | bytes 2359328 | tf_op jit(solution)/shard_map/all_to_all | solution.py:188
  62.0 0.4 fusion.53
  62.4 0.1 reshape.88
  62.5 0.4 fusion.68
  62.9 3.3 %fusion.16 = f32[1,128,1024]{2,1,0:T(8,128)S(1)} fusion(bf16[4096,128]{1,0:T(8,128)(2,1)S(1)} %bitcast.34, s32[4096]{0:T(1024)S(1)} %reshape.88), kind=kOutput, calls=%fused_computation.25 | convolution fusion | flops 1077936128 | bytes 1589248 | tf_op jit(solution)/shard_map/dot_general | solution.py:199
  66.1 3.3 %fusion.15 = f32[1,128,1024]{2,1,0:T(8,128)S(1)} fusion(bf16[4096,128]{1,0:T(8,128)(2,1)S(1)} %bitcast.32, s32[4096]{0:T(1024)S(1)} %reshape.88), kind=kOutput, calls=%fused_computation.24 | convolution fusion | flops 1077936128 | bytes 1589248 | tf_op jit(solution)/shard_map/dot_general | solution.py:199
  69.4 0.3 convolution_bitcast_fusion
  69.7 0.3 convolution_bitcast_fusion.1
  70.0 0.1 copy.45
  70.2 0.1 copy.44
  70.3 0.1 fusion.69
  70.4 3.4 %collective-permute-start.1 = (f32[2,128,4]{2,1,0:T(8,128)S(1)}, f32[2,128,4]{2,1,0:T(8,128)S(1)}, u32[]{:S(2)}, u32[]{:S(2)}) collective-permute-start(f32[2,128,4]{2,1,0:T(8,128)S(1)} %get-tuple-element.20), channel_id=1, source_target_pairs={{1,0},{2,1},{3,2},{4,3},{5,4},{6,5},{7,6},{8,7},{9,8},{10,9},{11,1... | collective-permute-start | bytes 12296 | tf_op jit(solution)/shard_map/ppermute | solution.py:213
  73.8 2.5 %collective-permute-start = (f32[2,128,4]{2,1,0:T(8,128)S(1)}, f32[2,128,4]{2,1,0:T(8,128)S(1)}, u32[]{:S(2)}, u32[]{:S(2)}) collective-permute-start(f32[2,128,4]{2,1,0:T(8,128)S(1)} %get-tuple-element.19), channel_id=1, source_target_pairs={{0,1},{1,2},{2,3},{3,4},{4,5},{5,6},{6,7},{7,8},{8,9},{9,10},{10,1... | collective-permute-start | bytes 12296 | tf_op jit(solution)/shard_map/ppermute | solution.py:212
  76.3 0.1 pad_maximum_fusion.2
  76.4 0.3 fusion.19
  76.7 1.4 %collective-permute-done.1 = f32[2,128,4]{2,1,0:T(8,128)S(1)} collective-permute-done((f32[2,128,4]{2,1,0:T(8,128)S(1)}, f32[2,128,4]{2,1,0:T(8,128)S(1)}, u32[]{:S(2)}, u32[]{:S(2)}) %collective-permute-start.1) | collective-permute-done | bytes 4128 | tf_op jit(solution)/shard_map/ppermute | solution.py:213
  78.1 6.2 %collective-permute-done = f32[2,128,4]{2,1,0:T(8,128)S(1)} collective-permute-done((f32[2,128,4]{2,1,0:T(8,128)S(1)}, f32[2,128,4]{2,1,0:T(8,128)S(1)}, u32[]{:S(2)}, u32[]{:S(2)}) %collective-permute-start) | collective-permute-done | bytes 4128 | tf_op jit(solution)/shard_map/ppermute | solution.py:212
  84.3 3.9 %fusion.23.t_ref = f32[2,128,1024]{2,1,0:T(8,128)} fusion(f32[2,128,1024]{2,1,0:T(8,128)S(1)} %fusion.19, f32[2,128,4]{2,1,0:T(8,128)S(1)} %collective-permute-done.1, f32[2,128,4]{2,1,0:T(8,128)S(1)} %collective-permute-done, f32[1024]{0:T(1024)S(1)} %get-tuple-element.13, f32[1024]{0:T(1024)S(1)} %get-tuple-element.14, f32[1024]{0:T(1024)S(1)} %get-tuple-element.7, ...), kind=kLoop, calls=%fused_computation.42 | loop fusion | flops 7077888 | bytes 2142208 | tf_op jit(solution)/shard_map/add | solution.py:223
  88.2 12.0 %shard_map.77 = (f32[6,2,1024]{2,1,0:T(2,128)}, f32[2,1024]{1,0:T(2,128)}) custom-call(f32[2,128,1024]{2,1,0:T(8,128)} %fusion.23.t_ref, f32[128,8]{1,0:T(8,128)} %constant.77.clone.phit_ref, f32[32,128]{1,0:T(8,128)} %constant.78.clone.psi_ref), custom_call_target="tpu_custom_call" | custom-call | tf_op jit(solution)/shard_map/pallas_call | solution.py:141
  (22 shorter events, 0.3 us)
Async XLA Ops:
  0.6 1.7 %copy-start.1 = (s32[2048,1]{0,1:T(1,128)S(1)}, s32[2048,1]{0,1:T(1,128)}, u32[]{:S(2)}) copy-start(s32[2048,1]{0,1:T(1,128)} %param.7) | copy-start | bytes 24580
  1.5 1.5 %copy-start.3 = (s32[2048]{0:T(1024)S(1)}, s32[2048]{0:T(1024)}, u32[]{:S(2)}) copy-start(s32[2048]{0:T(1024)} %param.8) | copy-start | bytes 24580
  2.0 2.2 %copy-start = (bf16[2048,3,256]{2,0,1:T(8,128)(2,1)S(1)}, bf16[2048,3,256]{2,0,1:T(8,128)(2,1)}, u32[]{:S(2)}) copy-start(bf16[2048,3,256]{2,0,1:T(8,128)(2,1)} %param.6) | copy-start | bytes 9437188
  19.1 10.6 %copy-start.2 = (s32[4,1024]{1,0:T(4,128)S(1)}, s32[4,1024]{1,0:T(4,128)}, u32[]{:S(2)}) copy-start(s32[4,1024]{1,0:T(4,128)} %param.9) | copy-start | bytes 49156
  19.1 43.0 %all-to-all-start = ((bf16[128,72,128]{2,1,0:T(8,128)(2,1)}), bf16[128,72,128]{2,1,0:T(8,128)(2,1)S(1)}, u32[]{:S(2)}, u32[]{:S(2)}) async-start(bf16[128,72,128]{2,1,0:T(8,128)(2,1)} %fusion.9), calls=%async_computation | async-start | bytes 4718592 | tf_op jit(solution)/shard_map/all_to_all | solution.py:188
  70.4 7.7 %collective-permute-start.1 = (f32[2,128,4]{2,1,0:T(8,128)S(1)}, f32[2,128,4]{2,1,0:T(8,128)S(1)}, u32[]{:S(2)}, u32[]{:S(2)}) collective-permute-start(f32[2,128,4]{2,1,0:T(8,128)S(1)} %get-tuple-element.20), channel_id=1, source_target_pairs={{1,0},{2,1},{3,2},{4,3},{5,4},{6,5},{7,6},{8,7},{9,8},{10,9},{11,1... | collective-permute-start | bytes 12296 | tf_op jit(solution)/shard_map/ppermute | solution.py:213
  73.8 10.5 %collective-permute-start = (f32[2,128,4]{2,1,0:T(8,128)S(1)}, f32[2,128,4]{2,1,0:T(8,128)S(1)}, u32[]{:S(2)}, u32[]{:S(2)}) collective-permute-start(f32[2,128,4]{2,1,0:T(8,128)S(1)} %get-tuple-element.19), channel_id=1, source_target_pairs={{0,1},{1,2},{2,3},{3,4},{4,5},{5,6},{6,7},{7,8},{8,9},{9,10},{10,1... | collective-permute-start | bytes 12296 | tf_op jit(solution)/shard_map/ppermute | solution.py:212

commit v14 on v13

--- a/solution.py
+++ b/solution.py
@@ -61,8 +61,29 @@
     return [lam[m] - 0.5 * delta[m] for m in range(count)]
 
 
-def fit_kernel(t_ref, phit_ref, psi_ref, lam_ref, fit_ref, lam_s, dense_ref):
+def fit_kernel(
+    h0_ref, h1_ref, below_ref, above_ref, w_ref, phit_ref, psi_ref, lam_ref, fit_ref, lam_s,
+    dense_ref, t_ref, ext_ref,
+):
     spec, levels, cells = t_ref.shape
+    h_refs = (h0_ref, h1_ref)
+    pad = (ext_ref.shape[2] - cells) // 2
+    rim = below_ref.shape[2]
+    ext_ref[...] = jnp.zeros(ext_ref.shape, jnp.float32)
+    for s in range(spec):
+        field = h_refs[s][...]
+        t_ref[s] = field
+        lower = jnp.concatenate([jnp.zeros((1, cells), jnp.float32), t_ref[s, : levels - 1, :]], axis=0)
+        upper = jnp.concatenate([t_ref[s, 1:, :], jnp.zeros((1, cells), jnp.float32)], axis=0)
+        levelled = 0.5 * field + 0.25 * (lower + upper)
+        ext_ref[s, :, pad : pad + cells] = levelled
+        ext_ref[s, :, pad - rim : pad] = below_ref[s]
+        ext_ref[s, :, pad + cells : pad + cells + rim] = above_ref[s]
+        target = 1.0 + levelled
+        for k in range(w_ref.shape[0]):
+            shift = k - w_ref.shape[0] // 2
+            target = target + w_ref[k : k + 1, :] * ext_ref[s, :, pad + shift : pad + shift + cells]
+        t_ref[s] = target
     count = lam_ref.shape[0]
     used = count + 1 + len(pair_list(count))
     groups = 8 // spec
@@ -126,8 +147,9 @@
     return np.stack(table, axis=0).astype(np.float32)
 
 
-def fit_all(target, count):
-    spec, levels, cells = target.shape
+def fit_all(hists, below, above, weights, count):
+    spec = len(hists)
+    levels, cells = hists[0].shape
     phi = legendre_numpy(levels, count)
     pairs = pair_list(count)
     width = 8
@@ -147,8 +169,10 @@
         scratch_shapes=[
             pltpu.VMEM((spec, width, cells), jnp.float32),
             pltpu.VMEM((height, 8, cells * spec // 8), jnp.float32),
+            pltpu.VMEM((spec, levels, cells), jnp.float32),
+            pltpu.VMEM((spec, levels, cells + 256), jnp.float32),
         ],
-    )(target, jnp.asarray(phit), jnp.asarray(psi))
+    )(*hists, below, above, weights, jnp.asarray(phit), jnp.asarray(psi))
     return jnp.transpose(lam, (1, 0, 2)), fit
 
 
@@ -194,19 +218,19 @@
     recv_cells = jnp.where(high > 0, (high - 1) * CODE + low, -1)
 
     def cell_sums(picked):
-        return jnp.stack(
-            [
-                lax.dot_general(
-                    part, picked, (((0,), (0,)), ((), ())), preferred_element_type=jnp.float32
-                )
-                for part in recv_halves
-            ]
-        )
+        return [
+            lax.dot_general(
+                part, picked, (((0,), (0,)), ((), ())), preferred_element_type=jnp.float32
+            )
+            for part in recv_halves
+        ]
 
     edges = jnp.concatenate(
         [jnp.arange(W, dtype=jnp.int32), jnp.arange(cells - W, cells, dtype=jnp.int32)]
     )
-    edge_lev = smooth_levels(cell_sums((recv_cells[:, None] == edges[None, :]).astype(jnp.bfloat16)))
+    edge_lev = smooth_levels(
+        jnp.stack(cell_sums((recv_cells[:, None] == edges[None, :]).astype(jnp.bfloat16)))
+    )
     forward = [(i, i + 1) for i in range(devices - 1)]
     backward = [(target, source) for source, target in forward]
     below = lax.ppermute(edge_lev[:, :, W:], ("cell", "own"), forward)
@@ -215,15 +239,10 @@
         jnp.bfloat16
     )
     cellhist = cell_sums(select)
-    levelled = smooth_levels(cellhist)
-    rimmed = jnp.concatenate([below, levelled, above], axis=2)
-    target = 1.0 + levelled
-    for shift in range(-W, W + 1):
-        weight = jnp.sum((offsets == shift).astype(jnp.float32), axis=0)
-        target = target + weight[None, None, :] * lax.slice_in_dim(
-            rimmed, W + shift, W + shift + cells, axis=2
-        )
-    return fit_all(target, MOM)
+    weights = jnp.stack(
+        [jnp.sum((offsets == shift).astype(jnp.float32), axis=0) for shift in range(-W, W + 1)]
+    )
+    return fit_all(cellhist, below, above, weights, MOM)
 
 
 def solution(mesh):

time: 101 us -> 98.1 us (0.971)
  waiting for transfers between devices: 40 us -> 31 us
  other arithmetic: 9.4 us -> 5.15 us
  starting transfers between devices: 16.3 us -> 20.2 us
  Pallas kernels: 12 us -> 14.6 us
  local copies, waits for them, and re-layouts: 4.14 us -> 6.71 us
  matrix products: 17.5 us -> 19.1 us
    ppermute x1, waiting for transfers between devices: 6.23 us -> 0.01 us  [body_inner(): below = lax.ppermute(edge_lev[:, :, W:], ('cell', 'own'), forward)]
    ppermute x1, starting transfers between devices: 3.38 us -> 7.29 us  [body_inner(): above = lax.ppermute(edge_lev[:, :, :W], ('cell', 'own'), backward)]
    add x1 -> x0, other arithmetic: 3.87 us -> none  [body_inner(): target + weight[None, None, :] * lax.slice_in_dim(rimmed, W + shift, W +...]
    pallas_call x1, Pallas kernels: 12 us -> 14.6 us  [fit_all(): pl.pallas_call(fit_kernel, out_shape=(jax.ShapeDtypeStruct((count, spec,...]
    dot_general x4, matrix products: 7.13 us -> 8.73 us  [cell_sums(): lax.dot_general(part, picked, (((0,), (0,)), ((), ())), preferred_element...]
    ppermute x1, waiting for transfers between devices: 1.41 us -> 0.01 us  [body_inner(): above = lax.ppermute(edge_lev[:, :, :W], ('cell', 'own'), backward)]
    unnamed x9 -> x13, local copies, waits for them, and re-layouts: 1.1 us -> 2.39 us
    all_to_all x1, waiting for transfers between devices: 32.3 us -> 31 us  [body_inner(): lax.all_to_all(message, ('cell', 'own'), split_axis=0, concat_axis=0, til...]
  transfers between devices with their start and end apart: 3 -> 3, of which waited for: 3 -> 1; matrix products, arithmetic and copies ran while one was open for 1% -> 6% of each run, Pallas kernels for 0% -> 0%
where the time goes in v14:
time: 98.1 us; the launch traced here: 97.7 us
  waiting for transfers between devices  31 us (32%)
  starting transfers between devices  20.2 us (21%)
  matrix products  19.1 us (19%)
  Pallas kernels  14.6 us (15%)
  local copies, waits for them, and re-layouts  6.71 us (7%)
  other arithmetic  5.15 us (5%)
    all_to_all x1, waiting for transfers between devices, body_inner(): lax.all_to_all(message, ('cell', 'own'), split_axis=0, concat_axis=0, til...  31 us
    pallas_call x1, Pallas kernels, fit_all(): pl.pallas_call(fit_kernel, out_shape=(jax.ShapeDtypeStruct((count, spec,...  14.6 us
    all_to_all x1, starting transfers between devices, body_inner(): lax.all_to_all(message, ('cell', 'own'), split_axis=0, concat_axis=0, til...  10.5 us
    dot_general x1, matrix products, body_inner(): sent = jnp.dot(place, payload, preferred_element_type=jnp.float32)  10.4 us
    dot_general x4, matrix products, cell_sums(): lax.dot_general(part, picked, (((0,), (0,)), ((), ())), preferred_element...  8.73 us
    ppermute x1, starting transfers between devices, body_inner(): above = lax.ppermute(edge_lev[:, :, :W], ('cell', 'own'), backward)  7.29 us
    ppermute x1, starting transfers between devices, body_inner(): below = lax.ppermute(edge_lev[:, :, W:], ('cell', 'own'), forward)  2.49 us
    unnamed x13, local copies, waits for them, and re-layouts  2.39 us
  transfers between devices with their start and end apart: 3, of which 1 were waited for; matrix products, arithmetic and copies ran while one was open for 6% of the time, Pallas kernels for 0%

profile of v14, /device:TPU:8, one launch (start us, length us, event | category | flops | bytes accessed | tf_op | source)
XLA Modules:
  0.0 97.7 jit_solution(12163859811478005686)
XLA Ops:
  0.6 0.9 copy.40
  1.5 0.3 fusion.16
  1.9 0.1 add_add_fusion
  2.0 0.3 copy.41
  2.4 0.6 fusion.15
  3.1 1.1 %copy.46 = bf16[2048,2]{1,0:T(8,128)(2,1)} copy(bf16[2048,2]{0,1:T(2,128)(2,1)S(1)} %pad_maximum_fusion) | data formatting | bytes 16384
  4.2 1.7 %reduce_sum.103 = bf16[2048,256]{1,0:T(8,128)(2,1)} reduce(bf16[2048,3,256]{2,0,1:T(8,128)(2,1)S(1)} %copy-done, bf16[]{:T(256)} %constant.32.clone.1), dimensions={1}, to_apply=%region_3.4 | reduce | flops 1048576 | bytes 4194306 | tf_op jit(solution)/shard_map/reduce_sum | solution.py:191
  5.9 10.4 %fusion.6 = bf16[4096,384]{1,0:T(8,128)(2,1)S(1)} fusion(s32[2048]{0:T(1024)S(1)} %multiply_add_fusion, bf16[2048,2]{1,0:T(8,128)(2,1)} %copy.46, bf16[2048,256]{1,0:T(8,128)(2,1)} %reduce_sum.103), kind=kOutput, calls=%fused_computation.8 | convolution fusion | flops 6457131008 | bytes 4210688 | tf_op jit(solution)/shard_map/dot_general | solution.py:202
  16.4 0.1 slice.59
  16.4 0.1 fusion.39
  16.6 0.8 copy.43
  17.4 1.7 %fusion.9 = bf16[128,72,128]{2,1,0:T(8,128)(2,1)} fusion(bf16[128,2,32]{2,1,0:T(2,128)(2,1)S(1)} %bitcast.41, bf16[128,32,128]{2,1,0:T(8,128)(2,1)S(1)} %bitcast.35, bf16[128,32,128]{2,1,0:T(8,128)(2,1)S(1)} %bitcast.34), kind=kLoop, calls=%fused_computation.13 | loop fusion | flops 9437184 | bytes 4472832 | tf_op jit(solution)/shard_map/concatenate | solution.py:211
  19.1 10.5 %all-to-all-start = ((bf16[128,72,128]{2,1,0:T(8,128)(2,1)}), bf16[128,72,128]{2,1,0:T(8,128)(2,1)S(1)}, u32[]{:S(2)}, u32[]{:S(2)}) async-start(bf16[128,72,128]{2,1,0:T(8,128)(2,1)} %fusion.9), calls=%async_computation | async-start | bytes 4718592 | tf_op jit(solution)/shard_map/all_to_all | solution.py:212
  29.6 0.1 convert_reduce_fusion
  29.7 1.3 %stack.66.w_ref = f32[9,1024]{1,0:T(8,128)} concatenate(f32[1,1024]{1,0:T(1,128)S(1)} %bitcast.52, f32[1,1024]{1,0:T(1,128)S(1)} %bitcast.51, f32[1,1024]{1,0:T(1,128)S(1)} %bitcast.50, f32[1,1024]{1,0:T(1,128)S(1)} %bitcast.49, f32[1,1024]{1,0:T(1,128)S(1)} %bitcast.48, f32[1,1024]{1,0:T(1,128)S(1)} %bitcast.47, f32[1,1024]{1,0:T(1,128)S(1)} %bitcast.46, ...), dimensions={0} | concatenate | bytes 73728 | tf_op jit(solution)/shard_map/stack | solution.py:242
  30.9 0.1 pad_add_fusion
  31.0 31.0 %all-to-all-done = bf16[128,72,128]{2,1,0:T(8,128)(2,1)S(1)} async-done(((bf16[128,72,128]{2,1,0:T(8,128)(2,1)}), bf16[128,72,128]{2,1,0:T(8,128)(2,1)S(1)}, u32[]{:S(2)}, u32[]{:S(2)}) %all-to-all-start) | async-done | bytes 2359328 | tf_op jit(solution)/shard_map/all_to_all | solution.py:212
  62.0 0.4 fusion.25
  62.4 0.1 reshape.79
  62.5 0.4 fusion.40
  62.9 4.1 %fusion.2.h0_ref = f32[128,1024]{1,0:T(8,128)} fusion(bf16[4096,128]{1,0:T(8,128)(2,1)S(1)} %bitcast.39, s32[4096]{0:T(1024)S(1)} %reshape.79), kind=kOutput, calls=%fused_computation.4 | convolution fusion | flops 1077936128 | bytes 1589248 | tf_op jit(solution)/shard_map/dot_general | solution.py:222
  66.9 0.3 convolution_bitcast_fusion.1
  67.2 0.3 convolution_bitcast_fusion
  67.5 0.1 copy.45
  67.7 0.1 copy.44
  67.9 0.1 fusion.41
  68.0 2.5 %collective-permute-start = (f32[2,128,4]{2,1,0:T(8,128)S(1)}, f32[2,128,4]{2,1,0:T(8,128)S(1)}, u32[]{:S(2)}, u32[]{:S(2)}) collective-permute-start(f32[2,128,4]{2,1,0:T(8,128)S(1)} %get-tuple-element.20), channel_id=1, source_target_pairs={{0,1},{1,2},{2,3},{3,4},{4,5},{5,6},{6,7},{7,8},{8,9},{9,10},{10,1... | collective-permute-start | bytes 12296 | tf_op jit(solution)/shard_map/ppermute | solution.py:236
  70.5 7.3 %collective-permute-start.1 = (f32[2,128,4]{2,1,0:T(8,128)S(1)}, f32[2,128,4]{2,1,0:T(8,128)S(1)}, u32[]{:S(2)}, u32[]{:S(2)}) collective-permute-start(f32[2,128,4]{2,1,0:T(8,128)S(1)} %get-tuple-element.19), channel_id=1, source_target_pairs={{1,0},{2,1},{3,2},{4,3},{5,4},{6,5},{7,6},{8,7},{9,8},{10,9},{11,1... | collective-permute-start | bytes 12296 | tf_op jit(solution)/shard_map/ppermute | solution.py:237
  77.8 4.1 %fusion.1.h1_ref = f32[128,1024]{1,0:T(8,128)} fusion(bf16[4096,128]{1,0:T(8,128)(2,1)S(1)} %bitcast.38, s32[4096]{0:T(1024)S(1)} %reshape.79), kind=kOutput, calls=%fused_computation.3 | convolution fusion | flops 1077936128 | bytes 1589248 | tf_op jit(solution)/shard_map/dot_general | solution.py:222
  81.8 0.6 copy-done.1
  82.5 0.7 copy-done.2
  83.1 14.6 %shard_map.77 = (f32[6,2,1024]{2,1,0:T(2,128)}, f32[2,1024]{1,0:T(2,128)}) custom-call(f32[128,1024]{1,0:T(8,128)} %fusion.2.h0_ref, f32[128,1024]{1,0:T(8,128)} %fusion.1.h1_ref, f32[2,128,4]{2,1,0:T(8,128)} %copy-done.1, f32[2,128,4]{2,1,0:T(8,128)} %copy-done.2, f32[9,1024]{1,0:T(8,128)} %stack.66.w_ref, f32[128,8]{1,0:T(8,128)} %constant.73.clone.phit_ref, ...), custom_call_target="tpu_custom_call" | custom-call | tf_op jit(solution)/shard_map/pallas_call | solution.py:163
  (24 shorter events, 0.2 us)
Async XLA Ops:
  0.6 1.7 %copy-start.3 = (s32[2048,1]{0,1:T(1,128)S(1)}, s32[2048,1]{0,1:T(1,128)}, u32[]{:S(2)}) copy-start(s32[2048,1]{0,1:T(1,128)} %param.7) | copy-start | bytes 24580
  1.5 1.5 %copy-start.5 = (s32[2048]{0:T(1024)S(1)}, s32[2048]{0:T(1024)}, u32[]{:S(2)}) copy-start(s32[2048]{0:T(1024)} %param.8) | copy-start | bytes 24580
  2.0 2.2 %copy-start = (bf16[2048,3,256]{2,0,1:T(8,128)(2,1)S(1)}, bf16[2048,3,256]{2,0,1:T(8,128)(2,1)}, u32[]{:S(2)}) copy-start(bf16[2048,3,256]{2,0,1:T(8,128)(2,1)} %param.6) | copy-start | bytes 9437188
  19.1 10.5 %copy-start.4 = (s32[4,1024]{1,0:T(4,128)S(1)}, s32[4,1024]{1,0:T(4,128)}, u32[]{:S(2)}) copy-start(s32[4,1024]{1,0:T(4,128)} %param.9) | copy-start | bytes 49156
  19.1 43.0 %all-to-all-start = ((bf16[128,72,128]{2,1,0:T(8,128)(2,1)}), bf16[128,72,128]{2,1,0:T(8,128)(2,1)S(1)}, u32[]{:S(2)}, u32[]{:S(2)}) async-start(bf16[128,72,128]{2,1,0:T(8,128)(2,1)} %fusion.9), calls=%async_computation | async-start | bytes 4718592 | tf_op jit(solution)/shard_map/all_to_all | solution.py:212
  68.0 13.9 %collective-permute-start = (f32[2,128,4]{2,1,0:T(8,128)S(1)}, f32[2,128,4]{2,1,0:T(8,128)S(1)}, u32[]{:S(2)}, u32[]{:S(2)}) collective-permute-start(f32[2,128,4]{2,1,0:T(8,128)S(1)} %get-tuple-element.20), channel_id=1, source_target_pairs={{0,1},{1,2},{2,3},{3,4},{4,5},{5,6},{6,7},{7,8},{8,9},{9,10},{10,1... | collective-permute-start | bytes 12296 | tf_op jit(solution)/shard_map/ppermute | solution.py:236
  70.5 11.4 %collective-permute-start.1 = (f32[2,128,4]{2,1,0:T(8,128)S(1)}, f32[2,128,4]{2,1,0:T(8,128)S(1)}, u32[]{:S(2)}, u32[]{:S(2)}) collective-permute-start(f32[2,128,4]{2,1,0:T(8,128)S(1)} %get-tuple-element.19), channel_id=1, source_target_pairs={{1,0},{2,1},{3,2},{4,3},{5,4},{6,5},{7,6},{8,7},{9,8},{10,9},{11,1... | collective-permute-start | bytes 12296 | tf_op jit(solution)/shard_map/ppermute | solution.py:237
  81.8 0.6 copy-start.1
  82.5 0.7 copy-start.2
